TPU v7x, 256 devices: a whole 4x4x8 slice. The times are simulated.
256 devices in a mesh: batch: 16 (over y_hi, z), gx: 4 (over y_lo, core), gy: 4 (over x).
Axes of the slice: x: 4, y: 4 (y_hi: 2, y_lo: 2; y = y_hi * 2 + y_lo), z: 8, core: 2. Of those that a mesh axis runs over, the one named last changes fastest.
Arguments:
- features: bfloat16 [1024, 64, 4, 256], P(('batch', 'gx'), 'gy'), parts along dimension 0, may hold values from -6 to 6
- conv_weight: bfloat16 [6912, 256], replicated, may hold values from -0.078125 to 0.078125
- down_weight: bfloat16 [2048, 512], replicated, may hold values from -0.125 to 0.125
- norm_gain: float32 [512], replicated, may hold values from 0.1 to 1.9
- qkv_weight: bfloat16 [512, 1536], replicated, may hold values from -0.25 to 0.25
- out_weight: bfloat16 [512, 512], replicated, may hold values from -0.25 to 0.25
- upstream: bfloat16 [512, 32, 2, 512], P(('batch', 'gx'), 'gy'), parts along dimension 0, may hold values from -6 to 6
Outputs:
- grad_features: bfloat16 [1024, 64, 4, 256], P(('batch', 'gx'), 'gy'), parts along dimension 0
- grad_conv: bfloat16 [110592, 256], P(('batch', 'gx', 'gy')), parts along dimension 0
- grad_down: bfloat16 [32768, 512], P(('batch', 'gx', 'gy')), parts along dimension 0
- grad_gain: float32 [8192], P(('batch', 'gx', 'gy')), parts along dimension 0
- grad_qkv: bfloat16 [8192, 1536], P(('batch', 'gx', 'gy')), parts along dimension 0
- grad_out: bfloat16 [8192, 512], P(('batch', 'gx', 'gy')), parts along dimension 0
There are 16 independent parts, one for each index of `batch`. A program takes and returns all parts, laid end to end along the dimension named above; an argument that names none is the same for every part. Nothing has to cross between parts.
All inputs are finite; a program needn't handle non-finite values.
Results may differ from a plain program's by a relative error of at most 0.02.
Values may be sent and summed in bfloat16 or wider, within the bound.
No kernel may reach another device: no remote copies, remote signals or barrier semaphores. Data moves between devices by JAX's collectives and lax.ppermute only.
A program may use at most 128 MiB of HBM per device.

v0:
```python
import jax
import jax.numpy as jnp
from jax import lax
from jax.sharding import PartitionSpec as P

H = 8
HD = 64


precise = lax.Precision.HIGHEST


def padded_2(block, sides, width):
    for axis, dim in sides:
        count = lax.axis_size(axis)
        forward = [(i, i + 1) for i in range(count - 1)]
        backward = [(target, source) for source, target in forward]
        low = lax.ppermute(
            lax.slice_in_dim(block, block.shape[dim] - width, None, axis=dim), axis, forward
        )
        high = lax.ppermute(lax.slice_in_dim(block, 0, width, axis=dim), axis, backward)
        block = jnp.concatenate([low, block, high], axis=dim)
    return block


def to_tokens(volume):
    extent_x, extent_y, extent_z, channels = volume.shape
    grid = volume.reshape(extent_x // 2, 2, extent_y // 2, 2, extent_z // 2, 2, channels)
    grid = grid.transpose(0, 2, 4, 1, 3, 5, 6)
    return grid.reshape(extent_x * extent_y * extent_z // 8, 8 * channels)


def from_tokens(matrix, extent_x, extent_y, extent_z):
    channels = matrix.shape[1] // 8
    grid = matrix.reshape(extent_x // 2, extent_y // 2, extent_z // 2, 2, 2, 2, channels)
    grid = grid.transpose(0, 3, 1, 4, 2, 5, 6)
    return grid.reshape(extent_x, extent_y, extent_z, channels)


def plane_columns(padded, extent_x, extent_y, flipped):
    channels = padded.shape[3]
    rows = extent_x * extent_y * padded.shape[2]
    pieces = []
    for offset_x in range(3):
        for offset_y in range(3):
            start_x = 2 - offset_x if flipped else offset_x
            start_y = 2 - offset_y if flipped else offset_y
            pieces.append(
                padded[start_x : start_x + extent_x, start_y : start_y + extent_y].reshape(
                    rows, channels
                )
            )
    return jnp.concatenate(pieces, axis=1)


def depth_sum(product, extent_z, channels, flipped):
    grid = product.reshape(-1, extent_z, 3, channels)
    first, last = (2, 0) if flipped else (0, 2)
    below = jnp.pad(grid[:, :-1, first], ((0, 0), (1, 0), (0, 0)))
    above = jnp.pad(grid[:, 1:, last], ((0, 0), (0, 1), (0, 0)))
    return (below + grid[:, :, 1] + above).reshape(-1, channels)


def local(features, conv_weight, down_weight, norm_gain, qkv_weight, out_weight, upstream):
    extent_x, extent_y, extent_z, channels = features.shape
    model_width = out_weight.shape[0]
    voxels = extent_x * extent_y * extent_z
    score_scale = HD ** (-0.5)
    taps = conv_weight.reshape(9, 3, channels, channels)
    padded = padded_2(features, (("gx", 0), ("gy", 1)), 1)
    columns = plane_columns(padded, extent_x, extent_y, False)
    weight_fwd = taps.transpose(0, 2, 1, 3).reshape(9 * channels, 3 * channels)
    hidden = depth_sum(
        jnp.dot(columns, weight_fwd, preferred_element_type=jnp.float32),
        extent_z,
        channels,
        False,
    )
    gate_sig = jax.nn.sigmoid(hidden)
    activation = (hidden * gate_sig).astype(jnp.bfloat16)
    tokens_in = to_tokens(activation.reshape(extent_x, extent_y, extent_z, channels))
    tok_count = tokens_in.shape[0]
    trunk_rows = jnp.dot(tokens_in, down_weight, preferred_element_type=jnp.float32)
    mean_rows = jnp.mean(trunk_rows, axis=-1, keepdims=True)
    centred = trunk_rows - mean_rows
    inverse_std = lax.rsqrt(jnp.mean(centred * centred, axis=-1, keepdims=True) + 1e-05)
    normed = centred * inverse_std
    normed_b = (normed * norm_gain).astype(jnp.bfloat16)
    qkv_rows = jnp.dot(normed_b, qkv_weight, preferred_element_type=jnp.float32).astype(
        jnp.bfloat16
    )
    queries = qkv_rows[:, :model_width]
    local_keys = qkv_rows[:, model_width : 2 * model_width]
    local_values = qkv_rows[:, 2 * model_width :]
    gathered = lax.all_gather(
        qkv_rows[:, model_width:], ("gx", "gy"), axis=0, tiled=True
    )
    all_keys = gathered[:, :model_width]
    all_values = gathered[:, model_width:]
    queries_h = queries.reshape(tok_count, H, HD)
    keys_h = all_keys.reshape(-1, H, HD)
    values_h = all_values.reshape(-1, H, HD)
    scores = (
        jnp.einsum("ihe,jhe->hij", queries_h, keys_h, preferred_element_type=jnp.float32)
        * score_scale
    )
    exp_scores = jnp.exp(scores)
    totals = jnp.sum(exp_scores, axis=-1)
    attn_probs = exp_scores / totals[:, :, None]
    probs_b = attn_probs.astype(jnp.bfloat16)
    attended = jnp.einsum("hij,jhe->ihe", probs_b, values_h, preferred_element_type=jnp.float32)
    attended = attended.reshape(tok_count, model_width).astype(jnp.bfloat16)
    cotangent = upstream.reshape(tok_count, model_width)
    cot_float = cotangent.astype(jnp.float32)
    out_part = jnp.einsum("td,te->de", attended, cotangent, preferred_element_type=jnp.float32)
    d_attended = jnp.dot(cotangent, out_weight.T, preferred_element_type=jnp.float32).astype(
        jnp.bfloat16
    )
    d_att_h = d_attended.reshape(tok_count, H, HD)
    d_probs = jnp.einsum("ihe,jhe->hij", d_att_h, values_h, preferred_element_type=jnp.float32)
    d_probs = d_probs.astype(jnp.bfloat16).astype(jnp.float32)
    row_delta = jnp.sum(attn_probs * d_probs, axis=-1)
    d_scores = attn_probs * (d_probs - row_delta[:, :, None])
    d_queries = (
        jnp.einsum(
            "hij,jhe->ihe", d_scores, keys_h, precision=precise, preferred_element_type=jnp.float32
        )
        * score_scale
    )
    key_term = (
        jnp.einsum(
            "hij,ihe->jhe",
            d_scores,
            queries_h,
            precision=precise,
            preferred_element_type=jnp.float32,
        )
        * score_scale
    )
    value_term = jnp.einsum("hij,ihe->jhe", probs_b, d_att_h, preferred_element_type=jnp.float32)
    groups = lax.axis_size(("gx", "gy"))
    key_parts = jnp.concatenate(
        [
            key_term.reshape(tok_count * groups, model_width),
            value_term.reshape(tok_count * groups, model_width),
        ],
        axis=1,
    ).astype(jnp.bfloat16)
    key_parts = lax.all_to_all(key_parts, ("gx", "gy"), 0, 0, tiled=True)
    key_sums = jnp.sum(
        key_parts.reshape(groups, tok_count, 2 * model_width).astype(jnp.float32), axis=0
    )
    d_keys = key_sums[:, :model_width].astype(jnp.bfloat16)
    d_values = key_sums[:, model_width:].astype(jnp.bfloat16)
    d_qkv = jnp.concatenate(
        [d_queries.reshape(tok_count, model_width).astype(jnp.bfloat16), d_keys, d_values], axis=1
    )
    qkv_part = jnp.einsum("td,te->de", normed_b, d_qkv, preferred_element_type=jnp.float32)
    d_normed = (
        jnp.dot(d_qkv, qkv_weight.T, preferred_element_type=jnp.float32)
        .astype(jnp.bfloat16)
        .astype(jnp.float32)
    )
    d_hat = d_normed * norm_gain
    gain_part = jnp.sum(d_normed * normed, axis=0)
    d_trunk = cot_float + inverse_std * (
        d_hat
        - jnp.mean(d_hat, axis=-1, keepdims=True)
        - normed * jnp.mean(d_hat * normed, axis=-1, keepdims=True)
    )
    down_part = jnp.einsum(
        "tr,td->rd", tokens_in, d_trunk, precision=precise, preferred_element_type=jnp.float32
    )
    d_activation = jnp.dot(
        d_trunk, down_weight.T, precision=precise, preferred_element_type=jnp.float32
    ).astype(jnp.bfloat16)
    d_act_grid = (
        from_tokens(d_activation, extent_x, extent_y, extent_z)
        .reshape(voxels, channels)
        .astype(jnp.float32)
    )
    d_hidden = (d_act_grid * gate_sig * (1.0 + hidden * (1.0 - gate_sig))).astype(jnp.bfloat16)
    d_depth = d_hidden.reshape(-1, extent_z, channels)
    d_shifted = jnp.concatenate(
        [
            jnp.pad(d_depth[:, 1:], ((0, 0), (0, 1), (0, 0))),
            d_depth,
            jnp.pad(d_depth[:, :-1], ((0, 0), (1, 0), (0, 0))),
        ],
        axis=2,
    ).reshape(voxels, 3 * channels)
    conv_grid = jnp.einsum("vr,vc->rc", columns, d_shifted, preferred_element_type=jnp.float32)
    conv_part = (
        conv_grid.astype(jnp.bfloat16)
        .reshape(9, channels, 3, channels)
        .transpose(0, 2, 1, 3)
        .reshape(27 * channels, channels)
    )
    d_padded = padded_2(
        d_hidden.reshape(extent_x, extent_y, extent_z, channels), (("gx", 0), ("gy", 1)), 1
    )
    d_columns = plane_columns(d_padded, extent_x, extent_y, True)
    weight_bwd = taps.transpose(0, 3, 1, 2).reshape(9 * channels, 3 * channels)
    grad_features = depth_sum(
        jnp.dot(d_columns, weight_bwd, preferred_element_type=jnp.float32),
        extent_z,
        channels,
        True,
    )
    grad_features = grad_features.reshape(extent_x, extent_y, extent_z, channels).astype(
        jnp.bfloat16
    )
    groups = lax.axis_size(("gx", "gy"))
    gain_rows = gain_part.reshape(groups, -1)
    gain_high = gain_rows.astype(jnp.bfloat16)
    gain_low = (gain_rows - gain_high.astype(jnp.float32)).astype(jnp.bfloat16)
    gain_pair = jnp.concatenate([gain_high, gain_low], axis=1)
    gain_pair = jnp.pad(gain_pair, ((0, 0), (0, 1024 - gain_pair.shape[1])))
    pieces = [
        down_part.astype(jnp.bfloat16),
        qkv_part.astype(jnp.bfloat16),
        out_part.astype(jnp.bfloat16),
    ]
    shapes = [piece.shape for piece in pieces]
    flat = [piece.reshape(groups, -1, 128) for piece in pieces] + [gain_pair.reshape(groups, -1, 128)]
    heights = [piece.shape[1] for piece in flat]
    joined = jnp.concatenate(flat, axis=1)
    summed = lax.psum_scatter(
        joined.reshape(-1, 128), ("gx", "gy"), scatter_dimension=0, tiled=True
    )
    summed = lax.optimization_barrier(summed)
    results = []
    offset = 0
    for height in heights:
        results.append(summed[offset : offset + height])
        offset += height
    down_sum, qkv_sum, out_sum = [
        piece.reshape(shape[0] // groups, shape[1]) for piece, shape in zip(results[:3], shapes)
    ]
    conv_rows = lax.all_to_all(conv_part, ("gx", "gy"), 0, 0, tiled=True)
    conv_sum = jnp.sum(
        conv_rows.reshape(groups, -1, channels).astype(jnp.float32), axis=0
    )
    gain_flat = results[3].reshape(-1).astype(jnp.float32)
    half = gain_high.shape[1]
    gain_sum = gain_flat[:half] + gain_flat[half : 2 * half]
    return (
        grad_features,
        conv_sum.astype(jnp.bfloat16),
        down_sum.astype(jnp.bfloat16),
        gain_sum,
        qkv_sum.astype(jnp.bfloat16),
        out_sum.astype(jnp.bfloat16),
    )


def solution(mesh):
    placed = (
        P(("batch", "gx"), "gy", None, None),
        P(),
        P(),
        P(),
        P(),
        P(),
        P(("batch", "gx"), "gy", None, None),
    )
    return jax.shard_map(
        local,
        mesh=mesh,
        in_specs=placed,
        out_specs=(
            P(("batch", "gx"), "gy", None, None),
            P(("batch", "gx", "gy"), None),
            P(("batch", "gx", "gy"), None),
            P(("batch", "gx", "gy")),
            P(("batch", "gx", "gy"), None),
            P(("batch", "gx", "gy"), None),
        ),
        check_vma=False,
    )
```

profile of v0, /device:TPU:1, one launch (start us, length us, event | category | flops | bytes accessed | tf_op | source)
XLA Modules:
  0.0 390.9 jit_solution(9383881829628084060)
XLA Ops:
  8.2 4.7 %collective-permute-start = (bf16[1,16,4,256]{3,2,1,0:T(4,128)(2,1)S(1)}, bf16[1,16,4,256]{3,2,1,0:T(4,128)(2,1)S(1)}, u32[]{:S(2)}, u32[]{:S(2)}) collective-permute-start(bf16[1,16,4,256]{3,2,1,0:T(4,128)(2,1)S(1)} %get-tuple-element.86), channel_id=1, source_target_pairs={{0,4},{4,8},{8,12},{1,5},{5,9},{9,13},{2,6},{6,10},{10,14},{3,7},{... | collective-permute-start | bytes 98312 | tf_op jit(solution)/shard_map/ppermute | solution.py:18
  14.9 3.3 collective-permute-done.1
  33.2 6.0 %copy.198 = bf16[768,2304]{1,0:T(8,128)(2,1)} copy(bf16[768,2304]{0,1:T(8,128)(2,1)} %bitcast.149) | data formatting | bytes 7077888 | tf_op jit(solution)/shard_map/dot_general | solution.py:74
  39.4 3.7 pad_maximum_fusion.5
  46.4 3.8 fusion.10
  70.1 47.9 %all-gather.2.cloned.1.call-done = bf16[2048,1024]{1,0:T(8,128)(2,1)} async-done(((bf16[128,1024]{1,0:T(8,128)(2,1)}), bf16[2048,1024]{1,0:T(8,128)(2,1)}) %all-gather.2.cloned.1.call-update) | async-done | bytes 4194320 | tf_op jit(solution)/shard_map/all_gather | solution.py:95
  118.0 4.5 %fusion.59 = (bf16[2048,512]{1,0:T(8,128)(2,1)}, bf16[2048,512]{1,0:T(8,128)(2,1)}) fusion(bf16[2048,1024]{1,0:T(8,128)(2,1)} %all-gather.2.cloned.1.call-done), kind=kLoop, calls=%fused_computation.133 | loop fusion | bytes 8388608 | tf_op jit(solution)/shard_map/slice | solution.py:99
  122.5 4.0 %copy.204 = bf16[2048,512]{0,1:T(8,128)(2,1)} copy(bf16[2048,512]{1,0:T(8,128)(2,1)} %get-tuple-element.50) | data formatting | bytes 4194304 | tf_op jit(solution)/shard_map/slice | solution.py:98
  126.5 4.0 %copy.207 = bf16[2048,512]{0,1:T(8,128)(2,1)} copy(bf16[2048,512]{1,0:T(8,128)(2,1)} %get-tuple-element.49) | data formatting | bytes 4194304 | tf_op jit(solution)/shard_map/slice | solution.py:99
  130.5 3.2 fusion.3
  140.1 5.9 %multiply_convert_fusion = bf16[8,64,2048]{2,1,0:T(8,128)(2,1)S(1)} fusion(bf16[128,8,64]{0,2,1:T(8,128)(2,1)S(1)} %bitcast.185, bf16[8,128,2048]{2,1,0:T(8,128)(2,1)S(1)} %get-tuple-element.92, f32[8,128]{1,0:T(8,128)S(1)} %get-tuple-element.91, f32[8,128,2048]{2,1,0:T(8,128)S(1)} %get-tuple-element.90, f32[8,128]{1,0:T(8,128)S(1)} %get-tuple-element.89), kind=kOutput, calls=%fused_computation.16 | convolution fusion | flops 1623195648 | bytes 14819328 | tf_op jit(solution)/shard_map/hij,ihe->jhe/dot_general | solution.py:131
  150.6 5.4 %all-to-all-start = ((bf16[16,128,1024]{1,2,0:T(8,128)(2,1)}), bf16[16,128,1024]{1,2,0:T(8,128)(2,1)}, u32[]{:S(2)}, u32[]{:S(2)}) async-start(bf16[16,128,1024]{1,2,0:T(8,128)(2,1)} %pad_maximum_fusion.1), calls=%async_computation | async-start | bytes 8388608 | tf_op jit(solution)/shard_map/all_to_all | solution.py:149
  178.1 5.7 %fusion.28 = bf16[8,64,128]{2,1,0:T(8,128)(2,1)S(1)} fusion(bf16[2048,8,64]{0,2,1:T(8,128)(2,1)} %bitcast.164, f32[8,128,2048]{2,1,0:T(8,128)} %copy-done.2, f32[8,128]{1,0:T(8,128)S(1)} %get-tuple-element.89), kind=kOutput, calls=%fused_computation.36 | convolution fusion | flops 274792448 | bytes 10620928 | tf_op jit(solution)/shard_map/hij,jhe->ihe/dot_general | solution.py:111
  187.1 12.6 %fusion.31 = bf16[8,64,128]{2,1,0:T(8,128)(2,1)} fusion(bf16[2048,8,64]{0,2,1:T(8,128)(2,1)} %bitcast.157, bf16[8,128,2048]{2,1,0:T(8,128)(2,1)} %copy-done.37, f32[8,128]{1,0:T(8,128)} %copy-done.38, f32[8,128,2048]{2,1,0:T(8,128)} %copy-done.2, f32[8,128]{1,0:T(8,128)S(1)} %get-tuple-element.89), kind=kOutput, calls=%fused_computation.38 | convolution fusion | flops 1621229568 | bytes 14819328 | tf_op jit(solution)/shard_map/hij,jhe->ihe/dot_general | solution.py:125
  199.6 11.7 %all-to-all-done = bf16[16,128,1024]{1,2,0:T(8,128)(2,1)} async-done(((bf16[16,128,1024]{1,2,0:T(8,128)(2,1)}), bf16[16,128,1024]{1,2,0:T(8,128)(2,1)}, u32[]{:S(2)}, u32[]{:S(2)}) %all-to-all-start) | async-done | bytes 4194336 | tf_op jit(solution)/shard_map/all_to_all | solution.py:149
  211.3 3.6 reduce.2
  221.5 3.3 convolution_convert_fusion.2
  224.8 4.4 %reshape.249 = bf16[16,512,128]{2,1,0:T(8,128)(2,1)} reshape(bf16[2048,512]{1,0:T(8,128)(2,1)} %convolution_convert_fusion.2) | data formatting | bytes 4194304 | tf_op jit(solution)/shard_map/reshape | solution.py:225
  229.2 4.3 %reshape.250 = bf16[16,384,128]{2,1,0:T(8,128)(2,1)} reshape(bf16[512,1536]{1,0:T(8,128)(2,1)} %convolution_convert_fusion.3) | data formatting | bytes 3145728 | tf_op jit(solution)/shard_map/reshape | solution.py:225
  234.3 3.8 pad_maximum_fusion
  246.2 3.2 fusion.16
  278.8 4.2 %collective-permute-start.7 = (bf16[18,1,4,256]{3,1,0,2:T(2,128)(2,1)S(1)}, bf16[18,1,4,256]{3,1,0,2:T(2,128)(2,1)S(1)}, u32[]{:S(2)}, u32[]{:S(2)}) collective-permute-start(bf16[18,1,4,256]{3,1,0,2:T(2,128)(2,1)S(1)} %get-tuple-element.69), channel_id=1, source_target_pairs={{0,1},{1,2},{2,3},{4,5},{5,6},{6,7},{8,9},{9,10},{10,11},{12,13},{... | collective-permute-start | bytes 110600 | tf_op jit(solution)/shard_map/ppermute | solution.py:18
  299.0 8.3 %convolution_convert_fusion = bf16[2304,768]{1,0:T(8,128)(2,1)} fusion(bf16[1024,2304]{1,0:T(8,128)(2,1)} %copy-done.28, bf16[1024,256]{1,0:T(8,128)(2,1)S(1)} %concatenate.148, bf16[1024,256]{1,0:T(8,128)(2,1)} %concatenate.147, bf16[1024,256]{1,0:T(8,128)(2,1)} %concatenate.146), kind=kOutput, calls=%fused_computation.9 | convolution fusion | flops 3630366720 | bytes 9830400 | tf_op jit(solution)/shard_map/vr,vc->rc/dot_general | solution.py:192
  307.4 8.8 %reshape.248 = bf16[9,256,3,256]{3,2,1,0:T(4,128)(2,1)} reshape(bf16[2304,768]{1,0:T(8,128)(2,1)} %convolution_convert_fusion) | data formatting | bytes 7077888 | tf_op jit(solution)/shard_map/reshape | solution.py:195
  316.1 4.8 %copy.226 = bf16[9,3,256,256]{3,2,1,0:T(8,128)(2,1)} copy(bf16[9,3,256,256]{3,1,2,0:T(4,128)(2,1)} %bitcast.144) | data formatting | bytes 7077888 | tf_op jit(solution)/shard_map/transpose | solution.py:196
  320.9 6.7 %all-to-all-start.1 = ((bf16[16,432,256]{2,1,0:T(8,128)(2,1)}), bf16[16,432,256]{2,1,0:T(8,128)(2,1)}, u32[]{:S(2)}, u32[]{:S(2)}) async-start(bf16[16,432,256]{2,1,0:T(8,128)(2,1)} %bitcast.148), calls=%async_computation.1 | async-start | bytes 7077888 | tf_op jit(solution)/shard_map/all_to_all | solution.py:240
  327.6 8.0 %copy.219 = bf16[9,3,256,256]{2,1,3,0:T(4,128)(2,1)} copy(bf16[9,3,256,256]{3,2,1,0:T(8,128)(2,1)} %bitcast.151) | data formatting | bytes 7077888 | tf_op jit(solution)/shard_map/reshape | solution.py:69
  335.6 5.1 %copy.241 = bf16[288,8,3,256]{3,1,2,0:T(8,128)(2,1)} copy(bf16[288,8,3,256]{3,2,1,0:T(4,128)(2,1)} %bitcast.146) | data formatting | bytes 7077888
  340.7 5.9 %copy.220 = bf16[768,2304]{1,0:T(8,128)(2,1)} copy(bf16[768,2304]{0,1:T(8,128)(2,1)} %bitcast.150) | data formatting | bytes 7077888 | tf_op jit(solution)/shard_map/dot_general | solution.py:205
  352.3 6.8 %fusion.8 = f32[256,4,3,256]{3,0,2,1:T(8,128)S(1)} fusion(bf16[3,256,2304,1]{2,1,0,3:T(8,128)(2,1)} %bitcast.161, bf16[256,4,2304]{2,0,1:T(8,128)(2,1)} %constant_dynamic-update-slice_fusion.12), kind=kOutput, calls=%fused_computation.10 | convolution fusion | flops 3623878656 | bytes 11403264 | tf_op jit(solution)/shard_map/dot_general | solution.py:205
  360.6 13.9 %all-to-all-done.1 = bf16[16,432,256]{2,1,0:T(8,128)(2,1)} async-done(((bf16[16,432,256]{2,1,0:T(8,128)(2,1)}), bf16[16,432,256]{2,1,0:T(8,128)(2,1)}, u32[]{:S(2)}, u32[]{:S(2)}) %all-to-all-start.1) | async-done | bytes 3538976 | tf_op jit(solution)/shard_map/all_to_all | solution.py:240
  374.5 3.3 reduce_sum.91
  (221 shorter events, 151.0 us)
Async XLA Ops:
  7.2 50.0 %copy-start = (bf16[2048,512]{1,0:T(8,128)(2,1)S(1)}, bf16[2048,512]{1,0:T(8,128)(2,1)}, u32[]{:S(2)}) copy-start(bf16[2048,512]{1,0:T(8,128)(2,1)} %param.9) | copy-start | bytes 6291460
  7.2 110.8 %all-gather.2.cloned.1.call-start = ((), (), s32[]{:S(2)}) async-start(), calls=%async_computation.3 | async-start | bytes 4456448 | tf_op jit(solution)/shard_map/all_gather | solution.py:95
  7.2 20.2 %copy-start.1 = (bf16[6912,256]{1,0:T(8,128)(2,1)S(1)}, bf16[6912,256]{1,0:T(8,128)(2,1)}, u32[]{:S(2)}) copy-start(bf16[6912,256]{1,0:T(8,128)(2,1)} %param.8) | copy-start | bytes 10616836
  8.2 6.7 %collective-permute-start = (bf16[1,16,4,256]{3,2,1,0:T(4,128)(2,1)S(1)}, bf16[1,16,4,256]{3,2,1,0:T(4,128)(2,1)S(1)}, u32[]{:S(2)}, u32[]{:S(2)}) collective-permute-start(bf16[1,16,4,256]{3,2,1,0:T(4,128)(2,1)S(1)} %get-tuple-element.86), channel_id=1, source_target_pairs={{0,4},{4,8},{8,12},{1,5},{5,9},{9,13},{2,6},{6,10},{10,14},{3,7},{... | collective-permute-start | bytes 98312 | tf_op jit(solution)/shard_map/ppermute | solution.py:18
  12.9 5.2 %collective-permute-start.1 = (bf16[1,16,4,256]{3,2,1,0:T(4,128)(2,1)S(1)}, bf16[1,16,4,256]{3,2,1,0:T(4,128)(2,1)S(1)}, u32[]{:S(2)}, u32[]{:S(2)}) collective-permute-start(bf16[1,16,4,256]{3,2,1,0:T(4,128)(2,1)S(1)} %get-tuple-element.85), channel_id=1, source_target_pairs={{4,0},{8,4},{12,8},{5,1},{9,5},{13,9},{6,2},{10,6},{14,10},{7,3},{... | collective-permute-start | bytes 98312 | tf_op jit(solution)/shard_map/ppermute | solution.py:21
  20.9 18.3 %copy-start.5 = (bf16[16,16,4,256]{3,2,1,0:T(4,128)(2,1)}, bf16[16,16,4,256]{3,2,1,0:T(4,128)(2,1)S(1)}, u32[]{:S(2)}) copy-start(bf16[16,16,4,256]{3,2,1,0:T(4,128)(2,1)S(1)} %get-tuple-element.84) | copy-start | bytes 1572868
  21.0 18.3 %copy-start.4 = (bf16[16,16,4,256]{3,2,1,0:T(4,128)(2,1)}, bf16[16,16,4,256]{3,2,1,0:T(4,128)(2,1)S(1)}, u32[]{:S(2)}) copy-start(bf16[16,16,4,256]{3,2,1,0:T(4,128)(2,1)S(1)} %get-tuple-element.82) | copy-start | bytes 1572868
  21.0 6.4 %copy-start.25 = (bf16[18,16,4,256]{3,2,1,0:T(4,128)(2,1)}, bf16[18,16,4,256]{3,2,1,0:T(4,128)(2,1)S(1)}, u32[]{:S(2)}) copy-start(bf16[18,16,4,256]{3,2,1,0:T(4,128)(2,1)S(1)} %constant_dynamic-update-slice_fusion) | copy-start | bytes 1769476
  21.0 18.3 %collective-permute-start.2 = (bf16[18,1,4,256]{3,2,1,0:T(4,128)(2,1)S(1)}, bf16[18,1,4,256]{3,2,1,0:T(4,128)(2,1)S(1)}, u32[]{:S(2)}, u32[]{:S(2)}) collective-permute-start(bf16[18,1,4,256]{3,2,1,0:T(4,128)(2,1)S(1)} %get-tuple-element.75), channel_id=1, source_target_pairs={{0,1},{1,2},{2,3},{4,5},{5,6},{6,7},{8,9},{9,10},{10,11},{12,13},{... | collective-permute-start | bytes 110600 | tf_op jit(solution)/shard_map/ppermute | solution.py:18
  24.2 15.2 %collective-permute-start.3 = (bf16[18,1,4,256]{3,2,1,0:T(4,128)(2,1)S(1)}, bf16[18,1,4,256]{3,2,1,0:T(4,128)(2,1)S(1)}, u32[]{:S(2)}, u32[]{:S(2)}) collective-permute-start(bf16[18,1,4,256]{3,2,1,0:T(4,128)(2,1)S(1)} %get-tuple-element.74), channel_id=1, source_target_pairs={{1,0},{2,1},{3,2},{5,4},{6,5},{7,6},{9,8},{10,9},{11,10},{13,12},{... | collective-permute-start | bytes 110600 | tf_op jit(solution)/shard_map/ppermute | solution.py:21
  50.6 8.4 %copy-start.30 = (f32[512]{0:T(512)S(1)}, f32[512]{0:T(512)}, u32[]{:S(2)}) copy-start(f32[512]{0:T(512)} %param.10) | copy-start | bytes 6148
  58.9 162.1 %copy-start.31 = (f32[128]{0:T(128)}, f32[128]{0:T(128)S(1)}, u32[]{:S(2)}) copy-start(f32[128]{0:T(128)S(1)} %add_rsqrt_fusion) | copy-start | bytes 1540
  133.7 6.3 %copy-start.2 = (f32[8,128,2048]{2,1,0:T(8,128)}, f32[8,128,2048]{2,1,0:T(8,128)S(1)}, u32[]{:S(2)}) copy-start(f32[8,128,2048]{2,1,0:T(8,128)S(1)} %get-tuple-element.90) | copy-start | bytes 25165828
  140.0 5.9 %copy-start.37 = (bf16[8,128,2048]{2,1,0:T(8,128)(2,1)}, bf16[8,128,2048]{2,1,0:T(8,128)(2,1)S(1)}, u32[]{:S(2)}) copy-start(bf16[8,128,2048]{2,1,0:T(8,128)(2,1)S(1)} %get-tuple-element.92) | copy-start | bytes 12582916
  140.0 5.9 %copy-start.38 = (f32[8,128]{1,0:T(8,128)}, f32[8,128]{1,0:T(8,128)S(1)}, u32[]{:S(2)}) copy-start(f32[8,128]{1,0:T(8,128)S(1)} %get-tuple-element.91) | copy-start | bytes 12292
  150.6 60.7 %all-to-all-start = ((bf16[16,128,1024]{1,2,0:T(8,128)(2,1)}), bf16[16,128,1024]{1,2,0:T(8,128)(2,1)}, u32[]{:S(2)}, u32[]{:S(2)}) async-start(bf16[16,128,1024]{1,2,0:T(8,128)(2,1)} %pad_maximum_fusion.1), calls=%async_computation | async-start | bytes 8388608 | tf_op jit(solution)/shard_map/all_to_all | solution.py:149
  156.1 221.8 %reduce-scatter.5.cloned.1.call-start = ((), (), s32[]{:S(2)}) async-start(), calls=%async_computation.4 | async-start | bytes 4491264
  214.9 6.6 %copy-start.3 = (bf16[128,2048]{1,0:T(8,128)(2,1)S(1)}, bf16[128,2048]{1,0:T(8,128)(2,1)}, u32[]{:S(2)}) copy-start(bf16[128,2048]{1,0:T(8,128)(2,1)} %reshape.231) | copy-start | bytes 1572868
  221.0 12.5 %copy-start.33 = (f32[128]{0:T(128)}, f32[128]{0:T(128)S(1)}, u32[]{:S(2)}) copy-start(f32[128]{0:T(128)S(1)} %get-tuple-element.94) | copy-start | bytes 1540
  238.2 5.7 %copy-start.16 = (bf16[1024,256]{1,0:T(8,128)(2,1)S(1)}, bf16[1024,256]{1,0:T(8,128)(2,1)}, u32[]{:S(2)}) copy-start(bf16[1024,256]{1,0:T(8,128)(2,1)} %reshape.246) | copy-start | bytes 1572868
  238.2 5.8 %copy-start.17 = (bf16[1024,256]{1,0:T(8,128)(2,1)S(1)}, bf16[1024,256]{1,0:T(8,128)(2,1)}, u32[]{:S(2)}) copy-start(bf16[1024,256]{1,0:T(8,128)(2,1)} %reshape.247) | copy-start | bytes 1572868
  238.2 8.0 %copy-start.24 = (f32[128,512]{1,0:T(8,128)S(1)}, f32[128,512]{1,0:T(8,128)}, u32[]{:S(2)}) copy-start(f32[128,512]{1,0:T(8,128)} %copy-done.23) | copy-start | bytes 786436
  238.2 8.0 %copy-start.32 = (f32[128]{0:T(128)S(1)}, f32[128]{0:T(128)}, u32[]{:S(2)}) copy-start(f32[128]{0:T(128)} %copy-done.31) | copy-start | bytes 1540
  238.2 7.9 %copy-start.34 = (f32[128]{0:T(128)S(1)}, f32[128]{0:T(128)}, u32[]{:S(2)}) copy-start(f32[128]{0:T(128)} %copy-done.33) | copy-start | bytes 1540
  238.2 7.9 %copy-start.36 = (f32[128]{0:T(128)S(1)}, f32[128]{0:T(128)}, u32[]{:S(2)}) copy-start(f32[128]{0:T(128)} %copy-done.35) | copy-start | bytes 1540
  263.3 13.0 %collective-permute-start.4 = (bf16[1,16,4,256]{3,2,1,0:T(4,128)(2,1)S(1)}, bf16[1,16,4,256]{3,2,1,0:T(4,128)(2,1)S(1)}, u32[]{:S(2)}, u32[]{:S(2)}) collective-permute-start(bf16[1,16,4,256]{3,2,1,0:T(4,128)(2,1)S(1)} %slice.178), channel_id=1, source_target_pairs={{0,4},{4,8},{8,12},{1,5},{5,9},{9,13},{2,6},{6,10},{10,14},{3,7},{... | collective-permute-start | bytes 98312 | tf_op jit(solution)/shard_map/ppermute | solution.py:18
  266.2 10.2 %collective-permute-start.5 = (bf16[1,16,4,256]{3,2,1,0:T(4,128)(2,1)S(1)}, bf16[1,16,4,256]{3,2,1,0:T(4,128)(2,1)S(1)}, u32[]{:S(2)}, u32[]{:S(2)}) collective-permute-start(bf16[1,16,4,256]{3,2,1,0:T(4,128)(2,1)S(1)} %slice.180), channel_id=1, source_target_pairs={{4,0},{8,4},{12,8},{5,1},{9,5},{13,9},{6,2},{10,6},{14,10},{7,3},{... | collective-permute-start | bytes 98312 | tf_op jit(solution)/shard_map/ppermute | solution.py:21
  277.5 7.7 %collective-permute-start.6 = (bf16[18,1,4,256]{3,1,0,2:T(2,128)(2,1)S(1)}, bf16[18,1,4,256]{3,1,0,2:T(2,128)(2,1)S(1)}, u32[]{:S(2)}, u32[]{:S(2)}) collective-permute-start(bf16[18,1,4,256]{3,1,0,2:T(2,128)(2,1)S(1)} %get-tuple-element.70), channel_id=1, source_target_pairs={{1,0},{2,1},{3,2},{5,4},{6,5},{7,6},{9,8},{10,9},{11,10},{13,12},{... | collective-permute-start | bytes 110600 | tf_op jit(solution)/shard_map/ppermute | solution.py:21
  278.8 7.0 %collective-permute-start.7 = (bf16[18,1,4,256]{3,1,0,2:T(2,128)(2,1)S(1)}, bf16[18,1,4,256]{3,1,0,2:T(2,128)(2,1)S(1)}, u32[]{:S(2)}, u32[]{:S(2)}) collective-permute-start(bf16[18,1,4,256]{3,1,0,2:T(2,128)(2,1)S(1)} %get-tuple-element.69), channel_id=1, source_target_pairs={{0,1},{1,2},{2,3},{4,5},{5,6},{6,7},{8,9},{9,10},{10,11},{12,13},{... | collective-permute-start | bytes 110600 | tf_op jit(solution)/shard_map/ppermute | solution.py:18
  320.9 53.6 %all-to-all-start.1 = ((bf16[16,432,256]{2,1,0:T(8,128)(2,1)}), bf16[16,432,256]{2,1,0:T(8,128)(2,1)}, u32[]{:S(2)}, u32[]{:S(2)}) async-start(bf16[16,432,256]{2,1,0:T(8,128)(2,1)} %bitcast.148), calls=%async_computation.1 | async-start | bytes 7077888 | tf_op jit(solution)/shard_map/all_to_all | solution.py:240
  340.7 7.8 %copy-start.21 = (bf16[16,16,4,256]{3,1,0,2:T(8,128)(2,1)S(1)}, bf16[16,16,4,256]{3,1,0,2:T(8,128)(2,1)}, u32[]{:S(2)}) copy-start(bf16[16,16,4,256]{3,1,0,2:T(8,128)(2,1)} %get-tuple-element.58) | copy-start | bytes 1572868
  340.7 8.7 %copy-start.14 = (bf16[16,16,4,256]{3,1,0,2:T(8,128)(2,1)S(1)}, bf16[16,16,4,256]{3,1,0,2:T(8,128)(2,1)}, u32[]{:S(2)}) copy-start(bf16[16,16,4,256]{3,1,0,2:T(8,128)(2,1)} %get-tuple-element.78) | copy-start | bytes 1572868
  (19 other events, 43.5 us)
Sparse Core Ops, SparseCore 0:
  62.4 55.5 all-gather.1
  238.3 73.5 reduce-scatter.4
where the time goes:
time: 399 us; the launch traced here: 391 us
  local copies, waits for them, and re-layouts  162 us (41%)
  waiting for transfers between devices  77.4 us (19%)
  matrix products  70.5 us (18%)
  starting transfers between devices  33.5 us (8%)
  other arithmetic  32.7 us (8%)
  between operations  15.3 us (4%)
    all_gather x1, waiting for transfers between devices, local(): lax.all_gather(qkv_rows[:, model_width:], ('gx', 'gy'), axis=0, tiled=True)  47.9 us
    unnamed x111, local copies, waits for them, and re-layouts  31.1 us
    convert_element_type x6, local copies, waits for them, and re-layouts, local(): d_act_grid = from_tokens(d_activation, extent_x, extent_y, extent_z).resh...  17.8 us
    reshape x9, local copies, waits for them, and re-layouts, plane_columns(): padded[start_x:start_x + extent_x, start_y:start_y + extent_y]  17.7 us
    ppermute x4, starting transfers between devices, padded_2(): lax.ppermute(lax.slice_in_dim(block, block.shape[dim] - width, None, axis...  14.9 us
    all_to_all x1, waiting for transfers between devices, local(): conv_rows = lax.all_to_all(conv_part, ('gx', 'gy'), 0, 0, tiled=True)  13.9 us
    dot_general x1, matrix products, local(): jnp.einsum('hij,jhe->ihe', d_scores, keys_h, precision=precise, preferred...  12.6 us
    all_to_all x1, waiting for transfers between devices, local(): key_parts = lax.all_to_all(key_parts, ('gx', 'gy'), 0, 0, tiled=True)  11.7 us
  transfers between devices with their start and end apart: 12, of which 5 were waited for; matrix products, arithmetic and copies ran while one was open for 43% of the time, Pallas kernels for 0%

commit v1 on v0

--- a/solution.py
+++ b/solution.py
@@ -181,21 +181,24 @@
     )
     d_hidden = (d_act_grid * gate_sig * (1.0 + hidden * (1.0 - gate_sig))).astype(jnp.bfloat16)
     d_depth = d_hidden.reshape(-1, extent_z, channels)
-    d_shifted = jnp.concatenate(
-        [
-            jnp.pad(d_depth[:, 1:], ((0, 0), (0, 1), (0, 0))),
-            d_depth,
-            jnp.pad(d_depth[:, :-1], ((0, 0), (1, 0), (0, 0))),
-        ],
-        axis=2,
-    ).reshape(voxels, 3 * channels)
-    conv_grid = jnp.einsum("vr,vc->rc", columns, d_shifted, preferred_element_type=jnp.float32)
-    conv_part = (
-        conv_grid.astype(jnp.bfloat16)
-        .reshape(9, channels, 3, channels)
-        .transpose(0, 2, 1, 3)
-        .reshape(27 * channels, channels)
-    )
+    d_shifts = [
+        jnp.pad(d_depth[:, 1:], ((0, 0), (0, 1), (0, 0))),
+        d_depth,
+        jnp.pad(d_depth[:, :-1], ((0, 0), (1, 0), (0, 0))),
+    ]
+    conv_blocks = [
+        jnp.einsum(
+            "vr,vc->rc",
+            columns,
+            shifted.reshape(voxels, channels),
+            preferred_element_type=jnp.float32,
+        )
+        .astype(jnp.bfloat16)
+        .reshape(9, channels, channels)
+        for shifted in d_shifts
+    ]
+    conv_part = jnp.stack(conv_blocks, axis=1).reshape(27 * channels, channels)
+    conv_part, d_hidden = lax.optimization_barrier((conv_part, d_hidden))
     d_padded = padded_2(
         d_hidden.reshape(extent_x, extent_y, extent_z, channels), (("gx", 0), ("gy", 1)), 1
     )

time: 399 us -> 405 us (1.015)
  local copies, waits for them, and re-layouts: 162 us -> 137 us
  waiting for transfers between devices: 77.4 us -> 99.9 us
  matrix products: 70.5 us -> 79.3 us
    all_to_all x1, waiting for transfers between devices: 11.7 us -> 33.7 us  [local(): key_parts = lax.all_to_all(key_parts, ('gx', 'gy'), 0, 0, tiled=True)]
    ppermute x4, waiting for transfers between devices: 3.28 us -> 18.2 us  [padded_2(): lax.ppermute(lax.slice_in_dim(block, 0, width, axis=dim), axis, backward)]
    all_to_all x1, waiting for transfers between devices: 13.9 us -> 0.01 us  [local(): conv_rows = lax.all_to_all(conv_part, ('gx', 'gy'), 0, 0, tiled=True)]
    dot_general x1, matrix products: 3.12 us -> 16.3 us  [local(): jnp.einsum('ihe,jhe->hij', d_att_h, values_h, preferred_element_type=jnp....]
    reshape x1 -> x3, local copies, waits for them, and re-layouts: 8.76 us -> 3.01 us  [the longest x2 2.88 us: local(): shifted.reshape(voxels, channels)]
    transpose x1 -> x0, local copies, waits for them, and re-layouts: 4.76 us -> none  [local(): conv_part = conv_grid.astype(jnp.bfloat16).reshape(9, channels, 3, channe...]
    convert_element_type x6 -> x5, local copies, waits for them, and re-layouts: 17.8 us -> 13.2 us  [local(): d_act_grid = from_tokens(d_activation, extent_x, extent_y, extent_z).resh...]
    concatenate x3 -> x0, local copies, waits for them, and re-layouts: 4.09 us -> none  [local(): jnp.concatenate([jnp.pad(d_depth[:, 1:], ((0, 0), (0, 1), (0, 0))), d_dep...]
  transfers between devices with their start and end apart: 12 -> 12, of which waited for: 5 -> 4; matrix products, arithmetic and copies ran while one was open for 43% -> 36% of each run, Pallas kernels for 0% -> 0%
where the time goes in v1:
time: 405 us; the launch traced here: 398 us
  local copies, waits for them, and re-layouts  137 us (34%)
  waiting for transfers between devices  99.9 us (25%)
  matrix products  79.3 us (20%)
  other arithmetic  34.5 us (9%)
  starting transfers between devices  31 us (8%)
  between operations  15.4 us (4%)
    all_gather x1, waiting for transfers between devices, local(): lax.all_gather(qkv_rows[:, model_width:], ('gx', 'gy'), axis=0, tiled=True)  47.9 us
    all_to_all x1, waiting for transfers between devices, local(): key_parts = lax.all_to_all(key_parts, ('gx', 'gy'), 0, 0, tiled=True)  33.7 us
    unnamed x119, local copies, waits for them, and re-layouts  28.7 us
    ppermute x4, waiting for transfers between devices, padded_2(): lax.ppermute(lax.slice_in_dim(block, 0, width, axis=dim), axis, backward)  18.2 us
    reshape x9, local copies, waits for them, and re-layouts, plane_columns(): padded[start_x:start_x + extent_x, start_y:start_y + extent_y]  17.7 us
    dot_general x1, matrix products, local(): jnp.einsum('ihe,jhe->hij', d_att_h, values_h, preferred_element_type=jnp....  16.3 us
    ppermute x4, starting transfers between devices, padded_2(): lax.ppermute(lax.slice_in_dim(block, block.shape[dim] - width, None, axis...  14.6 us
    convert_element_type x5, local copies, waits for them, and re-layouts, local(): d_act_grid = from_tokens(d_activation, extent_x, extent_y, extent_z).resh...  13.2 us
  transfers between devices with their start and end apart: 12, of which 4 were waited for; matrix products, arithmetic and copies ran while one was open for 36% of the time, Pallas kernels for 0%

profile of v1, /device:TPU:1, one launch (start us, length us, event | category | flops | bytes accessed | tf_op | source)
XLA Modules:
  0.0 397.6 jit_solution(17159091404439475648)
XLA Ops:
  8.2 4.7 %collective-permute-start = (bf16[1,16,4,256]{3,2,1,0:T(4,128)(2,1)S(1)}, bf16[1,16,4,256]{3,2,1,0:T(4,128)(2,1)S(1)}, u32[]{:S(2)}, u32[]{:S(2)}) collective-permute-start(bf16[1,16,4,256]{3,2,1,0:T(4,128)(2,1)S(1)} %get-tuple-element.90), channel_id=1, source_target_pairs={{0,4},{4,8},{8,12},{1,5},{5,9},{9,13},{2,6},{6,10},{10,14},{3,7},{... | collective-permute-start | bytes 98312 | tf_op jit(solution)/shard_map/ppermute | solution.py:18
  14.9 3.3 collective-permute-done.1
  33.0 6.1 %copy.218 = bf16[768,2304]{1,0:T(8,128)(2,1)} copy(bf16[768,2304]{0,1:T(8,128)(2,1)} %bitcast.160) | data formatting | bytes 7077888 | tf_op jit(solution)/shard_map/dot_general | solution.py:74
  39.3 3.6 pad_maximum_fusion.7
  46.2 3.8 fusion.10
  69.9 47.9 %all-gather.2.cloned.1.call-done = bf16[2048,1024]{1,0:T(8,128)(2,1)} async-done(((bf16[128,1024]{1,0:T(8,128)(2,1)}), bf16[2048,1024]{1,0:T(8,128)(2,1)}) %all-gather.2.cloned.1.call-update) | async-done | bytes 4194320 | tf_op jit(solution)/shard_map/all_gather | solution.py:95
  117.8 4.5 %fusion.55 = (bf16[2048,512]{1,0:T(8,128)(2,1)}, bf16[2048,512]{1,0:T(8,128)(2,1)}) fusion(bf16[2048,1024]{1,0:T(8,128)(2,1)} %all-gather.2.cloned.1.call-done), kind=kLoop, calls=%fused_computation.135 | loop fusion | bytes 8388608 | tf_op jit(solution)/shard_map/slice | solution.py:99
  122.3 4.0 copy.224
  126.3 4.0 %copy.227 = bf16[2048,512]{0,1:T(8,128)(2,1)} copy(bf16[2048,512]{1,0:T(8,128)(2,1)} %get-tuple-element.51) | data formatting | bytes 4194304 | tf_op jit(solution)/shard_map/slice | solution.py:99
  130.3 3.2 fusion.3
  136.7 16.3 %fusion = (f32[8,128]{1,0:T(8,128)S(1)}, bf16[8,128,2048]{2,1,0:T(8,128)(2,1)S(1)}) fusion(f32[8,128]{1,0:T(8,128)S(1)} %get-tuple-element.93, f32[8,128,2048]{2,1,0:T(8,128)S(1)} %get-tuple-element.94, bf16[128,8,64]{0,2,1:T(8,128)(2,1)S(1)} %bitcast.203, bf16[2048,8,64]{0,2,1:T(8,128)(2,1)S(1)} %bitcast.173), kind=kOutput, calls=%fused_computation.2 | convolution fusion | flops 281017344 | bytes 14819328 | tf_op jit(solution)/shard_map/ihe,jhe->hij/dot_general | solution.py:120
  153.0 5.9 %multiply_convert_fusion = bf16[8,64,2048]{2,1,0:T(8,128)(2,1)S(1)} fusion(bf16[128,8,64]{0,2,1:T(8,128)(2,1)S(1)} %bitcast.198, bf16[8,128,2048]{2,1,0:T(8,128)(2,1)S(1)} %get-tuple-element.96, f32[8,128]{1,0:T(8,128)S(1)} %get-tuple-element.95, f32[8,128,2048]{2,1,0:T(8,128)S(1)} %get-tuple-element.94, f32[8,128]{1,0:T(8,128)S(1)} %get-tuple-element.93), kind=kOutput, calls=%fused_computation.15 | convolution fusion | flops 1623195648 | bytes 14819328 | tf_op jit(solution)/shard_map/hij,ihe->jhe/dot_general | solution.py:131
  163.6 5.4 %all-to-all-start = ((bf16[16,128,1024]{1,2,0:T(8,128)(2,1)}), bf16[16,128,1024]{1,2,0:T(8,128)(2,1)}, u32[]{:S(2)}, u32[]{:S(2)}) async-start(bf16[16,128,1024]{1,2,0:T(8,128)(2,1)} %pad_maximum_fusion.1), calls=%async_computation | async-start | bytes 8388608 | tf_op jit(solution)/shard_map/all_to_all | solution.py:149
  169.1 5.7 %fusion.23 = bf16[8,64,128]{2,1,0:T(8,128)(2,1)S(1)} fusion(bf16[2048,8,64]{0,2,1:T(8,128)(2,1)} %bitcast.172, f32[8,128,2048]{2,1,0:T(8,128)} %copy-done.2, f32[8,128]{1,0:T(8,128)S(1)} %get-tuple-element.93), kind=kOutput, calls=%fused_computation.34 | convolution fusion | flops 274792448 | bytes 10620928 | tf_op jit(solution)/shard_map/hij,jhe->ihe/dot_general | solution.py:111
  178.0 12.6 %fusion.26 = bf16[8,64,128]{2,1,0:T(8,128)(2,1)} fusion(bf16[2048,8,64]{0,2,1:T(8,128)(2,1)} %bitcast.166, bf16[8,128,2048]{2,1,0:T(8,128)(2,1)} %copy-done.38, f32[8,128]{1,0:T(8,128)} %copy-done.39, f32[8,128,2048]{2,1,0:T(8,128)} %copy-done.2, f32[8,128]{1,0:T(8,128)S(1)} %get-tuple-element.93), kind=kOutput, calls=%fused_computation.36 | convolution fusion | flops 1621229568 | bytes 14819328 | tf_op jit(solution)/shard_map/hij,jhe->ihe/dot_general | solution.py:125
  190.6 33.7 %all-to-all-done = bf16[16,128,1024]{1,2,0:T(8,128)(2,1)} async-done(((bf16[16,128,1024]{1,2,0:T(8,128)(2,1)}), bf16[16,128,1024]{1,2,0:T(8,128)(2,1)}, u32[]{:S(2)}, u32[]{:S(2)}) %all-to-all-start) | async-done | bytes 4194336 | tf_op jit(solution)/shard_map/all_to_all | solution.py:149
  224.3 3.5 reduce.2
  234.3 3.3 convolution_convert_fusion.4
  237.6 4.4 %reshape.244 = bf16[16,512,128]{2,1,0:T(8,128)(2,1)} reshape(bf16[2048,512]{1,0:T(8,128)(2,1)} %convolution_convert_fusion.4) | data formatting | bytes 4194304 | tf_op jit(solution)/shard_map/reshape | solution.py:228
  241.9 4.3 %reshape.245 = bf16[16,384,128]{2,1,0:T(8,128)(2,1)} reshape(bf16[512,1536]{1,0:T(8,128)(2,1)} %convolution_convert_fusion.5) | data formatting | bytes 3145728 | tf_op jit(solution)/shard_map/reshape | solution.py:228
  247.1 4.1 %pad_maximum_fusion = bf16[16,1032,128]{2,1,0:T(8,128)(2,1)} fusion(bf16[16,8,128]{2,1,0:T(8,128)(2,1)S(1)} %bitcast.199, bf16[16,128,128]{2,1,0:T(8,128)(2,1)} %reshape.246, bf16[16,384,128]{2,1,0:T(8,128)(2,1)} %reshape.245, bf16[16,512,128]{2,1,0:T(8,128)(2,1)} %reshape.244), kind=kLoop, calls=%fused_computation.13 | loop fusion | flops 16908288 | bytes 8454144 | tf_op jit(solution)/shard_map/concatenate | solution.py:230
  281.3 3.2 fusion.16
  306.4 3.9 convolution_convert_fusion.2
  320.4 4.4 %all-to-all-start.1 = ((bf16[16,432,256]{2,1,0:T(8,128)(2,1)}), bf16[16,432,256]{2,1,0:T(8,128)(2,1)}, u32[]{:S(2)}, u32[]{:S(2)}) async-start(bf16[16,432,256]{2,1,0:T(8,128)(2,1)} %bitcast.159), calls=%async_computation.1 | async-start | bytes 7077888 | tf_op jit(solution)/shard_map/all_to_all | solution.py:243
  328.9 4.0 %collective-permute-start.7 = (bf16[18,1,4,256]{3,2,1,0:T(4,128)(2,1)S(1)}, bf16[18,1,4,256]{3,2,1,0:T(4,128)(2,1)S(1)}, u32[]{:S(2)}, u32[]{:S(2)}) collective-permute-start(bf16[18,1,4,256]{3,2,1,0:T(4,128)(2,1)S(1)} %get-tuple-element.72), channel_id=1, source_target_pairs={{0,1},{1,2},{2,3},{4,5},{5,6},{6,7},{8,9},{9,10},{10,11},{12,13},{... | collective-permute-start | bytes 110600 | tf_op jit(solution)/shard_map/ppermute | solution.py:18
  332.9 8.0 %copy.248 = bf16[9,3,256,256]{2,1,3,0:T(4,128)(2,1)} copy(bf16[9,3,256,256]{3,2,1,0:T(8,128)(2,1)} %bitcast.162) | data formatting | bytes 7077888 | tf_op jit(solution)/shard_map/reshape | solution.py:69
  340.9 5.1 %copy.266 = bf16[288,8,3,256]{3,1,2,0:T(8,128)(2,1)} copy(bf16[288,8,3,256]{3,2,1,0:T(4,128)(2,1)} %bitcast.157) | data formatting | bytes 7077888
  346.0 5.8 %copy.249 = bf16[768,2304]{1,0:T(8,128)(2,1)} copy(bf16[768,2304]{0,1:T(8,128)(2,1)} %bitcast.161) | data formatting | bytes 7077888 | tf_op jit(solution)/shard_map/dot_general | solution.py:208
  354.1 15.0 %collective-permute-done.6 = bf16[18,1,4,256]{3,2,1,0:T(4,128)(2,1)S(1)} collective-permute-done((bf16[18,1,4,256]{3,2,1,0:T(4,128)(2,1)S(1)}, bf16[18,1,4,256]{3,2,1,0:T(4,128)(2,1)S(1)}, u32[]{:S(2)}, u32[]{:S(2)}) %collective-permute-start.6) | collective-permute-done | bytes 36896 | tf_op jit(solution)/shard_map/ppermute | solution.py:21
  369.1 4.3 %pad_maximum_fusion.3 = (bf16[16,16,4,256]{3,2,1,0:T(4,128)(2,1)S(1)}, bf16[16,16,4,256]{3,2,1,0:T(4,128)(2,1)S(1)}, bf16[16,16,4,256]{3,2,1,0:T(4,128)(2,1)S(1)...) fusion(bf16[18,16,4,256]{3,2,1,0:T(4,128)(2,1)} %copy-done.24, ...), kind=kLoop, calls=%fused_computation.70 | loop fusion | flops 1572864 | bytes 3809280 | tf_op jit(solution)/shard_map/concatenate | solution.py:22
  375.9 3.8 fusion.8
  381.3 3.3 reduce_sum.91
  (234 shorter events, 137.1 us)
Async XLA Ops:
  7.2 49.8 %copy-start = (bf16[2048,512]{1,0:T(8,128)(2,1)S(1)}, bf16[2048,512]{1,0:T(8,128)(2,1)}, u32[]{:S(2)}) copy-start(bf16[2048,512]{1,0:T(8,128)(2,1)} %param.9) | copy-start | bytes 6291460
  7.2 110.6 %all-gather.2.cloned.1.call-start = ((), (), s32[]{:S(2)}) async-start(), calls=%async_computation.3 | async-start | bytes 4456448 | tf_op jit(solution)/shard_map/all_gather | solution.py:95
  7.2 19.9 %copy-start.1 = (bf16[6912,256]{1,0:T(8,128)(2,1)S(1)}, bf16[6912,256]{1,0:T(8,128)(2,1)}, u32[]{:S(2)}) copy-start(bf16[6912,256]{1,0:T(8,128)(2,1)} %param.8) | copy-start | bytes 10616836
  8.2 6.7 %collective-permute-start = (bf16[1,16,4,256]{3,2,1,0:T(4,128)(2,1)S(1)}, bf16[1,16,4,256]{3,2,1,0:T(4,128)(2,1)S(1)}, u32[]{:S(2)}, u32[]{:S(2)}) collective-permute-start(bf16[1,16,4,256]{3,2,1,0:T(4,128)(2,1)S(1)} %get-tuple-element.90), channel_id=1, source_target_pairs={{0,4},{4,8},{8,12},{1,5},{5,9},{9,13},{2,6},{6,10},{10,14},{3,7},{... | collective-permute-start | bytes 98312 | tf_op jit(solution)/shard_map/ppermute | solution.py:18
  12.9 5.2 %collective-permute-start.1 = (bf16[1,16,4,256]{3,2,1,0:T(4,128)(2,1)S(1)}, bf16[1,16,4,256]{3,2,1,0:T(4,128)(2,1)S(1)}, u32[]{:S(2)}, u32[]{:S(2)}) collective-permute-start(bf16[1,16,4,256]{3,2,1,0:T(4,128)(2,1)S(1)} %get-tuple-element.89), channel_id=1, source_target_pairs={{4,0},{8,4},{12,8},{5,1},{9,5},{13,9},{6,2},{10,6},{14,10},{7,3},{... | collective-permute-start | bytes 98312 | tf_op jit(solution)/shard_map/ppermute | solution.py:21
  20.7 18.4 %copy-start.5 = (bf16[16,16,4,256]{3,2,1,0:T(4,128)(2,1)}, bf16[16,16,4,256]{3,2,1,0:T(4,128)(2,1)S(1)}, u32[]{:S(2)}) copy-start(bf16[16,16,4,256]{3,2,1,0:T(4,128)(2,1)S(1)} %get-tuple-element.88) | copy-start | bytes 1572868
  20.7 18.5 %copy-start.4 = (bf16[16,16,4,256]{3,2,1,0:T(4,128)(2,1)}, bf16[16,16,4,256]{3,2,1,0:T(4,128)(2,1)S(1)}, u32[]{:S(2)}) copy-start(bf16[16,16,4,256]{3,2,1,0:T(4,128)(2,1)S(1)} %get-tuple-element.86) | copy-start | bytes 1572868
  20.7 9.4 %copy-start.25 = (bf16[18,16,4,256]{3,2,1,0:T(4,128)(2,1)}, bf16[18,16,4,256]{3,2,1,0:T(4,128)(2,1)S(1)}, u32[]{:S(2)}) copy-start(bf16[18,16,4,256]{3,2,1,0:T(4,128)(2,1)S(1)} %constant_dynamic-update-slice_fusion) | copy-start | bytes 1769476
  20.8 18.5 %collective-permute-start.2 = (bf16[18,1,4,256]{3,2,1,0:T(4,128)(2,1)S(1)}, bf16[18,1,4,256]{3,2,1,0:T(4,128)(2,1)S(1)}, u32[]{:S(2)}, u32[]{:S(2)}) collective-permute-start(bf16[18,1,4,256]{3,2,1,0:T(4,128)(2,1)S(1)} %get-tuple-element.78), channel_id=1, source_target_pairs={{0,1},{1,2},{2,3},{4,5},{5,6},{6,7},{8,9},{9,10},{10,11},{12,13},{... | collective-permute-start | bytes 110600 | tf_op jit(solution)/shard_map/ppermute | solution.py:18
  23.9 15.4 %collective-permute-start.3 = (bf16[18,1,4,256]{3,2,1,0:T(4,128)(2,1)S(1)}, bf16[18,1,4,256]{3,2,1,0:T(4,128)(2,1)S(1)}, u32[]{:S(2)}, u32[]{:S(2)}) collective-permute-start(bf16[18,1,4,256]{3,2,1,0:T(4,128)(2,1)S(1)} %get-tuple-element.77), channel_id=1, source_target_pairs={{1,0},{2,1},{3,2},{5,4},{6,5},{7,6},{9,8},{10,9},{11,10},{13,12},{... | collective-permute-start | bytes 110600 | tf_op jit(solution)/shard_map/ppermute | solution.py:21
  50.4 8.4 %copy-start.31 = (f32[512]{0:T(512)S(1)}, f32[512]{0:T(512)}, u32[]{:S(2)}) copy-start(f32[512]{0:T(512)} %param.10) | copy-start | bytes 6148
  58.7 175.1 %copy-start.32 = (f32[128]{0:T(128)}, f32[128]{0:T(128)S(1)}, u32[]{:S(2)}) copy-start(f32[128]{0:T(128)S(1)} %add_rsqrt_fusion) | copy-start | bytes 1540
  133.5 19.5 %copy-start.2 = (f32[8,128,2048]{2,1,0:T(8,128)}, f32[8,128,2048]{2,1,0:T(8,128)S(1)}, u32[]{:S(2)}) copy-start(f32[8,128,2048]{2,1,0:T(8,128)S(1)} %get-tuple-element.94) | copy-start | bytes 25165828
  136.7 16.4 %copy-start.26 = (bf16[128,512]{0,1:T(8,128)(2,1)S(1)}, bf16[128,512]{0,1:T(8,128)(2,1)}, u32[]{:S(2)}) copy-start(bf16[128,512]{0,1:T(8,128)(2,1)} %copy.225) | copy-start | bytes 393220
  153.0 5.9 %copy-start.38 = (bf16[8,128,2048]{2,1,0:T(8,128)(2,1)}, bf16[8,128,2048]{2,1,0:T(8,128)(2,1)S(1)}, u32[]{:S(2)}) copy-start(bf16[8,128,2048]{2,1,0:T(8,128)(2,1)S(1)} %get-tuple-element.96) | copy-start | bytes 12582916
  153.0 5.9 %copy-start.39 = (f32[8,128]{1,0:T(8,128)}, f32[8,128]{1,0:T(8,128)S(1)}, u32[]{:S(2)}) copy-start(f32[8,128]{1,0:T(8,128)S(1)} %get-tuple-element.95) | copy-start | bytes 12292
  163.6 60.7 %all-to-all-start = ((bf16[16,128,1024]{1,2,0:T(8,128)(2,1)}), bf16[16,128,1024]{1,2,0:T(8,128)(2,1)}, u32[]{:S(2)}, u32[]{:S(2)}) async-start(bf16[16,128,1024]{1,2,0:T(8,128)(2,1)} %pad_maximum_fusion.1), calls=%async_computation | async-start | bytes 8388608 | tf_op jit(solution)/shard_map/all_to_all | solution.py:149
  169.0 215.5 %reduce-scatter.5.cloned.1.call-start = ((), (), s32[]{:S(2)}) async-start(), calls=%async_computation.4 | async-start | bytes 4491264
  227.9 6.4 %copy-start.3 = (bf16[128,2048]{1,0:T(8,128)(2,1)S(1)}, bf16[128,2048]{1,0:T(8,128)(2,1)}, u32[]{:S(2)}) copy-start(bf16[128,2048]{1,0:T(8,128)(2,1)} %reshape.233) | copy-start | bytes 1572868
  233.8 12.4 %copy-start.34 = (f32[128]{0:T(128)}, f32[128]{0:T(128)S(1)}, u32[]{:S(2)}) copy-start(f32[128]{0:T(128)S(1)} %get-tuple-element.98) | copy-start | bytes 1540
  273.3 5.7 %copy-start.17 = (bf16[1024,256]{1,0:T(8,128)(2,1)S(1)}, bf16[1024,256]{1,0:T(8,128)(2,1)}, u32[]{:S(2)}) copy-start(bf16[1024,256]{1,0:T(8,128)(2,1)} %reshape.227) | copy-start | bytes 1572868
  273.3 5.8 %copy-start.18 = (bf16[1024,256]{1,0:T(8,128)(2,1)S(1)}, bf16[1024,256]{1,0:T(8,128)(2,1)}, u32[]{:S(2)}) copy-start(bf16[1024,256]{1,0:T(8,128)(2,1)} %reshape.228) | copy-start | bytes 1572868
  273.3 8.0 %copy-start.23 = (f32[128,512]{1,0:T(8,128)S(1)}, f32[128,512]{1,0:T(8,128)}, u32[]{:S(2)}) copy-start(f32[128,512]{1,0:T(8,128)} %copy-done.22) | copy-start | bytes 786436
  273.3 8.0 %copy-start.33 = (f32[128]{0:T(128)S(1)}, f32[128]{0:T(128)}, u32[]{:S(2)}) copy-start(f32[128]{0:T(128)} %copy-done.32) | copy-start | bytes 1540
  273.3 8.0 %copy-start.35 = (f32[128]{0:T(128)S(1)}, f32[128]{0:T(128)}, u32[]{:S(2)}) copy-start(f32[128]{0:T(128)} %copy-done.34) | copy-start | bytes 1540
  273.3 8.0 %copy-start.37 = (f32[128]{0:T(128)S(1)}, f32[128]{0:T(128)}, u32[]{:S(2)}) copy-start(f32[128]{0:T(128)} %copy-done.36) | copy-start | bytes 1540
  304.3 6.0 %slice-start = ((s8[4718592]{0:T(1024)(128)(4,1)}), s8[4194304]{0:T(1024)(128)(4,1)S(1)}, s32[]{:S(2)}) async-start(s8[4718592]{0:T(1024)(128)(4,1)} %bitcast.205), calls=%async_computation.5 | async-start | bytes 8388608
  315.5 9.3 %collective-permute-start.4 = (bf16[1,16,4,256]{3,2,1,0:T(4,128)(2,1)S(1)}, bf16[1,16,4,256]{3,2,1,0:T(4,128)(2,1)S(1)}, u32[]{:S(2)}, u32[]{:S(2)}) collective-permute-start(bf16[1,16,4,256]{3,2,1,0:T(4,128)(2,1)S(1)} %slice.180), channel_id=1, source_target_pairs={{0,4},{4,8},{8,12},{1,5},{5,9},{9,13},{2,6},{6,10},{10,14},{3,7},{... | collective-permute-start | bytes 98312 | tf_op jit(solution)/shard_map/ppermute | solution.py:18
  318.5 6.4 %collective-permute-start.5 = (bf16[1,16,4,256]{3,2,1,0:T(4,128)(2,1)S(1)}, bf16[1,16,4,256]{3,2,1,0:T(4,128)(2,1)S(1)}, u32[]{:S(2)}, u32[]{:S(2)}) collective-permute-start(bf16[1,16,4,256]{3,2,1,0:T(4,128)(2,1)S(1)} %slice.182), channel_id=1, source_target_pairs={{4,0},{8,4},{12,8},{5,1},{9,5},{13,9},{6,2},{10,6},{14,10},{7,3},{... | collective-permute-start | bytes 98312 | tf_op jit(solution)/shard_map/ppermute | solution.py:21
  320.4 60.9 %all-to-all-start.1 = ((bf16[16,432,256]{2,1,0:T(8,128)(2,1)}), bf16[16,432,256]{2,1,0:T(8,128)(2,1)}, u32[]{:S(2)}, u32[]{:S(2)}) async-start(bf16[16,432,256]{2,1,0:T(8,128)(2,1)} %bitcast.159), calls=%async_computation.1 | async-start | bytes 7077888 | tf_op jit(solution)/shard_map/all_to_all | solution.py:243
  327.6 41.5 %collective-permute-start.6 = (bf16[18,1,4,256]{3,2,1,0:T(4,128)(2,1)S(1)}, bf16[18,1,4,256]{3,2,1,0:T(4,128)(2,1)S(1)}, u32[]{:S(2)}, u32[]{:S(2)}) collective-permute-start(bf16[18,1,4,256]{3,2,1,0:T(4,128)(2,1)S(1)} %get-tuple-element.73), channel_id=1, source_target_pairs={{1,0},{2,1},{3,2},{5,4},{6,5},{7,6},{9,8},{10,9},{11,10},{13,12},{... | collective-permute-start | bytes 110600 | tf_op jit(solution)/shard_map/ppermute | solution.py:21
  328.9 40.2 %collective-permute-start.7 = (bf16[18,1,4,256]{3,2,1,0:T(4,128)(2,1)S(1)}, bf16[18,1,4,256]{3,2,1,0:T(4,128)(2,1)S(1)}, u32[]{:S(2)}, u32[]{:S(2)}) collective-permute-start(bf16[18,1,4,256]{3,2,1,0:T(4,128)(2,1)S(1)} %get-tuple-element.72), channel_id=1, source_target_pairs={{0,1},{1,2},{2,3},{4,5},{5,6},{6,7},{8,9},{9,10},{10,11},{12,13},{... | collective-permute-start | bytes 110600 | tf_op jit(solution)/shard_map/ppermute | solution.py:18
  (22 other events, 51.4 us)
Sparse Core Ops, SparseCore 0:
  62.2 55.5 all-gather.1
  251.4 73.6 reduce-scatter.4

commit v2 on v1

--- a/solution.py
+++ b/solution.py
@@ -198,7 +198,6 @@
         for shifted in d_shifts
     ]
     conv_part = jnp.stack(conv_blocks, axis=1).reshape(27 * channels, channels)
-    conv_part, d_hidden = lax.optimization_barrier((conv_part, d_hidden))
     d_padded = padded_2(
         d_hidden.reshape(extent_x, extent_y, extent_z, channels), (("gx", 0), ("gy", 1)), 1
     )

time: 405 us -> 383 us (0.946)
  waiting for transfers between devices: 99.9 us -> 67.2 us
  local copies, waits for them, and re-layouts: 137 us -> 150 us
    all_to_all x1, waiting for transfers between devices: 33.7 us -> 0.73 us  [local(): key_parts = lax.all_to_all(key_parts, ('gx', 'gy'), 0, 0, tiled=True)]
    ppermute x4, waiting for transfers between devices: 18.2 us -> 3.28 us  [padded_2(): lax.ppermute(lax.slice_in_dim(block, 0, width, axis=dim), axis, backward)]
    all_to_all x1, waiting for transfers between devices: 0.01 us -> 14 us  [local(): conv_rows = lax.all_to_all(conv_part, ('gx', 'gy'), 0, 0, tiled=True)]
    dot_general x1, matrix products: 16.3 us -> 3.11 us  [local(): jnp.einsum('ihe,jhe->hij', d_att_h, values_h, preferred_element_type=jnp....]
    unnamed x119 -> x111, local copies, waits for them, and re-layouts: 28.7 us -> 37.9 us
    dot_general x3, matrix products: 7.08 us -> 12.9 us  [local(): jnp.einsum('vr,vc->rc', columns, shifted.reshape(voxels, channels), prefe...]
    convert_element_type x5 -> x6, local copies, waits for them, and re-layouts: 13.2 us -> 16.5 us  [local(): d_act_grid = from_tokens(d_activation, extent_x, extent_y, extent_z).resh...]
    concatenate x4 -> x5, other arithmetic: 12.2 us -> 11.6 us  [padded_2(): block = jnp.concatenate([low, block, high], axis=dim)]
  transfers between devices with their start and end apart: 12 -> 12, of which waited for: 4 -> 5; matrix products, arithmetic and copies ran while one was open for 36% -> 44% of each run, Pallas kernels for 0% -> 0%
where the time goes in v2:
time: 383 us; the launch traced here: 376 us
  local copies, waits for them, and re-layouts  150 us (39%)
  matrix products  75.5 us (20%)
  waiting for transfers between devices  67.2 us (18%)
  starting transfers between devices  33.8 us (9%)
  other arithmetic  33.5 us (9%)
  between operations  15.2 us (4%)
    all_gather x1, waiting for transfers between devices, local(): lax.all_gather(qkv_rows[:, model_width:], ('gx', 'gy'), axis=0, tiled=True)  47.9 us
    unnamed x111, local copies, waits for them, and re-layouts  37.9 us
    reshape x9, local copies, waits for them, and re-layouts, plane_columns(): padded[start_x:start_x + extent_x, start_y:start_y + extent_y]  17.7 us
    convert_element_type x6, local copies, waits for them, and re-layouts, local(): d_act_grid = from_tokens(d_activation, extent_x, extent_y, extent_z).resh...  16.5 us
    ppermute x4, starting transfers between devices, padded_2(): lax.ppermute(lax.slice_in_dim(block, block.shape[dim] - width, None, axis...  14.5 us
    all_to_all x1, waiting for transfers between devices, local(): conv_rows = lax.all_to_all(conv_part, ('gx', 'gy'), 0, 0, tiled=True)  14 us
    dot_general x3, matrix products, local(): jnp.einsum('vr,vc->rc', columns, shifted.reshape(voxels, channels), prefe...  12.9 us
    dot_general x1, matrix products, local(): jnp.einsum('hij,jhe->ihe', d_scores, keys_h, precision=precise, preferred...  12.6 us
  transfers between devices with their start and end apart: 12, of which 5 were waited for; matrix products, arithmetic and copies ran while one was open for 44% of the time, Pallas kernels for 0%

profile of v2, /device:TPU:1, one launch (start us, length us, event | category | flops | bytes accessed | tf_op | source)
XLA Modules:
  0.0 375.6 jit_solution(8108205698264301399)
XLA Ops:
  8.2 4.7 %collective-permute-start = (bf16[1,16,4,256]{3,2,1,0:T(4,128)(2,1)S(1)}, bf16[1,16,4,256]{3,2,1,0:T(4,128)(2,1)S(1)}, u32[]{:S(2)}, u32[]{:S(2)}) collective-permute-start(bf16[1,16,4,256]{3,2,1,0:T(4,128)(2,1)S(1)} %get-tuple-element.86), channel_id=1, source_target_pairs={{0,4},{4,8},{8,12},{1,5},{5,9},{9,13},{2,6},{6,10},{10,14},{3,7},{... | collective-permute-start | bytes 98312 | tf_op jit(solution)/shard_map/ppermute | solution.py:18
  14.9 3.3 collective-permute-done.1
  33.3 6.0 %copy.202 = bf16[768,2304]{1,0:T(8,128)(2,1)} copy(bf16[768,2304]{0,1:T(8,128)(2,1)} %bitcast.161) | data formatting | bytes 7077888 | tf_op jit(solution)/shard_map/dot_general | solution.py:74
  39.5 3.7 pad_maximum_fusion.6
  46.5 3.8 %fusion.10 = f32[256,4,3,256]{3,0,2,1:T(8,128)S(1)} fusion(bf16[3,256,2304,1]{2,1,0,3:T(8,128)(2,1)S(1)} %bitcast.172, bf16[256,4,2304]{2,0,1:T(8,128)(2,1)S(1)} %constant_dynamic-update-slice_fusion.3), kind=kOutput, calls=%fused_computation.11 | convolution fusion | flops 3623878656 | bytes 11403264 | tf_op jit(solution)/shard_map/dot_general | solution.py:74
  70.2 47.9 %all-gather.2.cloned.1.call-done = bf16[2048,1024]{1,0:T(8,128)(2,1)} async-done(((bf16[128,1024]{1,0:T(8,128)(2,1)}), bf16[2048,1024]{1,0:T(8,128)(2,1)}) %all-gather.2.cloned.1.call-update) | async-done | bytes 4194320 | tf_op jit(solution)/shard_map/all_gather | solution.py:95
  118.1 4.5 %fusion.53 = (bf16[2048,512]{1,0:T(8,128)(2,1)}, bf16[2048,512]{1,0:T(8,128)(2,1)}) fusion(bf16[2048,1024]{1,0:T(8,128)(2,1)} %all-gather.2.cloned.1.call-done), kind=kLoop, calls=%fused_computation.130 | loop fusion | bytes 8388608 | tf_op jit(solution)/shard_map/slice | solution.py:99
  122.6 3.9 %copy.208 = bf16[2048,512]{0,1:T(8,128)(2,1)} copy(bf16[2048,512]{1,0:T(8,128)(2,1)} %get-tuple-element.50) | data formatting | bytes 4194304 | tf_op jit(solution)/shard_map/slice | solution.py:98
  126.6 4.0 %copy.211 = bf16[2048,512]{0,1:T(8,128)(2,1)} copy(bf16[2048,512]{1,0:T(8,128)(2,1)} %get-tuple-element.49) | data formatting | bytes 4194304 | tf_op jit(solution)/shard_map/slice | solution.py:99
  130.6 3.2 fusion.3
  140.1 5.9 %multiply_convert_fusion = bf16[8,64,2048]{2,1,0:T(8,128)(2,1)S(1)} fusion(bf16[128,8,64]{0,2,1:T(8,128)(2,1)S(1)} %bitcast.200, bf16[8,128,2048]{2,1,0:T(8,128)(2,1)S(1)} %get-tuple-element.92, f32[8,128]{1,0:T(8,128)S(1)} %get-tuple-element.91, f32[8,128,2048]{2,1,0:T(8,128)S(1)} %get-tuple-element.90, f32[8,128]{1,0:T(8,128)S(1)} %get-tuple-element.89), kind=kOutput, calls=%fused_computation.15 | convolution fusion | flops 1623195648 | bytes 14819328 | tf_op jit(solution)/shard_map/hij,ihe->jhe/dot_general | solution.py:131
  150.8 5.4 %all-to-all-start = ((bf16[16,128,1024]{1,2,0:T(8,128)(2,1)}), bf16[16,128,1024]{1,2,0:T(8,128)(2,1)}, u32[]{:S(2)}, u32[]{:S(2)}) async-start(bf16[16,128,1024]{1,2,0:T(8,128)(2,1)} %pad_maximum_fusion.1), calls=%async_computation | async-start | bytes 8388608 | tf_op jit(solution)/shard_map/all_to_all | solution.py:149
  189.8 5.1 %fusion.23 = bf16[8,64,128]{2,1,0:T(8,128)(2,1)S(1)} fusion(bf16[2048,8,64]{0,2,1:T(8,128)(2,1)S(1)} %bitcast.177, f32[8,128,2048]{2,1,0:T(8,128)} %copy-done.3, f32[8,128]{1,0:T(8,128)S(1)} %get-tuple-element.89), kind=kOutput, calls=%fused_computation.34 | convolution fusion | flops 274792448 | bytes 10620928 | tf_op jit(solution)/shard_map/hij,jhe->ihe/dot_general | solution.py:111
  198.2 12.6 %fusion.26 = bf16[8,64,128]{2,1,0:T(8,128)(2,1)} fusion(bf16[2048,8,64]{0,2,1:T(8,128)(2,1)} %bitcast.169, bf16[8,128,2048]{2,1,0:T(8,128)(2,1)} %copy-done.37, f32[8,128]{1,0:T(8,128)} %copy-done.38, f32[8,128,2048]{2,1,0:T(8,128)} %copy-done.3, f32[8,128]{1,0:T(8,128)S(1)} %get-tuple-element.89), kind=kOutput, calls=%fused_computation.36 | convolution fusion | flops 1621229568 | bytes 14819328 | tf_op jit(solution)/shard_map/hij,jhe->ihe/dot_general | solution.py:125
  211.5 3.5 reduce.2
  221.6 3.3 convolution_convert_fusion.4
  225.0 4.4 %reshape.249 = bf16[16,512,128]{2,1,0:T(8,128)(2,1)} reshape(bf16[2048,512]{1,0:T(8,128)(2,1)} %convolution_convert_fusion.4) | data formatting | bytes 4194304 | tf_op jit(solution)/shard_map/reshape | solution.py:227
  229.3 4.3 %reshape.250 = bf16[16,384,128]{2,1,0:T(8,128)(2,1)} reshape(bf16[512,1536]{1,0:T(8,128)(2,1)} %convolution_convert_fusion.5) | data formatting | bytes 3145728 | tf_op jit(solution)/shard_map/reshape | solution.py:227
  234.5 3.7 pad_maximum_fusion
  242.1 4.2 %fusion.16 = f32[128,2048]{1,0:T(8,128)} fusion(bf16[2048,512]{1,0:T(8,128)(2,1)S(1)} %copy-done, bf16[128,512]{1,0:T(8,128)(2,1)S(1)} %reshape.226, f32[128,512]{1,0:T(8,128)} %copy-done.25, f32[128,512]{1,0:T(8,128)S(1)} %get-tuple-element.88, f32[128]{0:T(128)S(1)} %copy-done.35, f32[128]{0:T(128)} %copy-done.36, f32[512]{0:T(512)S(1)} %copy-done.31, ...), kind=kOutput, calls=%fused_computation.27 | convolution fusion | flops 1611726848 | bytes 3805184 | tf_op jit(solution)/shard_map/dot_general | solution.py:174
  252.1 3.2 reshape.259
  266.0 5.0 %convolution_convert_fusion.1 = bf16[2304,256]{1,0:T(8,128)(2,1)} fusion(bf16[1024,2304]{1,0:T(8,128)(2,1)} %constant_dynamic-update-slice_fusion.21, bf16[1024,256]{1,0:T(8,128)(2,1)} %copy-done.27), kind=kOutput, calls=%fused_computation.19 | convolution fusion | flops 1208549376 | bytes 6422528 | tf_op jit(solution)/shard_map/vr,vc->rc/dot_general | solution.py:190
  279.3 4.0 %collective-permute-start.7 = (bf16[18,1,4,256]{3,1,0,2:T(2,128)(2,1)S(1)}, bf16[18,1,4,256]{3,1,0,2:T(2,128)(2,1)S(1)}, u32[]{:S(2)}, u32[]{:S(2)}) collective-permute-start(bf16[18,1,4,256]{3,1,0,2:T(2,128)(2,1)S(1)} %get-tuple-element.69), channel_id=1, source_target_pairs={{0,1},{1,2},{2,3},{4,5},{5,6},{6,7},{8,9},{9,10},{10,11},{12,13},{... | collective-permute-start | bytes 110600 | tf_op jit(solution)/shard_map/ppermute | solution.py:18
  295.3 3.9 %convolution_convert_fusion.2 = bf16[2304,256]{1,0:T(8,128)(2,1)S(1)} fusion(bf16[1024,2304]{1,0:T(8,128)(2,1)} %constant_dynamic-update-slice_fusion.21, bf16[1024,256]{1,0:T(8,128)(2,1)} %reshape.247), kind=kOutput, calls=%fused_computation.20 | convolution fusion | flops 1208549376 | bytes 6422528 | tf_op jit(solution)/shard_map/vr,vc->rc/dot_general | solution.py:190
  299.2 3.9 %convolution_convert_fusion = bf16[2304,256]{1,0:T(8,128)(2,1)S(1)} fusion(bf16[1024,2304]{1,0:T(8,128)(2,1)} %constant_dynamic-update-slice_fusion.21, bf16[1024,256]{1,0:T(8,128)(2,1)S(1)} %reshape.248), kind=kOutput, calls=%fused_computation.18 | convolution fusion | flops 1208549376 | bytes 6422528 | tf_op jit(solution)/shard_map/vr,vc->rc/dot_general | solution.py:190
  305.2 7.0 %all-to-all-start.1 = ((bf16[16,432,256]{2,1,0:T(8,128)(2,1)}), bf16[16,432,256]{2,1,0:T(8,128)(2,1)}, u32[]{:S(2)}, u32[]{:S(2)}) async-start(bf16[16,432,256]{2,1,0:T(8,128)(2,1)} %bitcast.160), calls=%async_computation.1 | async-start | bytes 7077888 | tf_op jit(solution)/shard_map/all_to_all | solution.py:242
  312.2 8.0 %copy.223 = bf16[9,3,256,256]{2,1,3,0:T(4,128)(2,1)} copy(bf16[9,3,256,256]{3,2,1,0:T(8,128)(2,1)} %bitcast.163) | data formatting | bytes 7077888 | tf_op jit(solution)/shard_map/reshape | solution.py:69
  320.3 5.1 %copy.246 = bf16[288,8,3,256]{3,1,2,0:T(8,128)(2,1)} copy(bf16[288,8,3,256]{3,2,1,0:T(4,128)(2,1)} %bitcast.158) | data formatting | bytes 7077888
  325.4 5.9 %copy.224 = bf16[768,2304]{1,0:T(8,128)(2,1)} copy(bf16[768,2304]{0,1:T(8,128)(2,1)} %bitcast.162) | data formatting | bytes 7077888 | tf_op jit(solution)/shard_map/dot_general | solution.py:207
  336.9 6.8 %fusion.8 = f32[256,4,3,256]{3,0,2,1:T(8,128)S(1)} fusion(bf16[3,256,2304,1]{2,1,0,3:T(8,128)(2,1)} %bitcast.173, bf16[256,4,2304]{2,0,1:T(8,128)(2,1)} %constant_dynamic-update-slice_fusion.12), kind=kOutput, calls=%fused_computation.9 | convolution fusion | flops 3623878656 | bytes 11403264 | tf_op jit(solution)/shard_map/dot_general | solution.py:207
  345.2 14.0 %all-to-all-done.1 = bf16[16,432,256]{2,1,0:T(8,128)(2,1)} async-done(((bf16[16,432,256]{2,1,0:T(8,128)(2,1)}), bf16[16,432,256]{2,1,0:T(8,128)(2,1)}, u32[]{:S(2)}, u32[]{:S(2)}) %all-to-all-start.1) | async-done | bytes 3538976 | tf_op jit(solution)/shard_map/all_to_all | solution.py:242
  359.2 3.3 reduce_sum.91
  (220 shorter events, 152.7 us)
Async XLA Ops:
  7.2 50.1 %copy-start = (bf16[2048,512]{1,0:T(8,128)(2,1)S(1)}, bf16[2048,512]{1,0:T(8,128)(2,1)}, u32[]{:S(2)}) copy-start(bf16[2048,512]{1,0:T(8,128)(2,1)} %param.9) | copy-start | bytes 6291460
  7.2 110.9 %all-gather.2.cloned.1.call-start = ((), (), s32[]{:S(2)}) async-start(), calls=%async_computation.3 | async-start | bytes 4456448 | tf_op jit(solution)/shard_map/all_gather | solution.py:95
  7.2 20.2 %copy-start.1 = (bf16[6912,256]{1,0:T(8,128)(2,1)S(1)}, bf16[6912,256]{1,0:T(8,128)(2,1)}, u32[]{:S(2)}) copy-start(bf16[6912,256]{1,0:T(8,128)(2,1)} %param.8) | copy-start | bytes 10616836
  8.2 6.7 %collective-permute-start = (bf16[1,16,4,256]{3,2,1,0:T(4,128)(2,1)S(1)}, bf16[1,16,4,256]{3,2,1,0:T(4,128)(2,1)S(1)}, u32[]{:S(2)}, u32[]{:S(2)}) collective-permute-start(bf16[1,16,4,256]{3,2,1,0:T(4,128)(2,1)S(1)} %get-tuple-element.86), channel_id=1, source_target_pairs={{0,4},{4,8},{8,12},{1,5},{5,9},{9,13},{2,6},{6,10},{10,14},{3,7},{... | collective-permute-start | bytes 98312 | tf_op jit(solution)/shard_map/ppermute | solution.py:18
  12.9 5.2 %collective-permute-start.1 = (bf16[1,16,4,256]{3,2,1,0:T(4,128)(2,1)S(1)}, bf16[1,16,4,256]{3,2,1,0:T(4,128)(2,1)S(1)}, u32[]{:S(2)}, u32[]{:S(2)}) collective-permute-start(bf16[1,16,4,256]{3,2,1,0:T(4,128)(2,1)S(1)} %get-tuple-element.85), channel_id=1, source_target_pairs={{4,0},{8,4},{12,8},{5,1},{9,5},{13,9},{6,2},{10,6},{14,10},{7,3},{... | collective-permute-start | bytes 98312 | tf_op jit(solution)/shard_map/ppermute | solution.py:21
  21.0 18.3 %copy-start.6 = (bf16[16,16,4,256]{3,2,1,0:T(4,128)(2,1)}, bf16[16,16,4,256]{3,2,1,0:T(4,128)(2,1)S(1)}, u32[]{:S(2)}) copy-start(bf16[16,16,4,256]{3,2,1,0:T(4,128)(2,1)S(1)} %get-tuple-element.84) | copy-start | bytes 1572868
  21.1 18.3 %copy-start.5 = (bf16[16,16,4,256]{3,2,1,0:T(4,128)(2,1)}, bf16[16,16,4,256]{3,2,1,0:T(4,128)(2,1)S(1)}, u32[]{:S(2)}) copy-start(bf16[16,16,4,256]{3,2,1,0:T(4,128)(2,1)S(1)} %get-tuple-element.82) | copy-start | bytes 1572868
  21.1 6.4 %copy-start.26 = (bf16[18,16,4,256]{3,2,1,0:T(4,128)(2,1)}, bf16[18,16,4,256]{3,2,1,0:T(4,128)(2,1)S(1)}, u32[]{:S(2)}) copy-start(bf16[18,16,4,256]{3,2,1,0:T(4,128)(2,1)S(1)} %constant_dynamic-update-slice_fusion) | copy-start | bytes 1769476
  21.1 18.3 %collective-permute-start.2 = (bf16[18,1,4,256]{3,2,1,0:T(4,128)(2,1)S(1)}, bf16[18,1,4,256]{3,2,1,0:T(4,128)(2,1)S(1)}, u32[]{:S(2)}, u32[]{:S(2)}) collective-permute-start(bf16[18,1,4,256]{3,2,1,0:T(4,128)(2,1)S(1)} %get-tuple-element.75), channel_id=1, source_target_pairs={{0,1},{1,2},{2,3},{4,5},{5,6},{6,7},{8,9},{9,10},{10,11},{12,13},{... | collective-permute-start | bytes 110600 | tf_op jit(solution)/shard_map/ppermute | solution.py:18
  24.3 15.2 %collective-permute-start.3 = (bf16[18,1,4,256]{3,2,1,0:T(4,128)(2,1)S(1)}, bf16[18,1,4,256]{3,2,1,0:T(4,128)(2,1)S(1)}, u32[]{:S(2)}, u32[]{:S(2)}) collective-permute-start(bf16[18,1,4,256]{3,2,1,0:T(4,128)(2,1)S(1)} %get-tuple-element.74), channel_id=1, source_target_pairs={{1,0},{2,1},{3,2},{5,4},{6,5},{7,6},{9,8},{10,9},{11,10},{13,12},{... | collective-permute-start | bytes 110600 | tf_op jit(solution)/shard_map/ppermute | solution.py:21
  50.7 8.3 %copy-start.31 = (f32[512]{0:T(512)S(1)}, f32[512]{0:T(512)}, u32[]{:S(2)}) copy-start(f32[512]{0:T(512)} %param.10) | copy-start | bytes 6148
  59.0 162.1 %copy-start.32 = (f32[128]{0:T(128)}, f32[128]{0:T(128)S(1)}, u32[]{:S(2)}) copy-start(f32[128]{0:T(128)S(1)} %add_rsqrt_fusion) | copy-start | bytes 1540
  133.8 6.3 %copy-start.3 = (f32[8,128,2048]{2,1,0:T(8,128)}, f32[8,128,2048]{2,1,0:T(8,128)S(1)}, u32[]{:S(2)}) copy-start(f32[8,128,2048]{2,1,0:T(8,128)S(1)} %get-tuple-element.90) | copy-start | bytes 25165828
  140.1 5.9 %copy-start.37 = (bf16[8,128,2048]{2,1,0:T(8,128)(2,1)}, bf16[8,128,2048]{2,1,0:T(8,128)(2,1)S(1)}, u32[]{:S(2)}) copy-start(bf16[8,128,2048]{2,1,0:T(8,128)(2,1)S(1)} %get-tuple-element.92) | copy-start | bytes 12582916
  140.1 5.9 %copy-start.38 = (f32[8,128]{1,0:T(8,128)}, f32[8,128]{1,0:T(8,128)S(1)}, u32[]{:S(2)}) copy-start(f32[8,128]{1,0:T(8,128)S(1)} %get-tuple-element.91) | copy-start | bytes 12292
  150.8 60.7 %all-to-all-start = ((bf16[16,128,1024]{1,2,0:T(8,128)(2,1)}), bf16[16,128,1024]{1,2,0:T(8,128)(2,1)}, u32[]{:S(2)}, u32[]{:S(2)}) async-start(bf16[16,128,1024]{1,2,0:T(8,128)(2,1)} %pad_maximum_fusion.1), calls=%async_computation | async-start | bytes 8388608 | tf_op jit(solution)/shard_map/all_to_all | solution.py:149
  156.2 206.3 %reduce-scatter.5.cloned.1.call-start = ((), (), s32[]{:S(2)}) async-start(), calls=%async_computation.4 | async-start | bytes 4491264
  178.2 9.8 %copy-start.21 = (bf16[1024,256]{1,0:T(8,128)(2,1)S(1)}, bf16[1024,256]{1,0:T(8,128)(2,1)}, u32[]{:S(2)}) copy-start(bf16[1024,256]{1,0:T(8,128)(2,1)} %reshape.243) | copy-start | bytes 1572868
  178.2 10.7 %copy-start.20 = (bf16[1024,256]{1,0:T(8,128)(2,1)S(1)}, bf16[1024,256]{1,0:T(8,128)(2,1)}, u32[]{:S(2)}) copy-start(bf16[1024,256]{1,0:T(8,128)(2,1)} %reshape.244) | copy-start | bytes 1572868
  178.2 11.6 %copy-start.18 = (bf16[2048,512]{0,1:T(8,128)(2,1)S(1)}, bf16[2048,512]{0,1:T(8,128)(2,1)}, u32[]{:S(2)}) copy-start(bf16[2048,512]{0,1:T(8,128)(2,1)} %copy.211) | copy-start | bytes 6291460
  215.0 6.6 %copy-start.4 = (bf16[128,2048]{1,0:T(8,128)(2,1)S(1)}, bf16[128,2048]{1,0:T(8,128)(2,1)}, u32[]{:S(2)}) copy-start(bf16[128,2048]{1,0:T(8,128)(2,1)} %reshape.230) | copy-start | bytes 1572868
  221.1 12.5 %copy-start.34 = (f32[128]{0:T(128)}, f32[128]{0:T(128)S(1)}, u32[]{:S(2)}) copy-start(f32[128]{0:T(128)S(1)} %get-tuple-element.94) | copy-start | bytes 1540
  261.0 15.8 %collective-permute-start.4 = (bf16[1,16,4,256]{3,2,1,0:T(4,128)(2,1)S(1)}, bf16[1,16,4,256]{3,2,1,0:T(4,128)(2,1)S(1)}, u32[]{:S(2)}, u32[]{:S(2)}) collective-permute-start(bf16[1,16,4,256]{3,2,1,0:T(4,128)(2,1)S(1)} %slice.178), channel_id=1, source_target_pairs={{0,4},{4,8},{8,12},{1,5},{5,9},{9,13},{2,6},{6,10},{10,14},{3,7},{... | collective-permute-start | bytes 98312 | tf_op jit(solution)/shard_map/ppermute | solution.py:18
  263.7 7.3 %copy-start.14 = (f32[16,16,4,256]{3,2,1,0:T(4,128)S(1)}, f32[16,16,4,256]{3,2,1,0:T(4,128)}, u32[]{:S(2)}) copy-start(f32[16,16,4,256]{3,2,1,0:T(4,128)} %reshape.259) | copy-start | bytes 3145732
  263.7 8.5 %copy-start.2 = (f32[8,8,2,2,2,2,256]{6,5,4,3,2,1,0:T(2,128)S(1)}, f32[8,8,2,2,2,2,256]{6,5,4,3,2,1,0:T(2,128)}, u32[]{:S(2)}) copy-start(f32[8,8,2,2,2,2,256]{6,5,4,3,2,1,0:T(2,128)} %reshape.262) | copy-start | bytes 3145732
  263.7 13.0 %collective-permute-start.5 = (bf16[1,16,4,256]{3,2,1,0:T(4,128)(2,1)S(1)}, bf16[1,16,4,256]{3,2,1,0:T(4,128)(2,1)S(1)}, u32[]{:S(2)}, u32[]{:S(2)}) collective-permute-start(bf16[1,16,4,256]{3,2,1,0:T(4,128)(2,1)S(1)} %slice.180), channel_id=1, source_target_pairs={{4,0},{8,4},{12,8},{5,1},{9,5},{13,9},{6,2},{10,6},{14,10},{7,3},{... | collective-permute-start | bytes 98312 | tf_op jit(solution)/shard_map/ppermute | solution.py:21
  278.0 7.4 %collective-permute-start.6 = (bf16[18,1,4,256]{3,1,0,2:T(2,128)(2,1)S(1)}, bf16[18,1,4,256]{3,1,0,2:T(2,128)(2,1)S(1)}, u32[]{:S(2)}, u32[]{:S(2)}) collective-permute-start(bf16[18,1,4,256]{3,1,0,2:T(2,128)(2,1)S(1)} %get-tuple-element.70), channel_id=1, source_target_pairs={{1,0},{2,1},{3,2},{5,4},{6,5},{7,6},{9,8},{10,9},{11,10},{13,12},{... | collective-permute-start | bytes 110600 | tf_op jit(solution)/shard_map/ppermute | solution.py:21
  279.3 7.4 %collective-permute-start.7 = (bf16[18,1,4,256]{3,1,0,2:T(2,128)(2,1)S(1)}, bf16[18,1,4,256]{3,1,0,2:T(2,128)(2,1)S(1)}, u32[]{:S(2)}, u32[]{:S(2)}) collective-permute-start(bf16[18,1,4,256]{3,1,0,2:T(2,128)(2,1)S(1)} %get-tuple-element.69), channel_id=1, source_target_pairs={{0,1},{1,2},{2,3},{4,5},{5,6},{6,7},{8,9},{9,10},{10,11},{12,13},{... | collective-permute-start | bytes 110600 | tf_op jit(solution)/shard_map/ppermute | solution.py:18
  299.2 3.9 %copy-start.24 = (bf16[2304,256]{1,0:T(8,128)(2,1)S(1)}, bf16[2304,256]{1,0:T(8,128)(2,1)}, u32[]{:S(2)}) copy-start(bf16[2304,256]{1,0:T(8,128)(2,1)} %convolution_convert_fusion.1) | copy-start | bytes 3538948
  305.2 54.0 %all-to-all-start.1 = ((bf16[16,432,256]{2,1,0:T(8,128)(2,1)}), bf16[16,432,256]{2,1,0:T(8,128)(2,1)}, u32[]{:S(2)}, u32[]{:S(2)}) async-start(bf16[16,432,256]{2,1,0:T(8,128)(2,1)} %bitcast.160), calls=%async_computation.1 | async-start | bytes 7077888 | tf_op jit(solution)/shard_map/all_to_all | solution.py:242
  325.4 7.8 %copy-start.22 = (bf16[16,16,4,256]{3,1,0,2:T(8,128)(2,1)S(1)}, bf16[16,16,4,256]{3,1,0,2:T(8,128)(2,1)}, u32[]{:S(2)}) copy-start(bf16[16,16,4,256]{3,1,0,2:T(8,128)(2,1)} %get-tuple-element.58) | copy-start | bytes 1572868
  325.4 8.7 %copy-start.16 = (bf16[16,16,4,256]{3,1,0,2:T(8,128)(2,1)S(1)}, bf16[16,16,4,256]{3,1,0,2:T(8,128)(2,1)}, u32[]{:S(2)}) copy-start(bf16[16,16,4,256]{3,1,0,2:T(8,128)(2,1)} %get-tuple-element.78) | copy-start | bytes 1572868
  (19 other events, 38.6 us)
Sparse Core Ops, SparseCore 0:
  62.5 55.5 all-gather.1
  238.3 75.7 reduce-scatter.4

commit v3 on v2

--- a/solution.py
+++ b/solution.py
@@ -174,11 +174,9 @@
     d_activation = jnp.dot(
         d_trunk, down_weight.T, precision=precise, preferred_element_type=jnp.float32
     ).astype(jnp.bfloat16)
-    d_act_grid = (
-        from_tokens(d_activation, extent_x, extent_y, extent_z)
-        .reshape(voxels, channels)
-        .astype(jnp.float32)
-    )
+    d_act_grid = lax.optimization_barrier(
+        from_tokens(d_activation, extent_x, extent_y, extent_z).reshape(voxels, channels)
+    ).astype(jnp.float32)
     d_hidden = (d_act_grid * gate_sig * (1.0 + hidden * (1.0 - gate_sig))).astype(jnp.bfloat16)
     d_depth = d_hidden.reshape(-1, extent_z, channels)
     d_shifts = [
@@ -217,18 +215,18 @@
     gain_high = gain_rows.astype(jnp.bfloat16)
     gain_low = (gain_rows - gain_high.astype(jnp.float32)).astype(jnp.bfloat16)
     gain_pair = jnp.concatenate([gain_high, gain_low], axis=1)
-    gain_pair = jnp.pad(gain_pair, ((0, 0), (0, 1024 - gain_pair.shape[1])))
+    gain_pair = jnp.pad(gain_pair, ((0, 0), (0, 4096 - gain_pair.shape[1])))
     pieces = [
         down_part.astype(jnp.bfloat16),
         qkv_part.astype(jnp.bfloat16),
         out_part.astype(jnp.bfloat16),
     ]
     shapes = [piece.shape for piece in pieces]
-    flat = [piece.reshape(groups, -1, 128) for piece in pieces] + [gain_pair.reshape(groups, -1, 128)]
+    flat = [piece.reshape(groups, -1, 512) for piece in pieces] + [gain_pair.reshape(groups, -1, 512)]
     heights = [piece.shape[1] for piece in flat]
     joined = jnp.concatenate(flat, axis=1)
     summed = lax.psum_scatter(
-        joined.reshape(-1, 128), ("gx", "gy"), scatter_dimension=0, tiled=True
+        joined.reshape(-1, 512), ("gx", "gy"), scatter_dimension=0, tiled=True
     )
     summed = lax.optimization_barrier(summed)
     results = []

time: 383 us -> 406 us (1.060)
  waiting for transfers between devices: 67.2 us -> 125 us
  local copies, waits for them, and re-layouts: 150 us -> 125 us
  matrix products: 75.5 us -> 67.8 us
    ppermute x4, waiting for transfers between devices: 3.28 us -> 40.1 us  [padded_2(): lax.ppermute(lax.slice_in_dim(block, 0, width, axis=dim), axis, backward)]
    all_to_all x1, waiting for transfers between devices: 0.73 us -> 37.2 us  [local(): key_parts = lax.all_to_all(key_parts, ('gx', 'gy'), 0, 0, tiled=True)]
    convert_element_type x6 -> x0, local copies, waits for them, and re-layouts: 16.5 us -> none  [local(): d_act_grid = from_tokens(d_activation, extent_x, extent_y, extent_z).resh...]
    all_to_all x1, waiting for transfers between devices: 14 us -> 0.01 us  [local(): conv_rows = lax.all_to_all(conv_part, ('gx', 'gy'), 0, 0, tiled=True)]
    unnamed x111 -> x118, local copies, waits for them, and re-layouts: 37.9 us -> 31 us
    reshape x3 -> x4, local copies, waits for them, and re-layouts: 10.8 us -> 5.64 us  [the longest x1 3.86 us: local(): piece.reshape(groups, -1, 512)]
    concatenate x5 -> x4, other arithmetic: 11.6 us -> 12.2 us  [padded_2(): block = jnp.concatenate([low, block, high], axis=dim)]
  transfers between devices with their start and end apart: 12 -> 12, of which waited for: 5 -> 4; matrix products, arithmetic and copies ran while one was open for 44% -> 34% of each run, Pallas kernels for 0% -> 0%
where the time goes in v3:
time: 406 us; the launch traced here: 398 us
  local copies, waits for them, and re-layouts  125 us (31%)
  waiting for transfers between devices  125 us (31%)
  matrix products  67.8 us (17%)
  other arithmetic  32.6 us (8%)
  starting transfers between devices  32 us (8%)
  between operations  15.3 us (4%)
    all_gather x1, waiting for transfers between devices, local(): lax.all_gather(qkv_rows[:, model_width:], ('gx', 'gy'), axis=0, tiled=True)  47.9 us
    ppermute x4, waiting for transfers between devices, padded_2(): lax.ppermute(lax.slice_in_dim(block, 0, width, axis=dim), axis, backward)  40.1 us
    all_to_all x1, waiting for transfers between devices, local(): key_parts = lax.all_to_all(key_parts, ('gx', 'gy'), 0, 0, tiled=True)  37.2 us
    unnamed x118, local copies, waits for them, and re-layouts  31 us
    reshape x9, local copies, waits for them, and re-layouts, plane_columns(): padded[start_x:start_x + extent_x, start_y:start_y + extent_y]  16.9 us
    ppermute x4, starting transfers between devices, padded_2(): lax.ppermute(lax.slice_in_dim(block, block.shape[dim] - width, None, axis...  15.1 us
    concatenate x4, other arithmetic, padded_2(): block = jnp.concatenate([low, block, high], axis=dim)  12.2 us
    dot_general x3, matrix products, local(): jnp.einsum('vr,vc->rc', columns, shifted.reshape(voxels, channels), prefe...  11.5 us
  transfers between devices with their start and end apart: 12, of which 4 were waited for; matrix products, arithmetic and copies ran while one was open for 34% of the time, Pallas kernels for 0%

profile of v3, /device:TPU:1, one launch (start us, length us, event | category | flops | bytes accessed | tf_op | source)
XLA Modules:
  0.0 398.0 jit_solution(1207178557978176199)
XLA Ops:
  8.2 4.7 %collective-permute-start = (bf16[1,16,4,256]{3,2,1,0:T(4,128)(2,1)S(1)}, bf16[1,16,4,256]{3,2,1,0:T(4,128)(2,1)S(1)}, u32[]{:S(2)}, u32[]{:S(2)}) collective-permute-start(bf16[1,16,4,256]{3,2,1,0:T(4,128)(2,1)S(1)} %get-tuple-element.86), channel_id=1, source_target_pairs={{0,4},{4,8},{8,12},{1,5},{5,9},{9,13},{2,6},{6,10},{10,14},{3,7},{... | collective-permute-start | bytes 98312 | tf_op jit(solution)/shard_map/ppermute | solution.py:18
  14.9 3.3 collective-permute-done.1
  20.8 3.1 collective-permute-start.2
  33.0 6.0 %copy.205 = bf16[768,2304]{1,0:T(8,128)(2,1)} copy(bf16[768,2304]{0,1:T(8,128)(2,1)} %bitcast.154) | data formatting | bytes 7077888 | tf_op jit(solution)/shard_map/dot_general | solution.py:74
  39.1 3.7 pad_maximum_fusion.7
  46.2 3.8 fusion.10
  69.9 47.9 %all-gather.2.cloned.1.call-done = bf16[2048,1024]{1,0:T(8,128)(2,1)} async-done(((bf16[128,1024]{1,0:T(8,128)(2,1)}), bf16[2048,1024]{1,0:T(8,128)(2,1)}) %all-gather.2.cloned.1.call-update) | async-done | bytes 4194320 | tf_op jit(solution)/shard_map/all_gather | solution.py:95
  117.8 4.5 %fusion.52 = (bf16[2048,512]{1,0:T(8,128)(2,1)}, bf16[2048,512]{1,0:T(8,128)(2,1)}) fusion(bf16[2048,1024]{1,0:T(8,128)(2,1)} %all-gather.2.cloned.1.call-done), kind=kLoop, calls=%fused_computation.131 | loop fusion | bytes 8388608 | tf_op jit(solution)/shard_map/slice | solution.py:99
  122.3 4.0 copy.211
  126.2 4.0 %copy.214 = bf16[2048,512]{0,1:T(8,128)(2,1)} copy(bf16[2048,512]{1,0:T(8,128)(2,1)} %get-tuple-element.47) | data formatting | bytes 4194304 | tf_op jit(solution)/shard_map/slice | solution.py:99
  130.2 3.2 fusion.3
  139.6 5.9 %multiply_convert_fusion = bf16[8,64,2048]{2,1,0:T(8,128)(2,1)S(1)} fusion(bf16[128,8,64]{0,2,1:T(8,128)(2,1)S(1)} %bitcast.193, bf16[8,128,2048]{2,1,0:T(8,128)(2,1)S(1)} %get-tuple-element.92, f32[8,128]{1,0:T(8,128)S(1)} %get-tuple-element.91, f32[8,128,2048]{2,1,0:T(8,128)S(1)} %get-tuple-element.90, f32[8,128]{1,0:T(8,128)S(1)} %get-tuple-element.89), kind=kOutput, calls=%fused_computation.15 | convolution fusion | flops 1623195648 | bytes 14819328 | tf_op jit(solution)/shard_map/hij,ihe->jhe/dot_general | solution.py:131
  150.2 5.4 %all-to-all-start = ((bf16[16,128,1024]{1,2,0:T(8,128)(2,1)}), bf16[16,128,1024]{1,2,0:T(8,128)(2,1)}, u32[]{:S(2)}, u32[]{:S(2)}) async-start(bf16[16,128,1024]{1,2,0:T(8,128)(2,1)} %pad_maximum_fusion.1), calls=%async_computation | async-start | bytes 8388608 | tf_op jit(solution)/shard_map/all_to_all | solution.py:149
  156.1 5.9 %fusion.22 = bf16[8,64,128]{2,1,0:T(8,128)(2,1)S(1)} fusion(bf16[2048,8,64]{0,2,1:T(8,128)(2,1)} %bitcast.166, f32[8,128,2048]{2,1,0:T(8,128)} %copy-done.3, f32[8,128]{1,0:T(8,128)S(1)} %get-tuple-element.89), kind=kOutput, calls=%fused_computation.33 | convolution fusion | flops 274792448 | bytes 10620928 | tf_op jit(solution)/shard_map/hij,jhe->ihe/dot_general | solution.py:111
  163.1 10.7 %fusion.25 = bf16[8,64,128]{2,1,0:T(8,128)(2,1)} fusion(bf16[2048,8,64]{0,2,1:T(8,128)(2,1)S(1)} %bitcast.159, bf16[8,128,2048]{2,1,0:T(8,128)(2,1)S(1)} %copy-done.39, f32[8,128]{1,0:T(8,128)S(1)} %copy-done.41, f32[8,128,2048]{2,1,0:T(8,128)} %copy-done.3, f32[8,128]{1,0:T(8,128)S(1)} %get-tuple-element.89), kind=kOutput, calls=%fused_computation.35 | convolution fusion | flops 1621229568 | bytes 14819328 | tf_op jit(solution)/shard_map/hij,jhe->ihe/dot_general | solution.py:125
  173.7 37.2 %all-to-all-done = bf16[16,128,1024]{1,2,0:T(8,128)(2,1)} async-done(((bf16[16,128,1024]{1,2,0:T(8,128)(2,1)}), bf16[16,128,1024]{1,2,0:T(8,128)(2,1)}, u32[]{:S(2)}, u32[]{:S(2)}) %all-to-all-start) | async-done | bytes 4194336 | tf_op jit(solution)/shard_map/all_to_all | solution.py:149
  210.9 3.5 reduce.2
  214.4 3.5 multiply_reduce_fusion
  220.8 3.9 reshape.231
  229.4 3.2 pad_maximum_fusion
  283.5 3.8 convolution_convert_fusion.1
  287.3 3.9 convolution_convert_fusion.2
  291.2 3.8 convolution_convert_fusion
  298.0 4.5 %all-to-all-start.1 = ((bf16[16,432,256]{2,1,0:T(8,128)(2,1)}), bf16[16,432,256]{2,1,0:T(8,128)(2,1)}, u32[]{:S(2)}, u32[]{:S(2)}) async-start(bf16[16,432,256]{2,1,0:T(8,128)(2,1)} %bitcast.153), calls=%async_computation.1 | async-start | bytes 7077888 | tf_op jit(solution)/shard_map/all_to_all | solution.py:240
  304.5 36.8 %collective-permute-done.5 = bf16[1,16,4,256]{3,2,1,0:T(4,128)(2,1)S(1)} collective-permute-done((bf16[1,16,4,256]{3,2,1,0:T(4,128)(2,1)S(1)}, bf16[1,16,4,256]{3,2,1,0:T(4,128)(2,1)S(1)}, u32[]{:S(2)}, u32[]{:S(2)}) %collective-permute-start.5) | collective-permute-done | bytes 32800 | tf_op jit(solution)/shard_map/ppermute | solution.py:21
  345.3 4.2 %collective-permute-start.7 = (bf16[18,1,4,256]{3,2,1,0:T(4,128)(2,1)S(1)}, bf16[18,1,4,256]{3,2,1,0:T(4,128)(2,1)S(1)}, u32[]{:S(2)}, u32[]{:S(2)}) collective-permute-start(bf16[18,1,4,256]{3,2,1,0:T(4,128)(2,1)S(1)} %get-tuple-element.68), channel_id=1, source_target_pairs={{0,1},{1,2},{2,3},{4,5},{5,6},{6,7},{8,9},{9,10},{10,11},{12,13},{... | collective-permute-start | bytes 110600 | tf_op jit(solution)/shard_map/ppermute | solution.py:18
  349.5 8.0 %copy.229 = bf16[9,3,256,256]{2,1,3,0:T(4,128)(2,1)} copy(bf16[9,3,256,256]{3,2,1,0:T(8,128)(2,1)} %bitcast.156) | data formatting | bytes 7077888 | tf_op jit(solution)/shard_map/reshape | solution.py:69
  357.5 5.1 %copy.247 = bf16[288,8,3,256]{3,1,2,0:T(8,128)(2,1)} copy(bf16[288,8,3,256]{3,2,1,0:T(4,128)(2,1)} %bitcast.151) | data formatting | bytes 7077888
  362.6 5.9 %copy.230 = bf16[768,2304]{1,0:T(8,128)(2,1)} copy(bf16[768,2304]{0,1:T(8,128)(2,1)} %bitcast.155) | data formatting | bytes 7077888 | tf_op jit(solution)/shard_map/dot_general | solution.py:205
  369.7 4.2 %pad_maximum_fusion.3 = (bf16[16,16,4,256]{3,2,1,0:T(4,128)(2,1)S(1)}, bf16[16,16,4,256]{3,2,1,0:T(4,128)(2,1)S(1)}, bf16[16,16,4,256]{3,2,1,0:T(4,128)(2,1)S(1)...) fusion(bf16[18,16,4,256]{3,2,1,0:T(4,128)(2,1)} %copy-done.27, ...), kind=kLoop, calls=%fused_computation.67 | loop fusion | flops 1572864 | bytes 3809280 | tf_op jit(solution)/shard_map/concatenate | solution.py:22
  376.4 3.8 fusion.8
  381.8 3.3 reduce_sum.91
  (225 shorter events, 128.0 us)
Async XLA Ops:
  7.2 49.7 %copy-start = (bf16[2048,512]{1,0:T(8,128)(2,1)S(1)}, bf16[2048,512]{1,0:T(8,128)(2,1)}, u32[]{:S(2)}) copy-start(bf16[2048,512]{1,0:T(8,128)(2,1)} %param.9) | copy-start | bytes 6291460
  7.2 110.6 %all-gather.2.cloned.1.call-start = ((), (), s32[]{:S(2)}) async-start(), calls=%async_computation.3 | async-start | bytes 4456448 | tf_op jit(solution)/shard_map/all_gather | solution.py:95
  7.2 19.9 %copy-start.1 = (bf16[6912,256]{1,0:T(8,128)(2,1)S(1)}, bf16[6912,256]{1,0:T(8,128)(2,1)}, u32[]{:S(2)}) copy-start(bf16[6912,256]{1,0:T(8,128)(2,1)} %param.8) | copy-start | bytes 10616836
  8.2 6.7 %collective-permute-start = (bf16[1,16,4,256]{3,2,1,0:T(4,128)(2,1)S(1)}, bf16[1,16,4,256]{3,2,1,0:T(4,128)(2,1)S(1)}, u32[]{:S(2)}, u32[]{:S(2)}) collective-permute-start(bf16[1,16,4,256]{3,2,1,0:T(4,128)(2,1)S(1)} %get-tuple-element.86), channel_id=1, source_target_pairs={{0,4},{4,8},{8,12},{1,5},{5,9},{9,13},{2,6},{6,10},{10,14},{3,7},{... | collective-permute-start | bytes 98312 | tf_op jit(solution)/shard_map/ppermute | solution.py:18
  12.9 5.2 %collective-permute-start.1 = (bf16[1,16,4,256]{3,2,1,0:T(4,128)(2,1)S(1)}, bf16[1,16,4,256]{3,2,1,0:T(4,128)(2,1)S(1)}, u32[]{:S(2)}, u32[]{:S(2)}) collective-permute-start(bf16[1,16,4,256]{3,2,1,0:T(4,128)(2,1)S(1)} %get-tuple-element.85), channel_id=1, source_target_pairs={{4,0},{8,4},{12,8},{5,1},{9,5},{13,9},{6,2},{10,6},{14,10},{7,3},{... | collective-permute-start | bytes 98312 | tf_op jit(solution)/shard_map/ppermute | solution.py:21
  20.7 18.3 %copy-start.6 = (bf16[16,16,4,256]{3,2,1,0:T(4,128)(2,1)}, bf16[16,16,4,256]{3,2,1,0:T(4,128)(2,1)S(1)}, u32[]{:S(2)}) copy-start(bf16[16,16,4,256]{3,2,1,0:T(4,128)(2,1)S(1)} %get-tuple-element.84) | copy-start | bytes 1572868
  20.7 18.3 %copy-start.5 = (bf16[16,16,4,256]{3,2,1,0:T(4,128)(2,1)}, bf16[16,16,4,256]{3,2,1,0:T(4,128)(2,1)S(1)}, u32[]{:S(2)}) copy-start(bf16[16,16,4,256]{3,2,1,0:T(4,128)(2,1)S(1)} %get-tuple-element.82) | copy-start | bytes 1572868
  20.7 9.4 %copy-start.28 = (bf16[18,16,4,256]{3,2,1,0:T(4,128)(2,1)}, bf16[18,16,4,256]{3,2,1,0:T(4,128)(2,1)S(1)}, u32[]{:S(2)}) copy-start(bf16[18,16,4,256]{3,2,1,0:T(4,128)(2,1)S(1)} %constant_dynamic-update-slice_fusion) | copy-start | bytes 1769476
  20.8 18.3 %collective-permute-start.2 = (bf16[18,1,4,256]{3,2,1,0:T(4,128)(2,1)S(1)}, bf16[18,1,4,256]{3,2,1,0:T(4,128)(2,1)S(1)}, u32[]{:S(2)}, u32[]{:S(2)}) collective-permute-start(bf16[18,1,4,256]{3,2,1,0:T(4,128)(2,1)S(1)} %get-tuple-element.74), channel_id=1, source_target_pairs={{0,1},{1,2},{2,3},{4,5},{5,6},{6,7},{8,9},{9,10},{10,11},{12,13},{... | collective-permute-start | bytes 110600 | tf_op jit(solution)/shard_map/ppermute | solution.py:18
  23.9 15.2 %collective-permute-start.3 = (bf16[18,1,4,256]{3,2,1,0:T(4,128)(2,1)S(1)}, bf16[18,1,4,256]{3,2,1,0:T(4,128)(2,1)S(1)}, u32[]{:S(2)}, u32[]{:S(2)}) collective-permute-start(bf16[18,1,4,256]{3,2,1,0:T(4,128)(2,1)S(1)} %get-tuple-element.73), channel_id=1, source_target_pairs={{1,0},{2,1},{3,2},{5,4},{6,5},{7,6},{9,8},{10,9},{11,10},{13,12},{... | collective-permute-start | bytes 110600 | tf_op jit(solution)/shard_map/ppermute | solution.py:21
  50.3 8.4 %copy-start.33 = (f32[512]{0:T(512)S(1)}, f32[512]{0:T(512)}, u32[]{:S(2)}) copy-start(f32[512]{0:T(512)} %param.10) | copy-start | bytes 6148
  58.7 159.3 %copy-start.34 = (f32[128]{0:T(128)}, f32[128]{0:T(128)S(1)}, u32[]{:S(2)}) copy-start(f32[128]{0:T(128)S(1)} %add_rsqrt_fusion) | copy-start | bytes 1540
  150.2 60.7 %all-to-all-start = ((bf16[16,128,1024]{1,2,0:T(8,128)(2,1)}), bf16[16,128,1024]{1,2,0:T(8,128)(2,1)}, u32[]{:S(2)}, u32[]{:S(2)}) async-start(bf16[16,128,1024]{1,2,0:T(8,128)(2,1)} %pad_maximum_fusion.1), calls=%async_computation | async-start | bytes 8388608 | tf_op jit(solution)/shard_map/all_to_all | solution.py:149
  155.6 229.4 %reduce-scatter.2.cloned.1.call-start = ((), (), s32[]{:S(2)}) async-start(), calls=%async_computation.4 | async-start | bytes 4595712 | tf_op jit(solution)/shard_map/reduce_scatter | solution.py:228
  156.1 7.0 %copy-start.2 = (bf16[2048,512]{0,1:T(8,128)(2,1)S(1)}, bf16[2048,512]{0,1:T(8,128)(2,1)}, u32[]{:S(2)}) copy-start(bf16[2048,512]{0,1:T(8,128)(2,1)} %copy.211) | copy-start | bytes 6291460
  156.1 7.0 %copy-start.39 = (bf16[8,128,2048]{2,1,0:T(8,128)(2,1)S(1)}, bf16[8,128,2048]{2,1,0:T(8,128)(2,1)}, u32[]{:S(2)}) copy-start(bf16[8,128,2048]{2,1,0:T(8,128)(2,1)} %copy-done.38) | copy-start | bytes 12582916
  240.2 10.1 %copy-start.8 = (bf16[16,16,4,256]{3,2,1,0:T(4,128)(2,1)S(1)}, bf16[16,16,4,256]{3,2,1,0:T(4,128)(2,1)}, u32[]{:S(2)}) copy-start(bf16[16,16,4,256]{3,2,1,0:T(4,128)(2,1)} %copy-done.7) | copy-start | bytes 1572868
  246.3 15.4 %copy-start.19 = (bf16[1024,256]{1,0:T(8,128)(2,1)S(1)}, bf16[1024,256]{1,0:T(8,128)(2,1)}, u32[]{:S(2)}) copy-start(bf16[1024,256]{1,0:T(8,128)(2,1)} %reshape.223) | copy-start | bytes 1572868
  251.2 13.1 %copy-start.18 = (bf16[1024,256]{1,0:T(8,128)(2,1)S(1)}, bf16[1024,256]{1,0:T(8,128)(2,1)}, u32[]{:S(2)}) copy-start(bf16[1024,256]{1,0:T(8,128)(2,1)} %reshape.226) | copy-start | bytes 1572868
  253.9 8.7 %copy-start.22 = (bf16[1024,256]{1,0:T(8,128)(2,1)S(1)}, bf16[1024,256]{1,0:T(8,128)(2,1)}, u32[]{:S(2)}) copy-start(bf16[1024,256]{1,0:T(8,128)(2,1)} %reshape.224) | copy-start | bytes 1572868
  253.9 9.6 %copy-start.21 = (bf16[1024,256]{1,0:T(8,128)(2,1)S(1)}, bf16[1024,256]{1,0:T(8,128)(2,1)}, u32[]{:S(2)}) copy-start(bf16[1024,256]{1,0:T(8,128)(2,1)} %reshape.225) | copy-start | bytes 1572868
  253.9 11.3 %copy-start.20 = (bf16[1024,256]{1,0:T(8,128)(2,1)S(1)}, bf16[1024,256]{1,0:T(8,128)(2,1)}, u32[]{:S(2)}) copy-start(bf16[1024,256]{1,0:T(8,128)(2,1)} %reshape.227) | copy-start | bytes 1572868
  253.9 12.2 %copy-start.26 = (f32[128,512]{1,0:T(8,128)S(1)}, f32[128,512]{1,0:T(8,128)}, u32[]{:S(2)}) copy-start(f32[128,512]{1,0:T(8,128)} %get-tuple-element.93) | copy-start | bytes 786436
  253.9 12.2 %copy-start.35 = (f32[128]{0:T(128)S(1)}, f32[128]{0:T(128)}, u32[]{:S(2)}) copy-start(f32[128]{0:T(128)} %copy-done.34) | copy-start | bytes 1540
  253.9 12.2 %copy-start.37 = (f32[128]{0:T(128)S(1)}, f32[128]{0:T(128)}, u32[]{:S(2)}) copy-start(f32[128]{0:T(128)} %copy-done.36) | copy-start | bytes 1540
  280.4 24.1 %collective-permute-start.4 = (bf16[1,16,4,256]{3,2,1,0:T(4,128)(2,1)S(1)}, bf16[1,16,4,256]{3,2,1,0:T(4,128)(2,1)S(1)}, u32[]{:S(2)}, u32[]{:S(2)}) collective-permute-start(bf16[1,16,4,256]{3,2,1,0:T(4,128)(2,1)S(1)} %slice.178), channel_id=1, source_target_pairs={{0,4},{4,8},{8,12},{1,5},{5,9},{9,13},{2,6},{6,10},{10,14},{3,7},{... | collective-permute-start | bytes 98312 | tf_op jit(solution)/shard_map/ppermute | solution.py:18
  298.0 43.3 %copy-start.23 = (bf16[16,16,4,256]{3,2,1,0:T(4,128)(2,1)S(1)}, bf16[16,16,4,256]{3,2,1,0:T(4,128)(2,1)}, u32[]{:S(2)}) copy-start(bf16[16,16,4,256]{3,2,1,0:T(4,128)(2,1)} %reshape.217) | copy-start | bytes 1572868
  298.0 83.8 %all-to-all-start.1 = ((bf16[16,432,256]{2,1,0:T(8,128)(2,1)}), bf16[16,432,256]{2,1,0:T(8,128)(2,1)}, u32[]{:S(2)}, u32[]{:S(2)}) async-start(bf16[16,432,256]{2,1,0:T(8,128)(2,1)} %bitcast.153), calls=%async_computation.1 | async-start | bytes 7077888 | tf_op jit(solution)/shard_map/all_to_all | solution.py:240
  302.5 38.8 %collective-permute-start.5 = (bf16[1,16,4,256]{3,2,1,0:T(4,128)(2,1)S(1)}, bf16[1,16,4,256]{3,2,1,0:T(4,128)(2,1)S(1)}, u32[]{:S(2)}, u32[]{:S(2)}) collective-permute-start(bf16[1,16,4,256]{3,2,1,0:T(4,128)(2,1)S(1)} %slice.180), channel_id=1, source_target_pairs={{4,0},{8,4},{12,8},{5,1},{9,5},{13,9},{6,2},{10,6},{14,10},{7,3},{... | collective-permute-start | bytes 98312 | tf_op jit(solution)/shard_map/ppermute | solution.py:21
  344.0 25.8 %collective-permute-start.6 = (bf16[18,1,4,256]{3,2,1,0:T(4,128)(2,1)S(1)}, bf16[18,1,4,256]{3,2,1,0:T(4,128)(2,1)S(1)}, u32[]{:S(2)}, u32[]{:S(2)}) collective-permute-start(bf16[18,1,4,256]{3,2,1,0:T(4,128)(2,1)S(1)} %get-tuple-element.69), channel_id=1, source_target_pairs={{1,0},{2,1},{3,2},{5,4},{6,5},{7,6},{9,8},{10,9},{11,10},{13,12},{... | collective-permute-start | bytes 110600 | tf_op jit(solution)/shard_map/ppermute | solution.py:21
  345.3 24.5 %collective-permute-start.7 = (bf16[18,1,4,256]{3,2,1,0:T(4,128)(2,1)S(1)}, bf16[18,1,4,256]{3,2,1,0:T(4,128)(2,1)S(1)}, u32[]{:S(2)}, u32[]{:S(2)}) collective-permute-start(bf16[18,1,4,256]{3,2,1,0:T(4,128)(2,1)S(1)} %get-tuple-element.68), channel_id=1, source_target_pairs={{0,1},{1,2},{2,3},{4,5},{5,6},{6,7},{8,9},{9,10},{10,11},{12,13},{... | collective-permute-start | bytes 110600 | tf_op jit(solution)/shard_map/ppermute | solution.py:18
  362.6 7.0 %copy-start.24 = (bf16[16,16,4,256]{3,2,1,0:T(4,128)(2,1)S(1)}, bf16[16,16,4,256]{3,2,1,0:T(4,128)(2,1)}, u32[]{:S(2)}) copy-start(bf16[16,16,4,256]{3,2,1,0:T(4,128)(2,1)} %get-tuple-element.77) | copy-start | bytes 1572868
  (22 other events, 70.8 us)
Sparse Core Ops, SparseCore 0:
  62.1 55.5 all-gather.1
  232.8 72.0 reduce-scatter.1

commit v4 on v2

--- a/solution.py
+++ b/solution.py
@@ -10,8 +10,8 @@
 precise = lax.Precision.HIGHEST
 
 
-def padded_2(block, sides, width):
-    for axis, dim in sides:
+def padded_2(block, sides):
+    for axis, dim, width in sides:
         count = lax.axis_size(axis)
         forward = [(i, i + 1) for i in range(count - 1)]
         backward = [(target, source) for source, target in forward]
@@ -37,18 +37,19 @@
     return grid.reshape(extent_x, extent_y, extent_z, channels)
 
 
-def plane_columns(padded, extent_x, extent_y, flipped):
-    channels = padded.shape[3]
-    rows = extent_x * extent_y * padded.shape[2]
+def plane_columns(padded, extent_x, extent_y, extent_z, flipped):
+    channels = padded.shape[2]
+    rows = extent_x * extent_y * extent_z
     pieces = []
     for offset_x in range(3):
         for offset_y in range(3):
             start_x = 2 - offset_x if flipped else offset_x
             start_y = 2 - offset_y if flipped else offset_y
             pieces.append(
-                padded[start_x : start_x + extent_x, start_y : start_y + extent_y].reshape(
-                    rows, channels
-                )
+                padded[
+                    start_x : start_x + extent_x,
+                    start_y * extent_z : (start_y + extent_y) * extent_z,
+                ].reshape(rows, channels)
             )
     return jnp.concatenate(pieces, axis=1)
 
@@ -67,8 +68,9 @@
     voxels = extent_x * extent_y * extent_z
     score_scale = HD ** (-0.5)
     taps = conv_weight.reshape(9, 3, channels, channels)
-    padded = padded_2(features, (("gx", 0), ("gy", 1)), 1)
-    columns = plane_columns(padded, extent_x, extent_y, False)
+    flat_features = features.reshape(extent_x, extent_y * extent_z, channels)
+    padded = padded_2(flat_features, (("gx", 0, 1), ("gy", 1, extent_z)))
+    columns = plane_columns(padded, extent_x, extent_y, extent_z, False)
     weight_fwd = taps.transpose(0, 2, 1, 3).reshape(9 * channels, 3 * channels)
     hidden = depth_sum(
         jnp.dot(columns, weight_fwd, preferred_element_type=jnp.float32),
@@ -199,9 +201,10 @@
     ]
     conv_part = jnp.stack(conv_blocks, axis=1).reshape(27 * channels, channels)
     d_padded = padded_2(
-        d_hidden.reshape(extent_x, extent_y, extent_z, channels), (("gx", 0), ("gy", 1)), 1
-    )
-    d_columns = plane_columns(d_padded, extent_x, extent_y, True)
+        d_hidden.reshape(extent_x, extent_y * extent_z, channels),
+        (("gx", 0, 1), ("gy", 1, extent_z)),
+    )
+    d_columns = plane_columns(d_padded, extent_x, extent_y, extent_z, True)
     weight_bwd = taps.transpose(0, 3, 1, 2).reshape(9 * channels, 3 * channels)
     grad_features = depth_sum(
         jnp.dot(d_columns, weight_bwd, preferred_element_type=jnp.float32),

time: 383 us -> 417 us (1.089)
  local copies, waits for them, and re-layouts: 150 us -> 183 us
    concatenate x3 -> x19, local copies, waits for them, and re-layouts: 3.85 us -> 27.8 us  [plane_columns(): return jnp.concatenate(pieces, axis=1)]
    unnamed x111 -> x105, local copies, waits for them, and re-layouts: 37.9 us -> 54.8 us
    reshape x9 -> x1, local copies, waits for them, and re-layouts: 17.7 us -> 1.96 us  [local(): flat_features = features.reshape(extent_x, extent_y * extent_z, channels)]
    all_to_all x1, waiting for transfers between devices: 0.73 us -> 14 us  [local(): key_parts = lax.all_to_all(key_parts, ('gx', 'gy'), 0, 0, tiled=True)]
    all_to_all x1, waiting for transfers between devices: 14 us -> 8.25 us  [local(): conv_rows = lax.all_to_all(conv_part, ('gx', 'gy'), 0, 0, tiled=True)]
  transfers between devices with their start and end apart: 12 -> 12, of which waited for: 5 -> 4; matrix products, arithmetic and copies ran while one was open for 44% -> 43% of each run, Pallas kernels for 0% -> 0%
where the time goes in v4:
time: 417 us; the launch traced here: 409 us
  local copies, waits for them, and re-layouts  183 us (44%)
  matrix products  77.2 us (19%)
  waiting for transfers between devices  67.6 us (16%)
  other arithmetic  34.4 us (8%)
  starting transfers between devices  31.6 us (8%)
  between operations  15 us (4%)
    unnamed x105, local copies, waits for them, and re-layouts  54.8 us
    all_gather x1, waiting for transfers between devices, local(): lax.all_gather(qkv_rows[:, model_width:], ('gx', 'gy'), axis=0, tiled=True)  43.9 us
    concatenate x19, local copies, waits for them, and re-layouts, plane_columns(): return jnp.concatenate(pieces, axis=1)  27.8 us
    convert_element_type x6, local copies, waits for them, and re-layouts, local(): d_act_grid = from_tokens(d_activation, extent_x, extent_y, extent_z).resh...  16.2 us
    ppermute x4, starting transfers between devices, padded_2(): lax.ppermute(lax.slice_in_dim(block, block.shape[dim] - width, None, axis...  14.8 us
    all_to_all x1, waiting for transfers between devices, local(): key_parts = lax.all_to_all(key_parts, ('gx', 'gy'), 0, 0, tiled=True)  14 us
    reshape x2, local copies, waits for them, and re-layouts, local(): taps = conv_weight.reshape(9, 3, channels, channels)  13 us
    dot_general x3, matrix products, local(): jnp.einsum('vr,vc->rc', columns, shifted.reshape(voxels, channels), prefe...  12.7 us
  transfers between devices with their start and end apart: 12, of which 4 were waited for; matrix products, arithmetic and copies ran while one was open for 43% of the time, Pallas kernels for 0%

profile of v4, /device:TPU:1, one launch (start us, length us, event | category | flops | bytes accessed | tf_op | source)
XLA Modules:
  0.0 408.6 jit_solution(13777915238675746372)
XLA Ops:
  8.2 4.6 %collective-permute-start = (bf16[1,64,256]{2,1,0:T(8,128)(2,1)S(1)}, bf16[1,64,256]{2,1,0:T(8,128)(2,1)S(1)}, u32[]{:S(2)}, u32[]{:S(2)}) collective-permute-start(bf16[1,64,256]{2,1,0:T(8,128)(2,1)S(1)} %slice.163), channel_id=1, source_target_pairs={{0,4},{4,8},{8,12},{1,5},{5,9},{9,13},{2,6},{6,10},{10,14},{3,7},{... | collective-permute-start | bytes 98312 | tf_op jit(solution)/shard_map/ppermute | solution.py:18
  26.1 5.0 %copy.209 = bf16[9,3,256,256]{3,1,2,0:T(4,128)(2,1)S(1)} copy(bf16[9,3,256,256]{3,2,1,0:T(8,128)(2,1)} %bitcast.157) | data formatting | bytes 7077888 | tf_op jit(solution)/shard_map/reshape | solution.py:70
  34.0 6.0 %copy.210 = bf16[768,2304]{1,0:T(8,128)(2,1)} copy(bf16[768,2304]{0,1:T(8,128)(2,1)} %bitcast.155) | data formatting | bytes 7077888 | tf_op jit(solution)/shard_map/dot_general | solution.py:76
  41.8 5.2 %pad_maximum_fusion.6 = (bf16[16,64,256]{2,1,0:T(8,128)(2,1)S(1)}, bf16[16,64,256]{2,1,0:T(8,128)(2,1)}, bf16[16,64,256]{2,1,0:T(8,128)(2,1)}, bf16[16,64,256]{2...) fusion(bf16[18,4,256]{2,1,0:T(4,128)(2,1)S(1)} %collective-permute-done.3, ...), kind=kLoop, calls=%fused_computation.71 | loop fusion | flops 6291456 | bytes 3809280 | tf_op jit(solution)/shard_map/concatenate | solution.py:22
  71.6 5.7 %fusion.10 = f32[256,4,3,256]{3,0,2,1:T(8,128)S(1)} fusion(bf16[3,256,2304,1]{2,1,0,3:T(8,128)(2,1)S(1)} %bitcast.174, bf16[256,4,2304]{2,0,1:T(8,128)(2,1)} %copy_dynamic-update-slice_fusion.8), kind=kOutput, calls=%fused_computation.11 | convolution fusion | flops 3623878656 | bytes 11403264 | tf_op jit(solution)/shard_map/dot_general | solution.py:76
  101.2 43.9 %all-gather.2.cloned.1.call-done = bf16[2048,1024]{1,0:T(8,128)(2,1)} async-done(((bf16[128,1024]{1,0:T(8,128)(2,1)}), bf16[2048,1024]{1,0:T(8,128)(2,1)}) %all-gather.2.cloned.1.call-update) | async-done | bytes 4194320 | tf_op jit(solution)/shard_map/all_gather | solution.py:97
  145.1 4.5 %fusion.51 = (bf16[2048,512]{1,0:T(8,128)(2,1)}, bf16[2048,512]{1,0:T(8,128)(2,1)}) fusion(bf16[2048,1024]{1,0:T(8,128)(2,1)} %all-gather.2.cloned.1.call-done), kind=kLoop, calls=%fused_computation.134 | loop fusion | bytes 8388608 | tf_op jit(solution)/shard_map/slice | solution.py:101
  149.6 3.9 copy.216
  153.6 3.9 copy.219
  157.5 3.2 fusion.3
  167.1 5.9 %multiply_convert_fusion = bf16[8,64,2048]{2,1,0:T(8,128)(2,1)S(1)} fusion(bf16[128,8,64]{0,2,1:T(8,128)(2,1)S(1)} %bitcast.186, bf16[8,128,2048]{2,1,0:T(8,128)(2,1)S(1)} %get-tuple-element.92, f32[8,128]{1,0:T(8,128)S(1)} %get-tuple-element.91, f32[8,128,2048]{2,1,0:T(8,128)S(1)} %get-tuple-element.90, f32[8,128]{1,0:T(8,128)S(1)} %get-tuple-element.89), kind=kOutput, calls=%fused_computation.15 | convolution fusion | flops 1623195648 | bytes 14819328 | tf_op jit(solution)/shard_map/hij,ihe->jhe/dot_general | solution.py:133
  177.7 5.4 %all-to-all-start = ((bf16[16,128,1024]{1,2,0:T(8,128)(2,1)}), bf16[16,128,1024]{1,2,0:T(8,128)(2,1)}, u32[]{:S(2)}, u32[]{:S(2)}) async-start(bf16[16,128,1024]{1,2,0:T(8,128)(2,1)} %pad_maximum_fusion.1), calls=%async_computation | async-start | bytes 8388608 | tf_op jit(solution)/shard_map/all_to_all | solution.py:151
  203.5 5.1 %fusion.23 = bf16[8,64,128]{2,1,0:T(8,128)(2,1)S(1)} fusion(bf16[2048,8,64]{0,2,1:T(8,128)(2,1)S(1)} %bitcast.177, f32[8,128,2048]{2,1,0:T(8,128)} %copy-done.2, f32[8,128]{1,0:T(8,128)S(1)} %get-tuple-element.89), kind=kOutput, calls=%fused_computation.34 | convolution fusion | flops 274792448 | bytes 10620928 | tf_op jit(solution)/shard_map/hij,jhe->ihe/dot_general | solution.py:113
  211.9 12.6 %fusion.26 = bf16[8,64,128]{2,1,0:T(8,128)(2,1)} fusion(bf16[2048,8,64]{0,2,1:T(8,128)(2,1)} %bitcast.163, bf16[8,128,2048]{2,1,0:T(8,128)(2,1)} %copy-done.34, f32[8,128]{1,0:T(8,128)} %copy-done.35, f32[8,128,2048]{2,1,0:T(8,128)} %copy-done.2, f32[8,128]{1,0:T(8,128)S(1)} %get-tuple-element.89), kind=kOutput, calls=%fused_computation.36 | convolution fusion | flops 1621229568 | bytes 14819328 | tf_op jit(solution)/shard_map/hij,jhe->ihe/dot_general | solution.py:127
  224.5 14.0 %all-to-all-done = bf16[16,128,1024]{1,2,0:T(8,128)(2,1)} async-done(((bf16[16,128,1024]{1,2,0:T(8,128)(2,1)}), bf16[16,128,1024]{1,2,0:T(8,128)(2,1)}, u32[]{:S(2)}, u32[]{:S(2)}) %all-to-all-start) | async-done | bytes 4194336 | tf_op jit(solution)/shard_map/all_to_all | solution.py:151
  238.5 3.5 reduce.2
  248.4 3.5 convolution_convert_fusion.4
  251.9 4.3 %reshape.251 = bf16[16,512,128]{2,1,0:T(8,128)(2,1)} reshape(bf16[2048,512]{1,0:T(8,128)(2,1)} %convolution_convert_fusion.4) | data formatting | bytes 4194304 | tf_op jit(solution)/shard_map/reshape | solution.py:230
  256.3 4.3 %reshape.252 = bf16[16,384,128]{2,1,0:T(8,128)(2,1)} reshape(bf16[512,1536]{1,0:T(8,128)(2,1)} %convolution_convert_fusion.5) | data formatting | bytes 3145728 | tf_op jit(solution)/shard_map/reshape | solution.py:230
  261.4 3.7 pad_maximum_fusion
  265.1 4.2 %fusion.16 = f32[128,2048]{1,0:T(8,128)} fusion(bf16[2048,512]{1,0:T(8,128)(2,1)S(1)} %copy-done, bf16[128,512]{1,0:T(8,128)(2,1)S(1)} %reshape.228, f32[128,512]{1,0:T(8,128)} %copy-done.22, f32[128,512]{1,0:T(8,128)S(1)} %get-tuple-element.88, f32[128]{0:T(128)S(1)} %copy-done.32, f32[128]{0:T(128)} %copy-done.33, f32[512]{0:T(512)S(1)} %copy-done.28, ...), kind=kOutput, calls=%fused_computation.27 | convolution fusion | flops 1611726848 | bytes 3805184 | tf_op jit(solution)/shard_map/dot_general | solution.py:176
  288.1 4.9 %convolution_convert_fusion.1 = bf16[2304,256]{1,0:T(8,128)(2,1)} fusion(bf16[1024,2304]{1,0:T(8,128)(2,1)} %constant_dynamic-update-slice_fusion.5, bf16[1024,256]{1,0:T(8,128)(2,1)S(1)} %multiply_convert_fusion.3), kind=kOutput, calls=%fused_computation.19 | convolution fusion | flops 1208549376 | bytes 6422528 | tf_op jit(solution)/shard_map/vr,vc->rc/dot_general | solution.py:192
  300.9 4.2 %collective-permute-start.7 = (bf16[18,4,256]{2,1,0:T(4,128)(2,1)S(1)}, bf16[18,4,256]{2,1,0:T(4,128)(2,1)S(1)}, u32[]{:S(2)}, u32[]{:S(2)}) collective-permute-start(bf16[18,4,256]{2,1,0:T(4,128)(2,1)S(1)} %get-tuple-element.69), channel_id=1, source_target_pairs={{0,1},{1,2},{2,3},{4,5},{5,6},{6,7},{8,9},{9,10},{10,11},{12,13},{... | collective-permute-start | bytes 110600 | tf_op jit(solution)/shard_map/ppermute | solution.py:18
  331.1 3.9 convolution_convert_fusion.2
  335.0 3.9 convolution_convert_fusion
  341.0 4.7 %all-to-all-start.1 = ((bf16[16,432,256]{2,1,0:T(8,128)(2,1)}), bf16[16,432,256]{2,1,0:T(8,128)(2,1)}, u32[]{:S(2)}, u32[]{:S(2)}) async-start(bf16[16,432,256]{2,1,0:T(8,128)(2,1)} %bitcast.154), calls=%async_computation.1 | async-start | bytes 7077888 | tf_op jit(solution)/shard_map/all_to_all | solution.py:245
  345.7 8.0 %copy.235 = bf16[9,3,256,256]{2,1,3,0:T(4,128)(2,1)} copy(bf16[9,3,256,256]{3,2,1,0:T(8,128)(2,1)} %bitcast.158) | data formatting | bytes 7077888 | tf_op jit(solution)/shard_map/reshape | solution.py:70
  353.7 5.1 %copy.258 = bf16[288,8,3,256]{3,1,2,0:T(8,128)(2,1)} copy(bf16[288,8,3,256]{3,2,1,0:T(4,128)(2,1)} %bitcast.152) | data formatting | bytes 7077888
  358.8 5.9 %copy.236 = bf16[768,2304]{1,0:T(8,128)(2,1)} copy(bf16[768,2304]{0,1:T(8,128)(2,1)} %bitcast.156) | data formatting | bytes 7077888 | tf_op jit(solution)/shard_map/dot_general | solution.py:210
  375.7 6.8 %fusion.8 = f32[256,4,3,256]{3,0,2,1:T(8,128)S(1)} fusion(bf16[3,256,2304,1]{2,1,0,3:T(8,128)(2,1)} %bitcast.175, bf16[256,4,2304]{2,0,1:T(8,128)(2,1)} %copy_dynamic-update-slice_fusion), kind=kOutput, calls=%fused_computation.9 | convolution fusion | flops 3623878656 | bytes 11403264 | tf_op jit(solution)/shard_map/dot_general | solution.py:210
  384.0 8.3 %all-to-all-done.1 = bf16[16,432,256]{2,1,0:T(8,128)(2,1)} async-done(((bf16[16,432,256]{2,1,0:T(8,128)(2,1)}), bf16[16,432,256]{2,1,0:T(8,128)(2,1)}, u32[]{:S(2)}, u32[]{:S(2)}) %all-to-all-start.1) | async-done | bytes 3538976 | tf_op jit(solution)/shard_map/all_to_all | solution.py:245
  392.2 3.3 reduce_sum.91
  (214 shorter events, 182.1 us)
Async XLA Ops:
  7.2 77.1 %copy-start = (bf16[2048,512]{1,0:T(8,128)(2,1)S(1)}, bf16[2048,512]{1,0:T(8,128)(2,1)}, u32[]{:S(2)}) copy-start(bf16[2048,512]{1,0:T(8,128)(2,1)} %param.9) | copy-start | bytes 6291460
  7.2 137.9 %all-gather.2.cloned.1.call-start = ((), (), s32[]{:S(2)}) async-start(), calls=%async_computation.3 | async-start | bytes 4456448 | tf_op jit(solution)/shard_map/all_gather | solution.py:97
  8.2 8.5 %collective-permute-start = (bf16[1,64,256]{2,1,0:T(8,128)(2,1)S(1)}, bf16[1,64,256]{2,1,0:T(8,128)(2,1)S(1)}, u32[]{:S(2)}, u32[]{:S(2)}) collective-permute-start(bf16[1,64,256]{2,1,0:T(8,128)(2,1)S(1)} %slice.163), channel_id=1, source_target_pairs={{0,4},{4,8},{8,12},{1,5},{5,9},{9,13},{2,6},{6,10},{10,14},{3,7},{... | collective-permute-start | bytes 98312 | tf_op jit(solution)/shard_map/ppermute | solution.py:18
  12.8 5.2 %collective-permute-start.1 = (bf16[1,64,256]{2,1,0:T(8,128)(2,1)S(1)}, bf16[1,64,256]{2,1,0:T(8,128)(2,1)S(1)}, u32[]{:S(2)}, u32[]{:S(2)}) collective-permute-start(bf16[1,64,256]{2,1,0:T(8,128)(2,1)S(1)} %slice.165), channel_id=1, source_target_pairs={{4,0},{8,4},{12,8},{5,1},{9,5},{13,9},{6,2},{10,6},{14,10},{7,3},{... | collective-permute-start | bytes 98312 | tf_op jit(solution)/shard_map/ppermute | solution.py:21
  19.7 20.2 %copy-start.6 = (bf16[16,64,256]{2,1,0:T(8,128)(2,1)}, bf16[16,64,256]{2,1,0:T(8,128)(2,1)S(1)}, u32[]{:S(2)}) copy-start(bf16[16,64,256]{2,1,0:T(8,128)(2,1)S(1)} %get-tuple-element.83) | copy-start | bytes 1572868
  19.7 21.1 %copy-start.4 = (bf16[16,64,256]{2,1,0:T(8,128)(2,1)}, bf16[16,64,256]{2,1,0:T(8,128)(2,1)S(1)}, u32[]{:S(2)}) copy-start(bf16[16,64,256]{2,1,0:T(8,128)(2,1)S(1)} %get-tuple-element.82) | copy-start | bytes 1572868
  19.7 6.4 %copy-start.23 = (bf16[18,64,256]{2,1,0:T(8,128)(2,1)}, bf16[18,64,256]{2,1,0:T(8,128)(2,1)S(1)}, u32[]{:S(2)}) copy-start(bf16[18,64,256]{2,1,0:T(8,128)(2,1)S(1)} %constant_dynamic-update-slice_fusion) | copy-start | bytes 1769476
  19.8 22.0 %collective-permute-start.2 = (bf16[18,4,256]{2,1,0:T(4,128)(2,1)S(1)}, bf16[18,4,256]{2,1,0:T(4,128)(2,1)S(1)}, u32[]{:S(2)}, u32[]{:S(2)}) collective-permute-start(bf16[18,4,256]{2,1,0:T(4,128)(2,1)S(1)} %get-tuple-element.75), channel_id=1, source_target_pairs={{0,1},{1,2},{2,3},{4,5},{5,6},{6,7},{8,9},{9,10},{10,11},{12,13},{... | collective-permute-start | bytes 110600 | tf_op jit(solution)/shard_map/ppermute | solution.py:18
  22.9 18.9 %collective-permute-start.3 = (bf16[18,4,256]{2,1,0:T(4,128)(2,1)S(1)}, bf16[18,4,256]{2,1,0:T(4,128)(2,1)S(1)}, u32[]{:S(2)}, u32[]{:S(2)}) collective-permute-start(bf16[18,4,256]{2,1,0:T(4,128)(2,1)S(1)} %get-tuple-element.74), channel_id=1, source_target_pairs={{1,0},{2,1},{3,2},{5,4},{6,5},{7,6},{9,8},{10,9},{11,10},{13,12},{... | collective-permute-start | bytes 110600 | tf_op jit(solution)/shard_map/ppermute | solution.py:21
  47.0 16.1 %copy-start.7 = (bf16[16,64,256]{2,1,0:T(8,128)(2,1)}, bf16[16,64,256]{2,1,0:T(8,128)(2,1)S(1)}, u32[]{:S(2)}) copy-start(bf16[16,64,256]{2,1,0:T(8,128)(2,1)S(1)} %get-tuple-element.61) | copy-start | bytes 1572868
  47.0 16.1 %copy-start.9 = (bf16[16,64,256]{2,1,0:T(8,128)(2,1)}, bf16[16,64,256]{2,1,0:T(8,128)(2,1)S(1)}, u32[]{:S(2)}) copy-start(bf16[16,64,256]{2,1,0:T(8,128)(2,1)S(1)} %get-tuple-element.73) | copy-start | bytes 1572868
  59.0 9.9 %copy-start.19 = (bf16[256,4,256]{2,1,0:T(4,128)(2,1)S(1)}, bf16[256,4,256]{2,1,0:T(4,128)(2,1)}, u32[]{:S(2)}) copy-start(bf16[256,4,256]{2,1,0:T(4,128)(2,1)} %concatenate.112) | copy-start | bytes 1572868
  59.0 10.8 %copy-start.17 = (bf16[256,4,256]{2,1,0:T(4,128)(2,1)S(1)}, bf16[256,4,256]{2,1,0:T(4,128)(2,1)}, u32[]{:S(2)}) copy-start(bf16[256,4,256]{2,1,0:T(4,128)(2,1)} %concatenate.114) | copy-start | bytes 1572868
  59.0 11.7 %copy-start.18 = (bf16[256,4,256]{2,1,0:T(4,128)(2,1)S(1)}, bf16[256,4,256]{2,1,0:T(4,128)(2,1)}, u32[]{:S(2)}) copy-start(bf16[256,4,256]{2,1,0:T(4,128)(2,1)} %concatenate.115) | copy-start | bytes 1572868
  59.0 12.6 %copy-start.13 = (bf16[768,2304]{1,0:T(8,128)(2,1)S(1)}, bf16[768,2304]{1,0:T(8,128)(2,1)}, u32[]{:S(2)}) copy-start(bf16[768,2304]{1,0:T(8,128)(2,1)} %copy.210) | copy-start | bytes 10616836
  77.7 8.3 %copy-start.28 = (f32[512]{0:T(512)S(1)}, f32[512]{0:T(512)}, u32[]{:S(2)}) copy-start(f32[512]{0:T(512)} %param.10) | copy-start | bytes 6148
  86.0 161.9 %copy-start.29 = (f32[128]{0:T(128)}, f32[128]{0:T(128)S(1)}, u32[]{:S(2)}) copy-start(f32[128]{0:T(128)S(1)} %add_rsqrt_fusion) | copy-start | bytes 1540
  177.7 60.7 %all-to-all-start = ((bf16[16,128,1024]{1,2,0:T(8,128)(2,1)}), bf16[16,128,1024]{1,2,0:T(8,128)(2,1)}, u32[]{:S(2)}, u32[]{:S(2)}) async-start(bf16[16,128,1024]{1,2,0:T(8,128)(2,1)} %pad_maximum_fusion.1), calls=%async_computation | async-start | bytes 8388608 | tf_op jit(solution)/shard_map/all_to_all | solution.py:151
  183.2 212.3 %reduce-scatter.5.cloned.1.call-start = ((), (), s32[]{:S(2)}) async-start(), calls=%async_computation.4 | async-start | bytes 4491264
  192.0 9.8 %copy-start.5 = (bf16[16,64,256]{2,1,0:T(8,128)(2,1)S(1)}, bf16[16,64,256]{2,1,0:T(8,128)(2,1)}, u32[]{:S(2)}) copy-start(bf16[16,64,256]{2,1,0:T(8,128)(2,1)} %copy-done.4) | copy-start | bytes 1572868
  192.0 10.7 %copy-start.8 = (bf16[16,64,256]{2,1,0:T(8,128)(2,1)S(1)}, bf16[16,64,256]{2,1,0:T(8,128)(2,1)}, u32[]{:S(2)}) copy-start(bf16[16,64,256]{2,1,0:T(8,128)(2,1)} %copy-done.7) | copy-start | bytes 1572868
  192.0 11.6 %copy-start.16 = (bf16[2048,512]{0,1:T(8,128)(2,1)S(1)}, bf16[2048,512]{0,1:T(8,128)(2,1)}, u32[]{:S(2)}) copy-start(bf16[2048,512]{0,1:T(8,128)(2,1)} %copy.219) | copy-start | bytes 6291460
  242.0 6.4 %copy-start.3 = (bf16[128,2048]{1,0:T(8,128)(2,1)S(1)}, bf16[128,2048]{1,0:T(8,128)(2,1)}, u32[]{:S(2)}) copy-start(bf16[128,2048]{1,0:T(8,128)(2,1)} %reshape.233) | copy-start | bytes 1572868
  247.9 12.6 %copy-start.31 = (f32[128]{0:T(128)}, f32[128]{0:T(128)S(1)}, u32[]{:S(2)}) copy-start(f32[128]{0:T(128)S(1)} %get-tuple-element.94) | copy-start | bytes 1540
  283.0 15.7 %collective-permute-start.4 = (bf16[1,64,256]{2,1,0:T(8,128)(2,1)S(1)}, bf16[1,64,256]{2,1,0:T(8,128)(2,1)S(1)}, u32[]{:S(2)}, u32[]{:S(2)}) collective-permute-start(bf16[1,64,256]{2,1,0:T(8,128)(2,1)S(1)} %get-tuple-element.80), channel_id=1, source_target_pairs={{0,4},{4,8},{8,12},{1,5},{5,9},{9,13},{2,6},{6,10},{10,14},{3,7},{... | collective-permute-start | bytes 98312 | tf_op jit(solution)/shard_map/ppermute | solution.py:18
  285.9 7.1 %copy-start.11 = (f32[16,64,256]{2,1,0:T(8,128)S(1)}, f32[16,64,256]{2,1,0:T(8,128)}, u32[]{:S(2)}) copy-start(f32[16,64,256]{2,1,0:T(8,128)} %reshape.239) | copy-start | bytes 3145732
  285.9 7.1 %copy-start.12 = (f32[16,64,256]{2,1,0:T(8,128)S(1)}, f32[16,64,256]{2,1,0:T(8,128)}, u32[]{:S(2)}) copy-start(f32[16,64,256]{2,1,0:T(8,128)} %reshape.261) | copy-start | bytes 3145732
  285.9 8.3 %copy-start.1 = (f32[8,8,2,2,2,2,256]{6,5,4,3,2,1,0:T(2,128)S(1)}, f32[8,8,2,2,2,2,256]{6,5,4,3,2,1,0:T(2,128)}, u32[]{:S(2)}) copy-start(f32[8,8,2,2,2,2,256]{6,5,4,3,2,1,0:T(2,128)} %reshape.264) | copy-start | bytes 3145732
  285.9 12.8 %collective-permute-start.5 = (bf16[1,64,256]{2,1,0:T(8,128)(2,1)S(1)}, bf16[1,64,256]{2,1,0:T(8,128)(2,1)S(1)}, u32[]{:S(2)}, u32[]{:S(2)}) collective-permute-start(bf16[1,64,256]{2,1,0:T(8,128)(2,1)S(1)} %get-tuple-element.81), channel_id=1, source_target_pairs={{4,0},{8,4},{12,8},{5,1},{9,5},{13,9},{6,2},{10,6},{14,10},{7,3},{... | collective-permute-start | bytes 98312 | tf_op jit(solution)/shard_map/ppermute | solution.py:21
  299.6 9.9 %collective-permute-start.6 = (bf16[18,4,256]{2,1,0:T(4,128)(2,1)S(1)}, bf16[18,4,256]{2,1,0:T(4,128)(2,1)S(1)}, u32[]{:S(2)}, u32[]{:S(2)}) collective-permute-start(bf16[18,4,256]{2,1,0:T(4,128)(2,1)S(1)} %get-tuple-element.70), channel_id=1, source_target_pairs={{1,0},{2,1},{3,2},{5,4},{6,5},{7,6},{9,8},{10,9},{11,10},{13,12},{... | collective-permute-start | bytes 110600 | tf_op jit(solution)/shard_map/ppermute | solution.py:21
  300.9 8.6 %collective-permute-start.7 = (bf16[18,4,256]{2,1,0:T(4,128)(2,1)S(1)}, bf16[18,4,256]{2,1,0:T(4,128)(2,1)S(1)}, u32[]{:S(2)}, u32[]{:S(2)}) collective-permute-start(bf16[18,4,256]{2,1,0:T(4,128)(2,1)S(1)} %get-tuple-element.69), channel_id=1, source_target_pairs={{0,1},{1,2},{2,3},{4,5},{5,6},{6,7},{8,9},{9,10},{10,11},{12,13},{... | collective-permute-start | bytes 110600 | tf_op jit(solution)/shard_map/ppermute | solution.py:18
  341.0 51.2 %all-to-all-start.1 = ((bf16[16,432,256]{2,1,0:T(8,128)(2,1)}), bf16[16,432,256]{2,1,0:T(8,128)(2,1)}, u32[]{:S(2)}, u32[]{:S(2)}) async-start(bf16[16,432,256]{2,1,0:T(8,128)(2,1)} %bitcast.154), calls=%async_computation.1 | async-start | bytes 7077888 | tf_op jit(solution)/shard_map/all_to_all | solution.py:245
  (16 other events, 59.8 us)
Sparse Core Ops, SparseCore 0:
  89.5 55.5 all-gather.1
  265.2 73.6 reduce-scatter.4

commit v5 on v2

--- a/solution.py
+++ b/solution.py
@@ -11,16 +11,44 @@
 
 
 def padded_2(block, sides, width):
-    for axis, dim in sides:
-        count = lax.axis_size(axis)
-        forward = [(i, i + 1) for i in range(count - 1)]
-        backward = [(target, source) for source, target in forward]
-        low = lax.ppermute(
-            lax.slice_in_dim(block, block.shape[dim] - width, None, axis=dim), axis, forward
-        )
-        high = lax.ppermute(lax.slice_in_dim(block, 0, width, axis=dim), axis, backward)
-        block = jnp.concatenate([low, block, high], axis=dim)
-    return block
+    (axis_x, dim_x), (axis_y, dim_y) = sides
+    count_x = lax.axis_size(axis_x)
+    count_y = lax.axis_size(axis_y)
+    extent_x = block.shape[dim_x]
+    extent_y = block.shape[dim_y]
+    edges = {
+        -1: (extent_x - width, extent_x),
+        0: (0, extent_x),
+        1: (0, width),
+    }
+    edges_y = {
+        -1: (extent_y - width, extent_y),
+        0: (0, extent_y),
+        1: (0, width),
+    }
+    received = {}
+    for offset_x in (-1, 0, 1):
+        for offset_y in (-1, 0, 1):
+            if offset_x == 0 and offset_y == 0:
+                continue
+            piece = lax.slice_in_dim(block, *edges[offset_x], axis=dim_x)
+            piece = lax.slice_in_dim(piece, *edges_y[offset_y], axis=dim_y)
+            pairs = []
+            for source_x in range(count_x):
+                for source_y in range(count_y):
+                    target_x = source_x - offset_x
+                    target_y = source_y - offset_y
+                    if 0 <= target_x < count_x and 0 <= target_y < count_y:
+                        pairs.append(
+                            (source_x * count_y + source_y, target_x * count_y + target_y)
+                        )
+            received[offset_x, offset_y] = lax.ppermute(piece, (axis_x, axis_y), pairs)
+    received[0, 0] = block
+    rows = [
+        jnp.concatenate([received[offset_x, offset_y] for offset_y in (-1, 0, 1)], axis=dim_y)
+        for offset_x in (-1, 0, 1)
+    ]
+    return jnp.concatenate(rows, axis=dim_x)
 
 
 def to_tokens(volume):

time: 383 us -> 400 us (1.044)
  starting transfers between devices: 33.8 us -> 53.2 us
  other arithmetic: 33.5 us -> 28 us
  local copies, waits for them, and re-layouts: 150 us -> 154 us
    ppermute x8 -> x16, starting transfers between devices: 21.3 us -> 41.5 us  [padded_2(): received[offset_x, offset_y] = lax.ppermute(piece, (axis_x, axis_y), pairs)]
    all_gather x1, waiting for transfers between devices: 47.9 us -> 40.6 us  [local(): lax.all_gather(qkv_rows[:, model_width:], ('gx', 'gy'), axis=0, tiled=True)]
    concatenate x5 -> x6, other arithmetic: 11.6 us -> 5.64 us  [the longest x2 3.77 us: padded_2(): return jnp.concatenate(rows, axis=dim_x)]
  transfers between devices with their start and end apart: 12 -> 20, of which waited for: 5 -> 5; matrix products, arithmetic and copies ran while one was open for 44% -> 42% of each run, Pallas kernels for 0% -> 0%
where the time goes in v5:
time: 400 us; the launch traced here: 392 us
  local copies, waits for them, and re-layouts  154 us (38%)
  matrix products  74 us (18%)
  waiting for transfers between devices  67.3 us (17%)
  starting transfers between devices  53.2 us (13%)
  other arithmetic  28 us (7%)
  between operations  15.3 us (4%)
    ppermute x16, starting transfers between devices, padded_2(): received[offset_x, offset_y] = lax.ppermute(piece, (axis_x, axis_y), pairs)  41.5 us
    all_gather x1, waiting for transfers between devices, local(): lax.all_gather(qkv_rows[:, model_width:], ('gx', 'gy'), axis=0, tiled=True)  40.6 us
    unnamed x111, local copies, waits for them, and re-layouts  39.8 us
    reshape x9, local copies, waits for them, and re-layouts, plane_columns(): padded[start_x:start_x + extent_x, start_y:start_y + extent_y]  17.7 us
    convert_element_type x6, local copies, waits for them, and re-layouts, local(): d_act_grid = from_tokens(d_activation, extent_x, extent_y, extent_z).resh...  16.5 us
    all_to_all x1, waiting for transfers between devices, local(): conv_rows = lax.all_to_all(conv_part, ('gx', 'gy'), 0, 0, tiled=True)  15.6 us
    reshape x2, local copies, waits for them, and re-layouts, local(): taps = conv_weight.reshape(9, 3, channels, channels)  13 us
    dot_general x3, matrix products, local(): jnp.einsum('vr,vc->rc', columns, shifted.reshape(voxels, channels), prefe...  12.9 us
  transfers between devices with their start and end apart: 20, of which 5 were waited for; matrix products, arithmetic and copies ran while one was open for 42% of the time, Pallas kernels for 0%

profile of v5, /device:TPU:1, one launch (start us, length us, event | category | flops | bytes accessed | tf_op | source)
XLA Modules:
  0.0 391.6 jit_solution(11261800631063552747)
XLA Ops:
  8.2 3.9 %collective-permute-start.3 = (bf16[16,1,4,256]{3,2,1,0:T(4,128)(2,1)S(1)}, bf16[16,1,4,256]{3,2,1,0:T(4,128)(2,1)S(1)}, u32[]{:S(2)}, u32[]{:S(2)}) collective-permute-start(bf16[16,1,4,256]{3,2,1,0:T(4,128)(2,1)S(1)} %get-tuple-element.89), channel_id=1, source_target_pairs={{0,1},{1,2},{2,3},{4,5},{5,6},{6,7},{8,9},{9,10},{10,11},{12,13},{... | collective-permute-start | bytes 98312 | tf_op jit(solution)/shard_map/ppermute | solution.py:45
  14.2 6.1 %collective-permute-start = (bf16[1,1,4,256]{3,2,1,0:T(4,128)(2,1)S(1)}, bf16[1,1,4,256]{3,2,1,0:T(4,128)(2,1)S(1)}, u32[]{:S(2)}, u32[]{:S(2)}) collective-permute-start(bf16[1,1,4,256]{3,2,1,0:T(4,128)(2,1)S(1)} %get-tuple-element.81), channel_id=1, source_target_pairs={{0,5},{1,6},{2,7},{4,9},{5,10},{6,11},{8,13},{9,14},{10,15},{16,21... | collective-permute-start | bytes 6152 | tf_op jit(solution)/shard_map/ppermute | solution.py:45
  21.6 4.3 %collective-permute-start.5 = (bf16[1,1,4,256]{3,2,1,0:T(4,128)(2,1)S(1)}, bf16[1,1,4,256]{3,2,1,0:T(4,128)(2,1)S(1)}, u32[]{:S(2)}, u32[]{:S(2)}) collective-permute-start(bf16[1,1,4,256]{3,2,1,0:T(4,128)(2,1)S(1)} %get-tuple-element.79), channel_id=1, source_target_pairs={{4,1},{5,2},{6,3},{8,5},{9,6},{10,7},{12,9},{13,10},{14,11},{20,17... | collective-permute-start | bytes 6152 | tf_op jit(solution)/shard_map/ppermute | solution.py:45
  28.6 5.0 %copy.193 = bf16[9,3,256,256]{3,1,2,0:T(4,128)(2,1)S(1)} copy(bf16[9,3,256,256]{3,2,1,0:T(8,128)(2,1)} %bitcast.163) | data formatting | bytes 7077888 | tf_op jit(solution)/shard_map/reshape | solution.py:97
  36.4 5.8 %copy.194 = bf16[768,2304]{1,0:T(8,128)(2,1)} copy(bf16[768,2304]{0,1:T(8,128)(2,1)} %bitcast.161) | data formatting | bytes 7077888 | tf_op jit(solution)/shard_map/dot_general | solution.py:102
  57.2 3.8 fusion.10
  88.8 40.6 %all-gather.2.cloned.1.call-done = bf16[2048,1024]{1,0:T(8,128)(2,1)} async-done(((bf16[128,1024]{1,0:T(8,128)(2,1)}), bf16[2048,1024]{1,0:T(8,128)(2,1)}) %all-gather.2.cloned.1.call-update) | async-done | bytes 4194320 | tf_op jit(solution)/shard_map/all_gather | solution.py:123
  129.4 4.5 %fusion.49 = (bf16[2048,512]{1,0:T(8,128)(2,1)}, bf16[2048,512]{1,0:T(8,128)(2,1)}) fusion(bf16[2048,1024]{1,0:T(8,128)(2,1)} %all-gather.2.cloned.1.call-done), kind=kLoop, calls=%fused_computation.121 | loop fusion | bytes 8388608 | tf_op jit(solution)/shard_map/slice | solution.py:127
  133.8 4.4 %copy.200 = bf16[2048,512]{0,1:T(8,128)(2,1)} copy(bf16[2048,512]{1,0:T(8,128)(2,1)} %get-tuple-element.50) | data formatting | bytes 4194304 | tf_op jit(solution)/shard_map/slice | solution.py:126
  138.3 3.9 %copy.203 = bf16[2048,512]{0,1:T(8,128)(2,1)} copy(bf16[2048,512]{1,0:T(8,128)(2,1)} %get-tuple-element.49) | data formatting | bytes 4194304 | tf_op jit(solution)/shard_map/slice | solution.py:127
  151.4 5.9 %multiply_convert_fusion = bf16[8,64,2048]{2,1,0:T(8,128)(2,1)S(1)} fusion(bf16[128,8,64]{0,2,1:T(8,128)(2,1)S(1)} %bitcast.200, bf16[8,128,2048]{2,1,0:T(8,128)(2,1)S(1)} %get-tuple-element.99, f32[8,128]{1,0:T(8,128)S(1)} %get-tuple-element.98, f32[8,128,2048]{2,1,0:T(8,128)S(1)} %get-tuple-element.97, f32[8,128]{1,0:T(8,128)S(1)} %get-tuple-element.96), kind=kOutput, calls=%fused_computation.15 | convolution fusion | flops 1623195648 | bytes 14819328 | tf_op jit(solution)/shard_map/hij,ihe->jhe/dot_general | solution.py:159
  162.1 5.4 %all-to-all-start = ((bf16[16,128,1024]{1,2,0:T(8,128)(2,1)}), bf16[16,128,1024]{1,2,0:T(8,128)(2,1)}, u32[]{:S(2)}, u32[]{:S(2)}) async-start(bf16[16,128,1024]{1,2,0:T(8,128)(2,1)} %pad_maximum_fusion.1), calls=%async_computation | async-start | bytes 8388608 | tf_op jit(solution)/shard_map/all_to_all | solution.py:177
  197.3 5.1 %fusion.23 = bf16[8,64,128]{2,1,0:T(8,128)(2,1)S(1)} fusion(bf16[2048,8,64]{0,2,1:T(8,128)(2,1)S(1)} %bitcast.175, f32[8,128,2048]{2,1,0:T(8,128)} %copy-done.2, f32[8,128]{1,0:T(8,128)S(1)} %get-tuple-element.96), kind=kOutput, calls=%fused_computation.34 | convolution fusion | flops 274792448 | bytes 10620928 | tf_op jit(solution)/shard_map/hij,jhe->ihe/dot_general | solution.py:139
  205.7 12.6 %fusion.26 = bf16[8,64,128]{2,1,0:T(8,128)(2,1)} fusion(bf16[2048,8,64]{0,2,1:T(8,128)(2,1)} %bitcast.169, bf16[8,128,2048]{2,1,0:T(8,128)(2,1)} %copy-done.37, f32[8,128]{1,0:T(8,128)} %copy-done.38, f32[8,128,2048]{2,1,0:T(8,128)} %copy-done.2, f32[8,128]{1,0:T(8,128)S(1)} %get-tuple-element.96), kind=kOutput, calls=%fused_computation.36 | convolution fusion | flops 1621229568 | bytes 14819328 | tf_op jit(solution)/shard_map/hij,jhe->ihe/dot_general | solution.py:153
  218.3 4.5 %all-to-all-done = bf16[16,128,1024]{1,2,0:T(8,128)(2,1)} async-done(((bf16[16,128,1024]{1,2,0:T(8,128)(2,1)}), bf16[16,128,1024]{1,2,0:T(8,128)(2,1)}, u32[]{:S(2)}, u32[]{:S(2)}) %all-to-all-start) | async-done | bytes 4194336 | tf_op jit(solution)/shard_map/all_to_all | solution.py:177
  222.8 3.5 reduce.2
  236.3 4.4 %reshape.249 = bf16[16,512,128]{2,1,0:T(8,128)(2,1)} reshape(bf16[2048,512]{1,0:T(8,128)(2,1)} %convolution_convert_fusion.4) | data formatting | bytes 4194304 | tf_op jit(solution)/shard_map/reshape | solution.py:255
  240.7 4.3 %reshape.250 = bf16[16,384,128]{2,1,0:T(8,128)(2,1)} reshape(bf16[512,1536]{1,0:T(8,128)(2,1)} %convolution_convert_fusion.5) | data formatting | bytes 3145728 | tf_op jit(solution)/shard_map/reshape | solution.py:255
  245.8 3.7 pad_maximum_fusion
  249.6 4.2 %fusion.16 = f32[128,2048]{1,0:T(8,128)} fusion(bf16[2048,512]{1,0:T(8,128)(2,1)S(1)} %copy-done, bf16[128,512]{1,0:T(8,128)(2,1)S(1)} %reshape.226, f32[128,512]{1,0:T(8,128)} %copy-done.26, f32[128,512]{1,0:T(8,128)S(1)} %get-tuple-element.95, f32[128]{0:T(128)S(1)} %copy-done.35, f32[128]{0:T(128)} %copy-done.36, f32[512]{0:T(512)S(1)} %copy-done.31, ...), kind=kOutput, calls=%fused_computation.27 | convolution fusion | flops 1611726848 | bytes 3805184 | tf_op jit(solution)/shard_map/dot_general | solution.py:202
  277.6 4.5 %collective-permute-start.14 = (bf16[1,16,4,256]{3,2,1,0:T(4,128)(2,1)S(1)}, bf16[1,16,4,256]{3,2,1,0:T(4,128)(2,1)S(1)}, u32[]{:S(2)}, u32[]{:S(2)}) collective-permute-start(bf16[1,16,4,256]{3,2,1,0:T(4,128)(2,1)S(1)} %slice.229), channel_id=1, source_target_pairs={{0,4},{1,5},{2,6},{3,7},{4,8},{5,9},{6,10},{7,11},{8,12},{9,13},{1... | collective-permute-start | bytes 98312 | tf_op jit(solution)/shard_map/ppermute | solution.py:45
  282.1 5.0 %convolution_convert_fusion.1 = bf16[2304,256]{1,0:T(8,128)(2,1)} fusion(bf16[1024,2304]{1,0:T(8,128)(2,1)} %constant_dynamic-update-slice_fusion.21, bf16[1024,256]{1,0:T(8,128)(2,1)} %copy-done.27), kind=kOutput, calls=%fused_computation.19 | convolution fusion | flops 1208549376 | bytes 6422528 | tf_op jit(solution)/shard_map/vr,vc->rc/dot_general | solution.py:218
  293.0 4.7 %collective-permute-start.13 = (bf16[1,1,4,256]{3,2,1,0:T(4,128)(2,1)S(1)}, bf16[1,1,4,256]{3,2,1,0:T(4,128)(2,1)S(1)}, u32[]{:S(2)}, u32[]{:S(2)}) collective-permute-start(bf16[1,1,4,256]{3,2,1,0:T(4,128)(2,1)S(1)} %get-tuple-element.90), channel_id=1, source_target_pairs={{0,5},{1,6},{2,7},{4,9},{5,10},{6,11},{8,13},{9,14},{10,15},{16,21... | collective-permute-start | bytes 6152 | tf_op jit(solution)/shard_map/ppermute | solution.py:45
  299.1 3.6 collective-permute-done.15
  312.4 3.9 %convolution_convert_fusion.2 = bf16[2304,256]{1,0:T(8,128)(2,1)S(1)} fusion(bf16[1024,2304]{1,0:T(8,128)(2,1)} %constant_dynamic-update-slice_fusion.21, bf16[1024,256]{1,0:T(8,128)(2,1)} %reshape.247), kind=kOutput, calls=%fused_computation.20 | convolution fusion | flops 1208549376 | bytes 6422528 | tf_op jit(solution)/shard_map/vr,vc->rc/dot_general | solution.py:218
  316.4 3.9 convolution_convert_fusion
  322.3 6.0 %all-to-all-start.1 = ((bf16[16,432,256]{2,1,0:T(8,128)(2,1)}), bf16[16,432,256]{2,1,0:T(8,128)(2,1)}, u32[]{:S(2)}, u32[]{:S(2)}) async-start(bf16[16,432,256]{2,1,0:T(8,128)(2,1)} %bitcast.160), calls=%async_computation.1 | async-start | bytes 7077888 | tf_op jit(solution)/shard_map/all_to_all | solution.py:270
  328.4 8.0 %copy.213 = bf16[9,3,256,256]{2,1,3,0:T(4,128)(2,1)} copy(bf16[9,3,256,256]{3,2,1,0:T(8,128)(2,1)} %bitcast.164) | data formatting | bytes 7077888 | tf_op jit(solution)/shard_map/reshape | solution.py:97
  336.4 5.1 %copy.236 = bf16[288,8,3,256]{3,1,2,0:T(8,128)(2,1)} copy(bf16[288,8,3,256]{3,2,1,0:T(4,128)(2,1)} %bitcast.158) | data formatting | bytes 7077888
  341.5 5.9 %copy.214 = bf16[768,2304]{1,0:T(8,128)(2,1)} copy(bf16[768,2304]{0,1:T(8,128)(2,1)} %bitcast.162) | data formatting | bytes 7077888 | tf_op jit(solution)/shard_map/dot_general | solution.py:235
  352.4 5.7 %fusion.8 = f32[256,4,3,256]{3,0,2,1:T(8,128)S(1)} fusion(bf16[3,256,2304,1]{2,1,0,3:T(8,128)(2,1)S(1)} %bitcast.173, bf16[256,4,2304]{2,0,1:T(8,128)(2,1)} %constant_dynamic-update-slice_fusion.12), kind=kOutput, calls=%fused_computation.9 | convolution fusion | flops 3623878656 | bytes 11403264 | tf_op jit(solution)/shard_map/dot_general | solution.py:235
  359.7 15.6 %all-to-all-done.1 = bf16[16,432,256]{2,1,0:T(8,128)(2,1)} async-done(((bf16[16,432,256]{2,1,0:T(8,128)(2,1)}), bf16[16,432,256]{2,1,0:T(8,128)(2,1)}, u32[]{:S(2)}, u32[]{:S(2)}) %all-to-all-start.1) | async-done | bytes 3538976 | tf_op jit(solution)/shard_map/all_to_all | solution.py:270
  (243 shorter events, 168.2 us)
Async XLA Ops:
  7.2 60.8 %copy-start = (bf16[2048,512]{1,0:T(8,128)(2,1)S(1)}, bf16[2048,512]{1,0:T(8,128)(2,1)}, u32[]{:S(2)}) copy-start(bf16[2048,512]{1,0:T(8,128)(2,1)} %param.9) | copy-start | bytes 6291460
  7.2 122.2 %all-gather.2.cloned.1.call-start = ((), (), s32[]{:S(2)}) async-start(), calls=%async_computation.3 | async-start | bytes 4456448 | tf_op jit(solution)/shard_map/all_gather | solution.py:123
  8.2 34.1 %collective-permute-start.3 = (bf16[16,1,4,256]{3,2,1,0:T(4,128)(2,1)S(1)}, bf16[16,1,4,256]{3,2,1,0:T(4,128)(2,1)S(1)}, u32[]{:S(2)}, u32[]{:S(2)}) collective-permute-start(bf16[16,1,4,256]{3,2,1,0:T(4,128)(2,1)S(1)} %get-tuple-element.89), channel_id=1, source_target_pairs={{0,1},{1,2},{2,3},{4,5},{5,6},{6,7},{8,9},{9,10},{10,11},{12,13},{... | collective-permute-start | bytes 98312 | tf_op jit(solution)/shard_map/ppermute | solution.py:45
  12.1 31.4 %collective-permute-start.4 = (bf16[16,1,4,256]{3,2,1,0:T(4,128)(2,1)S(1)}, bf16[16,1,4,256]{3,2,1,0:T(4,128)(2,1)S(1)}, u32[]{:S(2)}, u32[]{:S(2)}) collective-permute-start(bf16[16,1,4,256]{3,2,1,0:T(4,128)(2,1)S(1)} %get-tuple-element.88), channel_id=1, source_target_pairs={{1,0},{2,1},{3,2},{5,4},{6,5},{7,6},{9,8},{10,9},{11,10},{13,12},{... | collective-permute-start | bytes 98312 | tf_op jit(solution)/shard_map/ppermute | solution.py:45
  14.2 32.8 %collective-permute-start = (bf16[1,1,4,256]{3,2,1,0:T(4,128)(2,1)S(1)}, bf16[1,1,4,256]{3,2,1,0:T(4,128)(2,1)S(1)}, u32[]{:S(2)}, u32[]{:S(2)}) collective-permute-start(bf16[1,1,4,256]{3,2,1,0:T(4,128)(2,1)S(1)} %get-tuple-element.81), channel_id=1, source_target_pairs={{0,5},{1,6},{2,7},{4,9},{5,10},{6,11},{8,13},{9,14},{10,15},{16,21... | collective-permute-start | bytes 6152 | tf_op jit(solution)/shard_map/ppermute | solution.py:45
  20.3 28.9 %collective-permute-start.2 = (bf16[1,1,4,256]{3,2,1,0:T(4,128)(2,1)S(1)}, bf16[1,1,4,256]{3,2,1,0:T(4,128)(2,1)S(1)}, u32[]{:S(2)}, u32[]{:S(2)}) collective-permute-start(bf16[1,1,4,256]{3,2,1,0:T(4,128)(2,1)S(1)} %get-tuple-element.80), channel_id=1, source_target_pairs={{1,4},{2,5},{3,6},{5,8},{6,9},{7,10},{9,12},{10,13},{11,14},{17,20... | collective-permute-start | bytes 6152 | tf_op jit(solution)/shard_map/ppermute | solution.py:45
  21.6 27.6 %collective-permute-start.5 = (bf16[1,1,4,256]{3,2,1,0:T(4,128)(2,1)S(1)}, bf16[1,1,4,256]{3,2,1,0:T(4,128)(2,1)S(1)}, u32[]{:S(2)}, u32[]{:S(2)}) collective-permute-start(bf16[1,1,4,256]{3,2,1,0:T(4,128)(2,1)S(1)} %get-tuple-element.79), channel_id=1, source_target_pairs={{4,1},{5,2},{6,3},{8,5},{9,6},{10,7},{12,9},{13,10},{14,11},{20,17... | collective-permute-start | bytes 6152 | tf_op jit(solution)/shard_map/ppermute | solution.py:45
  36.4 10.0 %copy-start.4 = (bf16[16,16,4,256]{3,2,1,0:T(4,128)(2,1)S(1)}, bf16[16,16,4,256]{3,2,1,0:T(4,128)(2,1)}, u32[]{:S(2)}) copy-start(bf16[16,16,4,256]{3,2,1,0:T(4,128)(2,1)} %param.7) | copy-start | bytes 1572868
  42.2 7.0 %collective-permute-start.7 = (bf16[1,1,4,256]{3,2,1,0:T(4,128)(2,1)S(1)}, bf16[1,1,4,256]{3,2,1,0:T(4,128)(2,1)S(1)}, u32[]{:S(2)}, u32[]{:S(2)}) collective-permute-start(bf16[1,1,4,256]{3,2,1,0:T(4,128)(2,1)S(1)} %get-tuple-element.82), channel_id=1, source_target_pairs={{5,0},{6,1},{7,2},{9,4},{10,5},{11,6},{13,8},{14,9},{15,10},{21,16... | collective-permute-start | bytes 6152 | tf_op jit(solution)/shard_map/ppermute | solution.py:45
  43.6 5.7 %collective-permute-start.1 = (bf16[1,16,4,256]{3,2,1,0:T(4,128)(2,1)S(1)}, bf16[1,16,4,256]{3,2,1,0:T(4,128)(2,1)S(1)}, u32[]{:S(2)}, u32[]{:S(2)}) collective-permute-start(bf16[1,16,4,256]{3,2,1,0:T(4,128)(2,1)S(1)} %get-tuple-element.84), channel_id=1, source_target_pairs={{0,4},{1,5},{2,6},{3,7},{4,8},{5,9},{6,10},{7,11},{8,12},{9,13},{1... | collective-permute-start | bytes 98312 | tf_op jit(solution)/shard_map/ppermute | solution.py:45
  46.9 7.4 %copy-start.14 = (bf16[16,16,4,256]{3,2,1,0:T(4,128)(2,1)}, bf16[16,16,4,256]{3,2,1,0:T(4,128)(2,1)S(1)}, u32[]{:S(2)}) copy-start(bf16[16,16,4,256]{3,2,1,0:T(4,128)(2,1)S(1)} %get-tuple-element.85) | copy-start | bytes 1572868
  46.9 5.2 %collective-permute-start.6 = (bf16[1,16,4,256]{3,2,1,0:T(4,128)(2,1)S(1)}, bf16[1,16,4,256]{3,2,1,0:T(4,128)(2,1)S(1)}, u32[]{:S(2)}, u32[]{:S(2)}) collective-permute-start(bf16[1,16,4,256]{3,2,1,0:T(4,128)(2,1)S(1)} %get-tuple-element.83), channel_id=1, source_target_pairs={{4,0},{5,1},{6,2},{7,3},{8,4},{9,5},{10,6},{11,7},{12,8},{13,9},{1... | collective-permute-start | bytes 98312 | tf_op jit(solution)/shard_map/ppermute | solution.py:45
  61.4 8.4 %copy-start.31 = (f32[512]{0:T(512)S(1)}, f32[512]{0:T(512)}, u32[]{:S(2)}) copy-start(f32[512]{0:T(512)} %param.10) | copy-start | bytes 6148
  69.7 162.7 %copy-start.32 = (f32[128]{0:T(128)}, f32[128]{0:T(128)S(1)}, u32[]{:S(2)}) copy-start(f32[128]{0:T(128)S(1)} %add_rsqrt_fusion) | copy-start | bytes 1540
  162.1 60.7 %all-to-all-start = ((bf16[16,128,1024]{1,2,0:T(8,128)(2,1)}), bf16[16,128,1024]{1,2,0:T(8,128)(2,1)}, u32[]{:S(2)}, u32[]{:S(2)}) async-start(bf16[16,128,1024]{1,2,0:T(8,128)(2,1)} %pad_maximum_fusion.1), calls=%async_computation | async-start | bytes 8388608 | tf_op jit(solution)/shard_map/all_to_all | solution.py:177
  167.5 211.1 %reduce-scatter.5.cloned.1.call-start = ((), (), s32[]{:S(2)}) async-start(), calls=%async_computation.4 | async-start | bytes 4491264
  185.7 9.8 %copy-start.23 = (bf16[1024,256]{1,0:T(8,128)(2,1)S(1)}, bf16[1024,256]{1,0:T(8,128)(2,1)}, u32[]{:S(2)}) copy-start(bf16[1024,256]{1,0:T(8,128)(2,1)} %reshape.245) | copy-start | bytes 1572868
  185.7 10.7 %copy-start.22 = (bf16[1024,256]{1,0:T(8,128)(2,1)S(1)}, bf16[1024,256]{1,0:T(8,128)(2,1)}, u32[]{:S(2)}) copy-start(bf16[1024,256]{1,0:T(8,128)(2,1)} %reshape.246) | copy-start | bytes 1572868
  185.7 11.6 %copy-start.20 = (bf16[2048,512]{0,1:T(8,128)(2,1)S(1)}, bf16[2048,512]{0,1:T(8,128)(2,1)}, u32[]{:S(2)}) copy-start(bf16[2048,512]{0,1:T(8,128)(2,1)} %copy.203) | copy-start | bytes 6291460
  232.5 12.5 %copy-start.34 = (f32[128]{0:T(128)}, f32[128]{0:T(128)S(1)}, u32[]{:S(2)}) copy-start(f32[128]{0:T(128)S(1)} %broadcast_multiply_fusion) | copy-start | bytes 1540
  268.3 34.4 %collective-permute-start.8 = (bf16[16,1,4,256]{3,1,0,2:T(2,128)(2,1)S(1)}, bf16[16,1,4,256]{3,1,0,2:T(2,128)(2,1)S(1)}, u32[]{:S(2)}, u32[]{:S(2)}) collective-permute-start(bf16[16,1,4,256]{3,1,0,2:T(2,128)(2,1)S(1)} %get-tuple-element.77), channel_id=1, source_target_pairs={{0,1},{1,2},{2,3},{4,5},{5,6},{6,7},{8,9},{9,10},{10,11},{12,13},{... | collective-permute-start | bytes 98312 | tf_op jit(solution)/shard_map/ppermute | solution.py:45
  272.4 25.3 %collective-permute-start.11 = (bf16[1,16,4,256]{3,2,1,0:T(4,128)(2,1)S(1)}, bf16[1,16,4,256]{3,2,1,0:T(4,128)(2,1)S(1)}, u32[]{:S(2)}, u32[]{:S(2)}) collective-permute-start(bf16[1,16,4,256]{3,2,1,0:T(4,128)(2,1)S(1)} %slice.220), channel_id=1, source_target_pairs={{4,0},{5,1},{6,2},{7,3},{8,4},{9,5},{10,6},{11,7},{12,8},{13,9},{1... | collective-permute-start | bytes 98312 | tf_op jit(solution)/shard_map/ppermute | solution.py:45
  274.9 16.7 %collective-permute-start.10 = (bf16[1,1,4,256]{3,2,1,0:T(4,128)(2,1)S(1)}, bf16[1,1,4,256]{3,2,1,0:T(4,128)(2,1)S(1)}, u32[]{:S(2)}, u32[]{:S(2)}) collective-permute-start(bf16[1,1,4,256]{3,2,1,0:T(4,128)(2,1)S(1)} %get-tuple-element.92), channel_id=1, source_target_pairs={{4,1},{5,2},{6,3},{8,5},{9,6},{10,7},{12,9},{13,10},{14,11},{20,17... | collective-permute-start | bytes 6152 | tf_op jit(solution)/shard_map/ppermute | solution.py:45
  276.2 16.8 %collective-permute-start.12 = (bf16[1,1,4,256]{3,2,1,0:T(4,128)(2,1)S(1)}, bf16[1,1,4,256]{3,2,1,0:T(4,128)(2,1)S(1)}, u32[]{:S(2)}, u32[]{:S(2)}) collective-permute-start(bf16[1,1,4,256]{3,2,1,0:T(4,128)(2,1)S(1)} %get-tuple-element.93), channel_id=1, source_target_pairs={{5,0},{6,1},{7,2},{9,4},{10,5},{11,6},{13,8},{14,9},{15,10},{21,16... | collective-permute-start | bytes 6152 | tf_op jit(solution)/shard_map/ppermute | solution.py:45
  277.5 9.5 %copy-start.1 = (f32[8,8,2,2,2,2,256]{6,5,4,3,2,1,0:T(2,128)S(1)}, f32[8,8,2,2,2,2,256]{6,5,4,3,2,1,0:T(2,128)}, u32[]{:S(2)}) copy-start(f32[8,8,2,2,2,2,256]{6,5,4,3,2,1,0:T(2,128)} %reshape.262) | copy-start | bytes 3145732
  277.6 25.1 %collective-permute-start.14 = (bf16[1,16,4,256]{3,2,1,0:T(4,128)(2,1)S(1)}, bf16[1,16,4,256]{3,2,1,0:T(4,128)(2,1)S(1)}, u32[]{:S(2)}, u32[]{:S(2)}) collective-permute-start(bf16[1,16,4,256]{3,2,1,0:T(4,128)(2,1)S(1)} %slice.229), channel_id=1, source_target_pairs={{0,4},{1,5},{2,6},{3,7},{4,8},{5,9},{6,10},{7,11},{8,12},{9,13},{1... | collective-permute-start | bytes 98312 | tf_op jit(solution)/shard_map/ppermute | solution.py:45
  291.6 14.9 %copy-start.6 = (bf16[16,16,4,256]{3,1,0,2:T(8,128)(2,1)S(1)}, bf16[16,16,4,256]{3,1,0,2:T(8,128)(2,1)}, u32[]{:S(2)}) copy-start(bf16[16,16,4,256]{3,1,0,2:T(8,128)(2,1)} %copy-done.5) | copy-start | bytes 1572868
  291.6 11.1 %collective-permute-start.9 = (bf16[16,1,4,256]{3,1,0,2:T(2,128)(2,1)S(1)}, bf16[16,1,4,256]{3,1,0,2:T(2,128)(2,1)S(1)}, u32[]{:S(2)}, u32[]{:S(2)}) collective-permute-start(bf16[16,1,4,256]{3,1,0,2:T(2,128)(2,1)S(1)} %get-tuple-element.78), channel_id=1, source_target_pairs={{1,0},{2,1},{3,2},{5,4},{6,5},{7,6},{9,8},{10,9},{11,10},{13,12},{... | collective-permute-start | bytes 98312 | tf_op jit(solution)/shard_map/ppermute | solution.py:45
  293.0 6.0 %collective-permute-start.13 = (bf16[1,1,4,256]{3,2,1,0:T(4,128)(2,1)S(1)}, bf16[1,1,4,256]{3,2,1,0:T(4,128)(2,1)S(1)}, u32[]{:S(2)}, u32[]{:S(2)}) collective-permute-start(bf16[1,1,4,256]{3,2,1,0:T(4,128)(2,1)S(1)} %get-tuple-element.90), channel_id=1, source_target_pairs={{0,5},{1,6},{2,7},{4,9},{5,10},{6,11},{8,13},{9,14},{10,15},{16,21... | collective-permute-start | bytes 6152 | tf_op jit(solution)/shard_map/ppermute | solution.py:45
  297.8 4.9 %collective-permute-start.15 = (bf16[1,1,4,256]{3,2,1,0:T(4,128)(2,1)S(1)}, bf16[1,1,4,256]{3,2,1,0:T(4,128)(2,1)S(1)}, u32[]{:S(2)}, u32[]{:S(2)}) collective-permute-start(bf16[1,1,4,256]{3,2,1,0:T(4,128)(2,1)S(1)} %get-tuple-element.91), channel_id=1, source_target_pairs={{1,4},{2,5},{3,6},{5,8},{6,9},{7,10},{9,12},{10,13},{11,14},{17,20... | collective-permute-start | bytes 6152 | tf_op jit(solution)/shard_map/ppermute | solution.py:45
  322.3 53.0 %all-to-all-start.1 = ((bf16[16,432,256]{2,1,0:T(8,128)(2,1)}), bf16[16,432,256]{2,1,0:T(8,128)(2,1)}, u32[]{:S(2)}, u32[]{:S(2)}) async-start(bf16[16,432,256]{2,1,0:T(8,128)(2,1)} %bitcast.160), calls=%async_computation.1 | async-start | bytes 7077888 | tf_op jit(solution)/shard_map/all_to_all | solution.py:270
  341.5 8.0 %copy-start.3 = (bf16[17,18,4,256]{3,1,0,2:T(8,128)(2,1)S(1)}, bf16[17,18,4,256]{3,1,0,2:T(8,128)(2,1)}, u32[]{:S(2)}) copy-start(bf16[17,18,4,256]{3,1,0,2:T(8,128)(2,1)} %get-tuple-element.61) | copy-start | bytes 1880068
  (27 other events, 78.8 us)
Sparse Core Ops, SparseCore 0:
  73.2 56.0 all-gather.1
  249.7 73.6 reduce-scatter.4

commit v6 on v2

--- a/solution.py
+++ b/solution.py
@@ -203,15 +203,6 @@
     )
     d_columns = plane_columns(d_padded, extent_x, extent_y, True)
     weight_bwd = taps.transpose(0, 3, 1, 2).reshape(9 * channels, 3 * channels)
-    grad_features = depth_sum(
-        jnp.dot(d_columns, weight_bwd, preferred_element_type=jnp.float32),
-        extent_z,
-        channels,
-        True,
-    )
-    grad_features = grad_features.reshape(extent_x, extent_y, extent_z, channels).astype(
-        jnp.bfloat16
-    )
     groups = lax.axis_size(("gx", "gy"))
     gain_rows = gain_part.reshape(groups, -1)
     gain_high = gain_rows.astype(jnp.bfloat16)
@@ -246,6 +237,18 @@
     gain_flat = results[3].reshape(-1).astype(jnp.float32)
     half = gain_high.shape[1]
     gain_sum = gain_flat[:half] + gain_flat[half : 2 * half]
+    d_columns, down_sum, qkv_sum, out_sum, gain_sum = lax.optimization_barrier(
+        (d_columns, down_sum, qkv_sum, out_sum, gain_sum)
+    )
+    grad_features = depth_sum(
+        jnp.dot(d_columns, weight_bwd, preferred_element_type=jnp.float32),
+        extent_z,
+        channels,
+        True,
+    )
+    grad_features = grad_features.reshape(extent_x, extent_y, extent_z, channels).astype(
+        jnp.bfloat16
+    )
     return (
         grad_features,
         conv_sum.astype(jnp.bfloat16),

time: 383 us -> 438 us (1.14)
  the two profiles are of different devices: /device:TPU:1 before, /device:TPU:5 now
where the time goes in v6:
time: 438 us; the launch traced here: 430 us
  local copies, waits for them, and re-layouts  187 us (43%)
  waiting for transfers between devices  89.6 us (20%)
  matrix products  69.1 us (16%)
  starting transfers between devices  35.7 us (8%)
  other arithmetic  32.8 us (7%)
  between operations  15.3 us (3%)
    all_gather x1, waiting for transfers between devices, local(): lax.all_gather(qkv_rows[:, model_width:], ('gx', 'gy'), axis=0, tiled=True)  47 us
    unnamed x124, local copies, waits for them, and re-layouts  37.3 us
    all_to_all x1, waiting for transfers between devices, local(): key_parts = lax.all_to_all(key_parts, ('gx', 'gy'), 0, 0, tiled=True)  31.1 us
    reshape x17, local copies, waits for them, and re-layouts, plane_columns(): padded[start_x:start_x + extent_x, start_y:start_y + extent_y]  29.6 us
    convert_element_type x7, local copies, waits for them, and re-layouts, local(): d_act_grid = from_tokens(d_activation, extent_x, extent_y, extent_z).resh...  20.3 us
    dot_general x2, local copies, waits for them, and re-layouts, local(): jnp.dot(d_columns, weight_bwd, preferred_element_type=jnp.float32)  14.6 us
    ppermute x4, starting transfers between devices, padded_2(): lax.ppermute(lax.slice_in_dim(block, block.shape[dim] - width, None, axis...  14.3 us
    slice x18, local copies, waits for them, and re-layouts, plane_columns(): padded[start_x:start_x + extent_x, start_y:start_y + extent_y]  13.4 us
  transfers between devices with their start and end apart: 12, of which 5 were waited for; matrix products, arithmetic and copies ran while one was open for 42% of the time, Pallas kernels for 0%

profile of v6, /device:TPU:5, one launch (start us, length us, event | category | flops | bytes accessed | tf_op | source)
XLA Modules:
  0.0 429.9 jit_solution(4958516997286903308)
XLA Ops:
  8.2 3.9 collective-permute-start
  14.1 3.3 collective-permute-done.1
  33.0 6.3 %copy.203 = bf16[768,2304]{1,0:T(8,128)(2,1)} copy(bf16[768,2304]{0,1:T(8,128)(2,1)} %bitcast.154) | data formatting | bytes 7077888 | tf_op jit(solution)/shard_map/dot_general | solution.py:74
  39.5 3.7 pad_maximum_fusion.6
  46.5 3.8 fusion.8
  70.2 47.0 %all-gather.2.cloned.1.call-done = bf16[2048,1024]{1,0:T(8,128)(2,1)} async-done(((bf16[128,1024]{1,0:T(8,128)(2,1)}), bf16[2048,1024]{1,0:T(8,128)(2,1)}) %all-gather.2.cloned.1.call-update) | async-done | bytes 4194320 | tf_op jit(solution)/shard_map/all_gather | solution.py:95
  117.2 4.5 %fusion.51 = (bf16[2048,512]{1,0:T(8,128)(2,1)}, bf16[2048,512]{1,0:T(8,128)(2,1)}) fusion(bf16[2048,1024]{1,0:T(8,128)(2,1)} %all-gather.2.cloned.1.call-done), kind=kLoop, calls=%fused_computation.128 | loop fusion | bytes 8388608 | tf_op jit(solution)/shard_map/slice | solution.py:99
  121.7 4.0 copy.209
  125.7 4.0 copy.212
  129.7 3.2 fusion.3
  139.0 5.9 %multiply_convert_fusion = bf16[8,64,2048]{2,1,0:T(8,128)(2,1)S(1)} fusion(bf16[128,8,64]{0,2,1:T(8,128)(2,1)S(1)} %bitcast.184, bf16[8,128,2048]{2,1,0:T(8,128)(2,1)S(1)} %get-tuple-element.100, f32[8,128]{1,0:T(8,128)S(1)} %get-tuple-element.99, f32[8,128,2048]{2,1,0:T(8,128)S(1)} %get-tuple-element.98, f32[8,128]{1,0:T(8,128)S(1)} %get-tuple-element.97), kind=kOutput, calls=%fused_computation.15 | convolution fusion | flops 1623195648 | bytes 14819328 | tf_op jit(solution)/shard_map/hij,ihe->jhe/dot_general | solution.py:131
  149.6 5.6 %all-to-all-start = ((bf16[16,128,1024]{1,2,0:T(8,128)(2,1)}), bf16[16,128,1024]{1,2,0:T(8,128)(2,1)}, u32[]{:S(2)}, u32[]{:S(2)}) async-start(bf16[16,128,1024]{1,2,0:T(8,128)(2,1)} %pad_maximum_fusion.1), calls=%async_computation | async-start | bytes 8388608 | tf_op jit(solution)/shard_map/all_to_all | solution.py:149
  155.2 5.7 %fusion.23 = bf16[8,64,128]{2,1,0:T(8,128)(2,1)S(1)} fusion(bf16[2048,8,64]{0,2,1:T(8,128)(2,1)} %bitcast.166, f32[8,128,2048]{2,1,0:T(8,128)} %copy-done.3, f32[8,128]{1,0:T(8,128)S(1)} %get-tuple-element.97), kind=kOutput, calls=%fused_computation.34 | convolution fusion | flops 274792448 | bytes 10620928 | tf_op jit(solution)/shard_map/hij,jhe->ihe/dot_general | solution.py:111
  164.2 12.6 %fusion.26 = bf16[8,64,128]{2,1,0:T(8,128)(2,1)} fusion(bf16[2048,8,64]{0,2,1:T(8,128)(2,1)} %bitcast.159, bf16[8,128,2048]{2,1,0:T(8,128)(2,1)} %copy-done.41, f32[8,128]{1,0:T(8,128)} %copy-done.42, f32[8,128,2048]{2,1,0:T(8,128)} %copy-done.3, f32[8,128]{1,0:T(8,128)S(1)} %get-tuple-element.97), kind=kOutput, calls=%fused_computation.36 | convolution fusion | flops 1621229568 | bytes 14819328 | tf_op jit(solution)/shard_map/hij,jhe->ihe/dot_general | solution.py:125
  176.7 31.1 %all-to-all-done = bf16[16,128,1024]{1,2,0:T(8,128)(2,1)} async-done(((bf16[16,128,1024]{1,2,0:T(8,128)(2,1)}), bf16[16,128,1024]{1,2,0:T(8,128)(2,1)}, u32[]{:S(2)}, u32[]{:S(2)}) %all-to-all-start) | async-done | bytes 4194336 | tf_op jit(solution)/shard_map/all_to_all | solution.py:149
  207.8 3.5 reduce.2
  217.8 3.3 convolution_convert_fusion.4
  221.1 4.3 %reshape.243 = bf16[16,512,128]{2,1,0:T(8,128)(2,1)} reshape(bf16[2048,512]{1,0:T(8,128)(2,1)} %convolution_convert_fusion.4) | data formatting | bytes 4194304 | tf_op jit(solution)/shard_map/reshape | solution.py:218
  225.4 4.3 reshape.244
  230.6 4.2 pad_maximum_fusion
  267.9 3.2 reshape.268
  293.1 4.1 convolution_convert_fusion.2
  302.5 7.6 %all-to-all-start.1 = ((bf16[16,432,256]{2,1,0:T(8,128)(2,1)}), bf16[16,432,256]{2,1,0:T(8,128)(2,1)}, u32[]{:S(2)}, u32[]{:S(2)}) async-start(bf16[16,432,256]{2,1,0:T(8,128)(2,1)} %bitcast.153), calls=%async_computation.1 | async-start | bytes 7077888 | tf_op jit(solution)/shard_map/all_to_all | solution.py:233
  310.1 8.0 %copy.231 = bf16[9,3,256,256]{2,1,3,0:T(4,128)(2,1)} copy(bf16[9,3,256,256]{3,2,1,0:T(8,128)(2,1)} %bitcast.156) | data formatting | bytes 7077888 | tf_op jit(solution)/shard_map/reshape | solution.py:69
  318.1 5.2 %copy.260 = bf16[288,8,3,256]{3,1,2,0:T(8,128)(2,1)} copy(bf16[288,8,3,256]{3,2,1,0:T(4,128)(2,1)} %bitcast.149) | data formatting | bytes 7077888
  323.2 5.8 %copy.232 = bf16[768,2304]{1,0:T(8,128)(2,1)} copy(bf16[768,2304]{0,1:T(8,128)(2,1)} %bitcast.155) | data formatting | bytes 7077888 | tf_op jit(solution)/shard_map/dot_general | solution.py:244
  335.6 3.4 collective-permute-start.4
  342.6 6.2 %collective-permute-done.4 = bf16[1,16,4,256]{3,1,2,0:T(8,128)(2,1)S(1)} collective-permute-done((bf16[1,16,4,256]{3,1,2,0:T(8,128)(2,1)S(1)}, bf16[1,16,4,256]{3,1,2,0:T(8,128)(2,1)S(1)}, u32[]{:S(2)}, u32[]{:S(2)}) %collective-permute-start.4) | collective-permute-done | bytes 32800 | tf_op jit(solution)/shard_map/ppermute | solution.py:18
  353.4 4.2 collective-permute-start.7
  396.4 3.3 reduce_sum.92
  405.7 8.8 %dot_general.84 = bf16[256,4,2304]{2,1,0:T(4,128)(2,1)} reshape(bf16[1024,2304]{1,0:T(8,128)(2,1)} %constant_dynamic-update-slice_fusion.12) | data formatting | bytes 9437184 | tf_op jit(solution)/shard_map/dot_general | solution.py:244
  414.4 6.8 %fusion.10 = f32[256,4,3,256]{3,0,2,1:T(8,128)S(1)} fusion(bf16[3,256,2304,1]{2,1,0,3:T(8,128)(2,1)} %bitcast.164, bf16[256,4,2304,1]{2,1,0,3:T(4,128)(2,1)} %bitcast.162), kind=kOutput, calls=%fused_computation.11 | convolution fusion | flops 3623878656 | bytes 11403264 | tf_op jit(solution)/shard_map/dot_general | solution.py:244
  (252 shorter events, 183.9 us)
Async XLA Ops:
  7.2 50.0 %copy-start = (bf16[2048,512]{1,0:T(8,128)(2,1)S(1)}, bf16[2048,512]{1,0:T(8,128)(2,1)}, u32[]{:S(2)}) copy-start(bf16[2048,512]{1,0:T(8,128)(2,1)} %param.9) | copy-start | bytes 6291460
  7.2 110.0 %all-gather.2.cloned.1.call-start = ((), (), s32[]{:S(2)}) async-start(), calls=%async_computation.3 | async-start | bytes 4456448 | tf_op jit(solution)/shard_map/all_gather | solution.py:95
  7.2 19.9 %copy-start.1 = (bf16[6912,256]{1,0:T(8,128)(2,1)S(1)}, bf16[6912,256]{1,0:T(8,128)(2,1)}, u32[]{:S(2)}) copy-start(bf16[6912,256]{1,0:T(8,128)(2,1)} %param.8) | copy-start | bytes 10616836
  8.2 5.8 %collective-permute-start = (bf16[1,16,4,256]{3,2,1,0:T(4,128)(2,1)S(1)}, bf16[1,16,4,256]{3,2,1,0:T(4,128)(2,1)S(1)}, u32[]{:S(2)}, u32[]{:S(2)}) collective-permute-start(bf16[1,16,4,256]{3,2,1,0:T(4,128)(2,1)S(1)} %get-tuple-element.94), channel_id=1, source_target_pairs={{0,4},{4,8},{8,12},{1,5},{5,9},{9,13},{2,6},{6,10},{10,14},{3,7},{... | collective-permute-start | bytes 98312 | tf_op jit(solution)/shard_map/ppermute | solution.py:18
  12.1 5.2 %collective-permute-start.1 = (bf16[1,16,4,256]{3,2,1,0:T(4,128)(2,1)S(1)}, bf16[1,16,4,256]{3,2,1,0:T(4,128)(2,1)S(1)}, u32[]{:S(2)}, u32[]{:S(2)}) collective-permute-start(bf16[1,16,4,256]{3,2,1,0:T(4,128)(2,1)S(1)} %get-tuple-element.93), channel_id=1, source_target_pairs={{4,0},{8,4},{12,8},{5,1},{9,5},{13,9},{6,2},{10,6},{14,10},{7,3},{... | collective-permute-start | bytes 98312 | tf_op jit(solution)/shard_map/ppermute | solution.py:21
  19.9 19.4 %copy-start.6 = (bf16[16,16,4,256]{3,2,1,0:T(4,128)(2,1)}, bf16[16,16,4,256]{3,2,1,0:T(4,128)(2,1)S(1)}, u32[]{:S(2)}) copy-start(bf16[16,16,4,256]{3,2,1,0:T(4,128)(2,1)S(1)} %get-tuple-element.92) | copy-start | bytes 1572868
  19.9 19.5 %copy-start.5 = (bf16[16,16,4,256]{3,2,1,0:T(4,128)(2,1)}, bf16[16,16,4,256]{3,2,1,0:T(4,128)(2,1)S(1)}, u32[]{:S(2)}) copy-start(bf16[16,16,4,256]{3,2,1,0:T(4,128)(2,1)S(1)} %get-tuple-element.90) | copy-start | bytes 1572868
  19.9 10.3 %copy-start.28 = (bf16[18,16,4,256]{3,2,1,0:T(4,128)(2,1)}, bf16[18,16,4,256]{3,2,1,0:T(4,128)(2,1)S(1)}, u32[]{:S(2)}) copy-start(bf16[18,16,4,256]{3,2,1,0:T(4,128)(2,1)S(1)} %constant_dynamic-update-slice_fusion) | copy-start | bytes 1769476
  20.0 19.5 %collective-permute-start.2 = (bf16[18,1,4,256]{3,2,1,0:T(4,128)(2,1)S(1)}, bf16[18,1,4,256]{3,2,1,0:T(4,128)(2,1)S(1)}, u32[]{:S(2)}, u32[]{:S(2)}) collective-permute-start(bf16[18,1,4,256]{3,2,1,0:T(4,128)(2,1)S(1)} %get-tuple-element.83), channel_id=1, source_target_pairs={{0,1},{1,2},{2,3},{4,5},{5,6},{6,7},{8,9},{9,10},{10,11},{12,13},{... | collective-permute-start | bytes 110600 | tf_op jit(solution)/shard_map/ppermute | solution.py:18
  22.8 16.7 %collective-permute-start.3 = (bf16[18,1,4,256]{3,2,1,0:T(4,128)(2,1)S(1)}, bf16[18,1,4,256]{3,2,1,0:T(4,128)(2,1)S(1)}, u32[]{:S(2)}, u32[]{:S(2)}) collective-permute-start(bf16[18,1,4,256]{3,2,1,0:T(4,128)(2,1)S(1)} %get-tuple-element.82), channel_id=1, source_target_pairs={{1,0},{2,1},{3,2},{5,4},{6,5},{7,6},{9,8},{10,9},{11,10},{13,12},{... | collective-permute-start | bytes 110600 | tf_op jit(solution)/shard_map/ppermute | solution.py:21
  50.6 8.3 %copy-start.34 = (f32[512]{0:T(512)S(1)}, f32[512]{0:T(512)}, u32[]{:S(2)}) copy-start(f32[512]{0:T(512)} %param.10) | copy-start | bytes 6148
  59.0 158.3 %copy-start.35 = (f32[128]{0:T(128)}, f32[128]{0:T(128)S(1)}, u32[]{:S(2)}) copy-start(f32[128]{0:T(128)S(1)} %add_rsqrt_fusion) | copy-start | bytes 1540
  149.6 58.3 %all-to-all-start = ((bf16[16,128,1024]{1,2,0:T(8,128)(2,1)}), bf16[16,128,1024]{1,2,0:T(8,128)(2,1)}, u32[]{:S(2)}, u32[]{:S(2)}) async-start(bf16[16,128,1024]{1,2,0:T(8,128)(2,1)} %pad_maximum_fusion.1), calls=%async_computation | async-start | bytes 8388608 | tf_op jit(solution)/shard_map/all_to_all | solution.py:149
  155.1 244.5 %reduce-scatter.5.cloned.1.call-start = ((), (), s32[]{:S(2)}) async-start(), calls=%async_computation.4 | async-start | bytes 4491264
  211.4 6.4 %copy-start.4 = (bf16[128,2048]{1,0:T(8,128)(2,1)S(1)}, bf16[128,2048]{1,0:T(8,128)(2,1)}, u32[]{:S(2)}) copy-start(bf16[128,2048]{1,0:T(8,128)(2,1)} %reshape.228) | copy-start | bytes 1572868
  217.3 12.5 %copy-start.37 = (f32[128]{0:T(128)}, f32[128]{0:T(128)S(1)}, u32[]{:S(2)}) copy-start(f32[128]{0:T(128)S(1)} %get-tuple-element.102) | copy-start | bytes 1540
  256.7 8.0 %copy-start.27 = (f32[128,512]{1,0:T(8,128)S(1)}, f32[128,512]{1,0:T(8,128)}, u32[]{:S(2)}) copy-start(f32[128,512]{1,0:T(8,128)} %copy-done.26) | copy-start | bytes 786436
  256.7 8.0 %copy-start.36 = (f32[128]{0:T(128)S(1)}, f32[128]{0:T(128)}, u32[]{:S(2)}) copy-start(f32[128]{0:T(128)} %copy-done.35) | copy-start | bytes 1540
  256.8 8.0 %copy-start.38 = (f32[128]{0:T(128)S(1)}, f32[128]{0:T(128)}, u32[]{:S(2)}) copy-start(f32[128]{0:T(128)} %copy-done.37) | copy-start | bytes 1540
  256.8 8.0 %copy-start.40 = (f32[128]{0:T(128)S(1)}, f32[128]{0:T(128)}, u32[]{:S(2)}) copy-start(f32[128]{0:T(128)} %copy-done.39) | copy-start | bytes 1540
  291.0 6.2 %slice-start = ((s8[4718592]{0:T(1024)(128)(4,1)}), s8[4194304]{0:T(1024)(128)(4,1)S(1)}, s32[]{:S(2)}) async-start(s8[4718592]{0:T(1024)(128)(4,1)} %bitcast.191), calls=%async_computation.5 | async-start | bytes 8388608
  302.5 93.9 %all-to-all-start.1 = ((bf16[16,432,256]{2,1,0:T(8,128)(2,1)}), bf16[16,432,256]{2,1,0:T(8,128)(2,1)}, u32[]{:S(2)}, u32[]{:S(2)}) async-start(bf16[16,432,256]{2,1,0:T(8,128)(2,1)} %bitcast.153), calls=%async_computation.1 | async-start | bytes 7077888 | tf_op jit(solution)/shard_map/all_to_all | solution.py:233
  335.6 13.2 %collective-permute-start.4 = (bf16[1,16,4,256]{3,1,2,0:T(8,128)(2,1)S(1)}, bf16[1,16,4,256]{3,1,2,0:T(8,128)(2,1)S(1)}, u32[]{:S(2)}, u32[]{:S(2)}) collective-permute-start(bf16[1,16,4,256]{3,1,2,0:T(8,128)(2,1)S(1)} %copy.218), channel_id=1, source_target_pairs={{0,4},{4,8},{8,12},{1,5},{5,9},{9,13},{2,6},{6,10},{10,14},{3,7},{... | collective-permute-start | bytes 98312 | tf_op jit(solution)/shard_map/ppermute | solution.py:18
  339.0 11.7 %collective-permute-start.5 = (bf16[1,16,4,256]{3,1,2,0:T(8,128)(2,1)S(1)}, bf16[1,16,4,256]{3,1,2,0:T(8,128)(2,1)S(1)}, u32[]{:S(2)}, u32[]{:S(2)}) collective-permute-start(bf16[1,16,4,256]{3,1,2,0:T(8,128)(2,1)S(1)} %copy.222), channel_id=1, source_target_pairs={{4,0},{8,4},{12,8},{5,1},{9,5},{13,9},{6,2},{10,6},{14,10},{7,3},{... | collective-permute-start | bytes 98312 | tf_op jit(solution)/shard_map/ppermute | solution.py:21
  342.5 15.0 %copy-start.2 = (bf16[16,16,4,256]{3,1,2,0:T(8,128)(2,1)}, bf16[16,16,4,256]{3,1,2,0:T(8,128)(2,1)S(1)}, u32[]{:S(2)}) copy-start(bf16[16,16,4,256]{3,1,2,0:T(8,128)(2,1)S(1)} %multiply_convert_fusion.2) | copy-start | bytes 1572868
  350.7 8.2 %copy-start.31 = (bf16[1,16,4,256]{3,1,2,0:T(8,128)(2,1)}, bf16[1,16,4,256]{3,1,2,0:T(8,128)(2,1)S(1)}, u32[]{:S(2)}) copy-start(bf16[1,16,4,256]{3,1,2,0:T(8,128)(2,1)S(1)} %collective-permute-done.5) | copy-start | bytes 98308
  351.5 9.6 %collective-permute-start.6 = (bf16[18,1,4,256]{3,1,2,0:T(2,128)(2,1)}, bf16[18,1,4,256]{3,1,2,0:T(2,128)(2,1)}, u32[]{:S(2)}, u32[]{:S(2)}) collective-permute-start(bf16[18,1,4,256]{3,1,2,0:T(2,128)(2,1)} %get-tuple-element.78), channel_id=1, source_target_pairs={{1,0},{2,1},{3,2},{5,4},{6,5},{7,6},{9,8},{10,9},{11,10},{13,12},{... | collective-permute-start | bytes 110600 | tf_op jit(solution)/shard_map/ppermute | solution.py:21
  353.4 7.7 %collective-permute-start.7 = (bf16[18,1,4,256]{3,1,2,0:T(2,128)(2,1)}, bf16[18,1,4,256]{3,1,2,0:T(2,128)(2,1)}, u32[]{:S(2)}, u32[]{:S(2)}) collective-permute-start(bf16[18,1,4,256]{3,1,2,0:T(2,128)(2,1)} %get-tuple-element.77), channel_id=1, source_target_pairs={{0,1},{1,2},{2,3},{4,5},{5,6},{6,7},{8,9},{9,10},{10,11},{12,13},{... | collective-permute-start | bytes 110600 | tf_op jit(solution)/shard_map/ppermute | solution.py:18
  374.0 18.0 %copy-start.15 = (bf16[1024,256]{1,0:T(8,128)(2,1)S(1)}, bf16[1024,256]{1,0:T(8,128)(2,1)}, u32[]{:S(2)}) copy-start(bf16[1024,256]{1,0:T(8,128)(2,1)} %copy-done.14) | copy-start | bytes 1572868
  384.2 8.7 %copy-start.20 = (bf16[1024,256]{1,0:T(8,128)(2,1)S(1)}, bf16[1024,256]{1,0:T(8,128)(2,1)}, u32[]{:S(2)}) copy-start(bf16[1024,256]{1,0:T(8,128)(2,1)} %reshape.239) | copy-start | bytes 1572868
  384.2 9.5 %copy-start.23 = (bf16[1024,256]{1,0:T(8,128)(2,1)S(1)}, bf16[1024,256]{1,0:T(8,128)(2,1)}, u32[]{:S(2)}) copy-start(bf16[1024,256]{1,0:T(8,128)(2,1)} %reshape.240) | copy-start | bytes 1572868
  384.2 11.3 %copy-start.21 = (bf16[1024,256]{1,0:T(8,128)(2,1)S(1)}, bf16[1024,256]{1,0:T(8,128)(2,1)}, u32[]{:S(2)}) copy-start(bf16[1024,256]{1,0:T(8,128)(2,1)} %reshape.242) | copy-start | bytes 1572868
  (25 other events, 82.4 us)
Sparse Core Ops, SparseCore 0:
  62.5 54.6 all-gather.1
  234.9 75.0 reduce-scatter.4

commit v7 on v2

--- a/solution.py
+++ b/solution.py
@@ -123,7 +123,7 @@
     d_scores = attn_probs * (d_probs - row_delta[:, :, None])
     d_queries = (
         jnp.einsum(
-            "hij,jhe->ihe", d_scores, keys_h, precision=precise, preferred_element_type=jnp.float32
+            "hij,jhe->ihe", d_scores, keys_h, preferred_element_type=jnp.float32
         )
         * score_scale
     )
@@ -132,7 +132,6 @@
             "hij,ihe->jhe",
             d_scores,
             queries_h,
-            precision=precise,
             preferred_element_type=jnp.float32,
         )
         * score_scale
@@ -169,10 +168,10 @@
         - normed * jnp.mean(d_hat * normed, axis=-1, keepdims=True)
     )
     down_part = jnp.einsum(
-        "tr,td->rd", tokens_in, d_trunk, precision=precise, preferred_element_type=jnp.float32
+        "tr,td->rd", tokens_in, d_trunk, preferred_element_type=jnp.float32
     )
     d_activation = jnp.dot(
-        d_trunk, down_weight.T, precision=precise, preferred_element_type=jnp.float32
+        d_trunk, down_weight.T, preferred_element_type=jnp.float32
     ).astype(jnp.bfloat16)
     d_act_grid = (
         from_tokens(d_activation, extent_x, extent_y, extent_z)

time: 383 us -> 376 us (0.982)
  matrix products: 75.5 us -> 65.5 us
  waiting for transfers between devices: 67.2 us -> 71.1 us
    dot_general x4, matrix products: 25.9 us -> 16.3 us  [the longest x1 8.35 us: local(): jnp.einsum('hij,jhe->ihe', d_scores, keys_h, preferred_element_type=jnp.f...]
    all_to_all x1, waiting for transfers between devices: 0.73 us -> 4.95 us  [local(): key_parts = lax.all_to_all(key_parts, ('gx', 'gy'), 0, 0, tiled=True)]
  transfers between devices with their start and end apart: 12 -> 12, of which waited for: 5 -> 5; matrix products, arithmetic and copies ran while one was open for 44% -> 43% of each run, Pallas kernels for 0% -> 0%
where the time goes in v7:
time: 376 us; the launch traced here: 369 us
  local copies, waits for them, and re-layouts  151 us (40%)
  waiting for transfers between devices  71.1 us (19%)
  matrix products  65.5 us (17%)
  other arithmetic  33.5 us (9%)
  starting transfers between devices  32.7 us (9%)
  between operations  15.3 us (4%)
    all_gather x1, waiting for transfers between devices, local(): lax.all_gather(qkv_rows[:, model_width:], ('gx', 'gy'), axis=0, tiled=True)  47.9 us
    unnamed x111, local copies, waits for them, and re-layouts  37.9 us
    reshape x9, local copies, waits for them, and re-layouts, plane_columns(): padded[start_x:start_x + extent_x, start_y:start_y + extent_y]  17.7 us
    convert_element_type x6, local copies, waits for them, and re-layouts, local(): d_act_grid = from_tokens(d_activation, extent_x, extent_y, extent_z).resh...  16.5 us
    ppermute x4, starting transfers between devices, padded_2(): lax.ppermute(lax.slice_in_dim(block, block.shape[dim] - width, None, axis...  14.9 us
    all_to_all x1, waiting for transfers between devices, local(): conv_rows = lax.all_to_all(conv_part, ('gx', 'gy'), 0, 0, tiled=True)  14.1 us
    dot_general x3, matrix products, local(): jnp.einsum('vr,vc->rc', columns, shifted.reshape(voxels, channels), prefe...  12.9 us
    concatenate x5, other arithmetic, padded_2(): block = jnp.concatenate([low, block, high], axis=dim)  11.6 us
  transfers between devices with their start and end apart: 12, of which 5 were waited for; matrix products, arithmetic and copies ran while one was open for 43% of the time, Pallas kernels for 0%

profile of v7, /device:TPU:1, one launch (start us, length us, event | category | flops | bytes accessed | tf_op | source)
XLA Modules:
  0.0 368.9 jit_solution(12876079405221461084)
XLA Ops:
  8.2 4.7 %collective-permute-start = (bf16[1,16,4,256]{3,2,1,0:T(4,128)(2,1)S(1)}, bf16[1,16,4,256]{3,2,1,0:T(4,128)(2,1)S(1)}, u32[]{:S(2)}, u32[]{:S(2)}) collective-permute-start(bf16[1,16,4,256]{3,2,1,0:T(4,128)(2,1)S(1)} %get-tuple-element.86), channel_id=1, source_target_pairs={{0,4},{4,8},{8,12},{1,5},{5,9},{9,13},{2,6},{6,10},{10,14},{3,7},{... | collective-permute-start | bytes 98312 | tf_op jit(solution)/shard_map/ppermute | solution.py:18
  14.9 3.3 collective-permute-done.1
  21.1 3.1 collective-permute-start.2
  33.3 6.3 %copy.202 = bf16[768,2304]{1,0:T(8,128)(2,1)} copy(bf16[768,2304]{0,1:T(8,128)(2,1)} %bitcast.161) | data formatting | bytes 7077888 | tf_op jit(solution)/shard_map/dot_general | solution.py:74
  39.8 3.7 %pad_maximum_fusion.6 = (bf16[16,16,4,256]{3,2,1,0:T(4,128)(2,1)S(1)}, bf16[16,16,4,256]{3,2,1,0:T(4,128)(2,1)S(1)}, bf16[16,16,4,256]{3,2,1,0:T(4,128)(2,1)S(1)...) fusion(bf16[18,1,4,256]{3,2,1,0:T(4,128)(2,1)S(1)} %collective-, ...), kind=kLoop, calls=%fused_computation.69 | loop fusion | flops 1572864 | bytes 3809280 | tf_op jit(solution)/shard_map/concatenate | solution.py:22
  46.8 3.8 %fusion.10 = f32[256,4,3,256]{3,0,2,1:T(8,128)S(1)} fusion(bf16[3,256,2304,1]{2,1,0,3:T(8,128)(2,1)S(1)} %bitcast.172, bf16[256,4,2304]{2,0,1:T(8,128)(2,1)S(1)} %constant_dynamic-update-slice_fusion.3), kind=kOutput, calls=%fused_computation.11 | convolution fusion | flops 3623878656 | bytes 11403264 | tf_op jit(solution)/shard_map/dot_general | solution.py:74
  70.5 47.9 %all-gather.2.cloned.1.call-done = bf16[2048,1024]{1,0:T(8,128)(2,1)} async-done(((bf16[128,1024]{1,0:T(8,128)(2,1)}), bf16[2048,1024]{1,0:T(8,128)(2,1)}) %all-gather.2.cloned.1.call-update) | async-done | bytes 4194320 | tf_op jit(solution)/shard_map/all_gather | solution.py:95
  118.4 4.5 %fusion.53 = (bf16[2048,512]{1,0:T(8,128)(2,1)}, bf16[2048,512]{1,0:T(8,128)(2,1)}) fusion(bf16[2048,1024]{1,0:T(8,128)(2,1)} %all-gather.2.cloned.1.call-done), kind=kLoop, calls=%fused_computation.130 | loop fusion | bytes 8388608 | tf_op jit(solution)/shard_map/slice | solution.py:99
  122.9 3.9 %copy.208 = bf16[2048,512]{0,1:T(8,128)(2,1)} copy(bf16[2048,512]{1,0:T(8,128)(2,1)} %get-tuple-element.50) | data formatting | bytes 4194304 | tf_op jit(solution)/shard_map/slice | solution.py:98
  126.9 4.0 %copy.211 = bf16[2048,512]{0,1:T(8,128)(2,1)} copy(bf16[2048,512]{1,0:T(8,128)(2,1)} %get-tuple-element.49) | data formatting | bytes 4194304 | tf_op jit(solution)/shard_map/slice | solution.py:99
  130.8 3.2 fusion.3
  147.9 5.4 %all-to-all-start = ((bf16[16,128,1024]{1,2,0:T(8,128)(2,1)}), bf16[16,128,1024]{1,2,0:T(8,128)(2,1)}, u32[]{:S(2)}, u32[]{:S(2)}) async-start(bf16[16,128,1024]{1,2,0:T(8,128)(2,1)} %pad_maximum_fusion.1), calls=%async_computation | async-start | bytes 8388608 | tf_op jit(solution)/shard_map/all_to_all | solution.py:148
  187.0 5.2 %fusion.23 = bf16[8,64,128]{2,1,0:T(8,128)(2,1)S(1)} fusion(bf16[2048,8,64]{0,2,1:T(8,128)(2,1)S(1)} %bitcast.177, f32[8,128,2048]{2,1,0:T(8,128)} %copy-done.3, f32[8,128]{1,0:T(8,128)S(1)} %get-tuple-element.89), kind=kOutput, calls=%fused_computation.34 | convolution fusion | flops 274792448 | bytes 10620928 | tf_op jit(solution)/shard_map/hij,jhe->ihe/dot_general | solution.py:111
  195.4 8.3 %fusion.26 = bf16[8,64,128]{2,1,0:T(8,128)(2,1)} fusion(bf16[2048,8,64]{0,2,1:T(8,128)(2,1)} %bitcast.169, bf16[8,128,2048]{2,1,0:T(8,128)(2,1)} %copy-done.37, f32[8,128]{1,0:T(8,128)} %copy-done.38, f32[8,128,2048]{2,1,0:T(8,128)} %copy-done.3, f32[8,128]{1,0:T(8,128)S(1)} %get-tuple-element.89), kind=kOutput, calls=%fused_computation.36 | convolution fusion | flops 279052288 | bytes 14819328 | tf_op jit(solution)/shard_map/hij,jhe->ihe/dot_general | solution.py:125
  203.7 4.9 %all-to-all-done = bf16[16,128,1024]{1,2,0:T(8,128)(2,1)} async-done(((bf16[16,128,1024]{1,2,0:T(8,128)(2,1)}), bf16[16,128,1024]{1,2,0:T(8,128)(2,1)}, u32[]{:S(2)}, u32[]{:S(2)}) %all-to-all-start) | async-done | bytes 4194336 | tf_op jit(solution)/shard_map/all_to_all | solution.py:148
  208.7 3.5 reduce.2
  220.8 4.6 %reshape.249 = bf16[16,512,128]{2,1,0:T(8,128)(2,1)} reshape(bf16[2048,512]{1,0:T(8,128)(2,1)} %convolution_convert_fusion.4) | data formatting | bytes 4194304 | tf_op jit(solution)/shard_map/reshape | solution.py:226
  225.4 4.3 %reshape.250 = bf16[16,384,128]{2,1,0:T(8,128)(2,1)} reshape(bf16[512,1536]{1,0:T(8,128)(2,1)} %convolution_convert_fusion.5) | data formatting | bytes 3145728 | tf_op jit(solution)/shard_map/reshape | solution.py:226
  230.5 3.7 pad_maximum_fusion
  240.9 3.1 reshape.262
  246.7 3.2 reshape.259
  260.5 5.0 %convolution_convert_fusion.1 = bf16[2304,256]{1,0:T(8,128)(2,1)} fusion(bf16[1024,2304]{1,0:T(8,128)(2,1)} %constant_dynamic-update-slice_fusion.21, bf16[1024,256]{1,0:T(8,128)(2,1)} %copy-done.27), kind=kOutput, calls=%fused_computation.19 | convolution fusion | flops 1208549376 | bytes 6422528 | tf_op jit(solution)/shard_map/vr,vc->rc/dot_general | solution.py:189
  273.8 4.2 %collective-permute-start.7 = (bf16[18,1,4,256]{3,1,0,2:T(2,128)(2,1)S(1)}, bf16[18,1,4,256]{3,1,0,2:T(2,128)(2,1)S(1)}, u32[]{:S(2)}, u32[]{:S(2)}) collective-permute-start(bf16[18,1,4,256]{3,1,0,2:T(2,128)(2,1)S(1)} %get-tuple-element.69), channel_id=1, source_target_pairs={{0,1},{1,2},{2,3},{4,5},{5,6},{6,7},{8,9},{9,10},{10,11},{12,13},{... | collective-permute-start | bytes 110600 | tf_op jit(solution)/shard_map/ppermute | solution.py:18
  289.5 4.0 %convolution_convert_fusion.2 = bf16[2304,256]{1,0:T(8,128)(2,1)S(1)} fusion(bf16[1024,2304]{1,0:T(8,128)(2,1)} %constant_dynamic-update-slice_fusion.21, bf16[1024,256]{1,0:T(8,128)(2,1)} %reshape.247), kind=kOutput, calls=%fused_computation.20 | convolution fusion | flops 1208549376 | bytes 6422528 | tf_op jit(solution)/shard_map/vr,vc->rc/dot_general | solution.py:189
  293.5 3.9 %convolution_convert_fusion = bf16[2304,256]{1,0:T(8,128)(2,1)S(1)} fusion(bf16[1024,2304]{1,0:T(8,128)(2,1)} %constant_dynamic-update-slice_fusion.21, bf16[1024,256]{1,0:T(8,128)(2,1)S(1)} %reshape.248), kind=kOutput, calls=%fused_computation.18 | convolution fusion | flops 1208549376 | bytes 6422528 | tf_op jit(solution)/shard_map/vr,vc->rc/dot_general | solution.py:189
  299.5 5.8 %all-to-all-start.1 = ((bf16[16,432,256]{2,1,0:T(8,128)(2,1)}), bf16[16,432,256]{2,1,0:T(8,128)(2,1)}, u32[]{:S(2)}, u32[]{:S(2)}) async-start(bf16[16,432,256]{2,1,0:T(8,128)(2,1)} %bitcast.160), calls=%async_computation.1 | async-start | bytes 7077888 | tf_op jit(solution)/shard_map/all_to_all | solution.py:241
  305.2 8.0 %copy.223 = bf16[9,3,256,256]{2,1,3,0:T(4,128)(2,1)} copy(bf16[9,3,256,256]{3,2,1,0:T(8,128)(2,1)} %bitcast.163) | data formatting | bytes 7077888 | tf_op jit(solution)/shard_map/reshape | solution.py:69
  313.2 5.1 %copy.246 = bf16[288,8,3,256]{3,1,2,0:T(8,128)(2,1)} copy(bf16[288,8,3,256]{3,2,1,0:T(4,128)(2,1)} %bitcast.158) | data formatting | bytes 7077888
  318.4 5.9 %copy.224 = bf16[768,2304]{1,0:T(8,128)(2,1)} copy(bf16[768,2304]{0,1:T(8,128)(2,1)} %bitcast.162) | data formatting | bytes 7077888 | tf_op jit(solution)/shard_map/dot_general | solution.py:206
  329.8 6.8 %fusion.8 = f32[256,4,3,256]{3,0,2,1:T(8,128)S(1)} fusion(bf16[3,256,2304,1]{2,1,0,3:T(8,128)(2,1)} %bitcast.173, bf16[256,4,2304]{2,0,1:T(8,128)(2,1)} %constant_dynamic-update-slice_fusion.12), kind=kOutput, calls=%fused_computation.9 | convolution fusion | flops 3623878656 | bytes 11403264 | tf_op jit(solution)/shard_map/dot_general | solution.py:206
  338.2 14.1 %all-to-all-done.1 = bf16[16,432,256]{2,1,0:T(8,128)(2,1)} async-done(((bf16[16,432,256]{2,1,0:T(8,128)(2,1)}), bf16[16,432,256]{2,1,0:T(8,128)(2,1)}, u32[]{:S(2)}, u32[]{:S(2)}) %all-to-all-start.1) | async-done | bytes 3538976 | tf_op jit(solution)/shard_map/all_to_all | solution.py:241
  352.3 3.3 reduce_sum.91
  (220 shorter events, 152.6 us)
Async XLA Ops:
  7.2 50.3 %copy-start = (bf16[2048,512]{1,0:T(8,128)(2,1)S(1)}, bf16[2048,512]{1,0:T(8,128)(2,1)}, u32[]{:S(2)}) copy-start(bf16[2048,512]{1,0:T(8,128)(2,1)} %param.9) | copy-start | bytes 6291460
  7.2 111.2 %all-gather.2.cloned.1.call-start = ((), (), s32[]{:S(2)}) async-start(), calls=%async_computation.3 | async-start | bytes 4456448 | tf_op jit(solution)/shard_map/all_gather | solution.py:95
  7.2 20.2 %copy-start.1 = (bf16[6912,256]{1,0:T(8,128)(2,1)S(1)}, bf16[6912,256]{1,0:T(8,128)(2,1)}, u32[]{:S(2)}) copy-start(bf16[6912,256]{1,0:T(8,128)(2,1)} %param.8) | copy-start | bytes 10616836
  8.2 6.7 %collective-permute-start = (bf16[1,16,4,256]{3,2,1,0:T(4,128)(2,1)S(1)}, bf16[1,16,4,256]{3,2,1,0:T(4,128)(2,1)S(1)}, u32[]{:S(2)}, u32[]{:S(2)}) collective-permute-start(bf16[1,16,4,256]{3,2,1,0:T(4,128)(2,1)S(1)} %get-tuple-element.86), channel_id=1, source_target_pairs={{0,4},{4,8},{8,12},{1,5},{5,9},{9,13},{2,6},{6,10},{10,14},{3,7},{... | collective-permute-start | bytes 98312 | tf_op jit(solution)/shard_map/ppermute | solution.py:18
  12.9 5.2 %collective-permute-start.1 = (bf16[1,16,4,256]{3,2,1,0:T(4,128)(2,1)S(1)}, bf16[1,16,4,256]{3,2,1,0:T(4,128)(2,1)S(1)}, u32[]{:S(2)}, u32[]{:S(2)}) collective-permute-start(bf16[1,16,4,256]{3,2,1,0:T(4,128)(2,1)S(1)} %get-tuple-element.85), channel_id=1, source_target_pairs={{4,0},{8,4},{12,8},{5,1},{9,5},{13,9},{6,2},{10,6},{14,10},{7,3},{... | collective-permute-start | bytes 98312 | tf_op jit(solution)/shard_map/ppermute | solution.py:21
  21.0 18.6 %copy-start.6 = (bf16[16,16,4,256]{3,2,1,0:T(4,128)(2,1)}, bf16[16,16,4,256]{3,2,1,0:T(4,128)(2,1)S(1)}, u32[]{:S(2)}) copy-start(bf16[16,16,4,256]{3,2,1,0:T(4,128)(2,1)S(1)} %get-tuple-element.84) | copy-start | bytes 1572868
  21.1 18.6 %copy-start.5 = (bf16[16,16,4,256]{3,2,1,0:T(4,128)(2,1)}, bf16[16,16,4,256]{3,2,1,0:T(4,128)(2,1)S(1)}, u32[]{:S(2)}) copy-start(bf16[16,16,4,256]{3,2,1,0:T(4,128)(2,1)S(1)} %get-tuple-element.82) | copy-start | bytes 1572868
  21.1 6.4 %copy-start.26 = (bf16[18,16,4,256]{3,2,1,0:T(4,128)(2,1)}, bf16[18,16,4,256]{3,2,1,0:T(4,128)(2,1)S(1)}, u32[]{:S(2)}) copy-start(bf16[18,16,4,256]{3,2,1,0:T(4,128)(2,1)S(1)} %constant_dynamic-update-slice_fusion) | copy-start | bytes 1769476
  21.1 18.6 %collective-permute-start.2 = (bf16[18,1,4,256]{3,2,1,0:T(4,128)(2,1)S(1)}, bf16[18,1,4,256]{3,2,1,0:T(4,128)(2,1)S(1)}, u32[]{:S(2)}, u32[]{:S(2)}) collective-permute-start(bf16[18,1,4,256]{3,2,1,0:T(4,128)(2,1)S(1)} %get-tuple-element.75), channel_id=1, source_target_pairs={{0,1},{1,2},{2,3},{4,5},{5,6},{6,7},{8,9},{9,10},{10,11},{12,13},{... | collective-permute-start | bytes 110600 | tf_op jit(solution)/shard_map/ppermute | solution.py:18
  24.3 15.5 %collective-permute-start.3 = (bf16[18,1,4,256]{3,2,1,0:T(4,128)(2,1)S(1)}, bf16[18,1,4,256]{3,2,1,0:T(4,128)(2,1)S(1)}, u32[]{:S(2)}, u32[]{:S(2)}) collective-permute-start(bf16[18,1,4,256]{3,2,1,0:T(4,128)(2,1)S(1)} %get-tuple-element.74), channel_id=1, source_target_pairs={{1,0},{2,1},{3,2},{5,4},{6,5},{7,6},{9,8},{10,9},{11,10},{13,12},{... | collective-permute-start | bytes 110600 | tf_op jit(solution)/shard_map/ppermute | solution.py:21
  50.9 8.4 %copy-start.31 = (f32[512]{0:T(512)S(1)}, f32[512]{0:T(512)}, u32[]{:S(2)}) copy-start(f32[512]{0:T(512)} %param.10) | copy-start | bytes 6148
  59.3 158.8 %copy-start.32 = (f32[128]{0:T(128)}, f32[128]{0:T(128)S(1)}, u32[]{:S(2)}) copy-start(f32[128]{0:T(128)S(1)} %add_rsqrt_fusion) | copy-start | bytes 1540
  134.1 6.2 %copy-start.3 = (f32[8,128,2048]{2,1,0:T(8,128)}, f32[8,128,2048]{2,1,0:T(8,128)S(1)}, u32[]{:S(2)}) copy-start(f32[8,128,2048]{2,1,0:T(8,128)S(1)} %get-tuple-element.90) | copy-start | bytes 25165828
  147.9 60.7 %all-to-all-start = ((bf16[16,128,1024]{1,2,0:T(8,128)(2,1)}), bf16[16,128,1024]{1,2,0:T(8,128)(2,1)}, u32[]{:S(2)}, u32[]{:S(2)}) async-start(bf16[16,128,1024]{1,2,0:T(8,128)(2,1)} %pad_maximum_fusion.1), calls=%async_computation | async-start | bytes 8388608 | tf_op jit(solution)/shard_map/all_to_all | solution.py:148
  153.4 202.2 %reduce-scatter.5.cloned.1.call-start = ((), (), s32[]{:S(2)}) async-start(), calls=%async_computation.4 | async-start | bytes 4491264
  175.4 9.8 %copy-start.21 = (bf16[1024,256]{1,0:T(8,128)(2,1)S(1)}, bf16[1024,256]{1,0:T(8,128)(2,1)}, u32[]{:S(2)}) copy-start(bf16[1024,256]{1,0:T(8,128)(2,1)} %reshape.243) | copy-start | bytes 1572868
  175.4 10.7 %copy-start.20 = (bf16[1024,256]{1,0:T(8,128)(2,1)S(1)}, bf16[1024,256]{1,0:T(8,128)(2,1)}, u32[]{:S(2)}) copy-start(bf16[1024,256]{1,0:T(8,128)(2,1)} %reshape.244) | copy-start | bytes 1572868
  175.4 11.6 %copy-start.18 = (bf16[2048,512]{0,1:T(8,128)(2,1)S(1)}, bf16[2048,512]{0,1:T(8,128)(2,1)}, u32[]{:S(2)}) copy-start(bf16[2048,512]{0,1:T(8,128)(2,1)} %copy.211) | copy-start | bytes 6291460
  212.2 6.4 %copy-start.4 = (bf16[128,2048]{1,0:T(8,128)(2,1)S(1)}, bf16[128,2048]{1,0:T(8,128)(2,1)}, u32[]{:S(2)}) copy-start(bf16[128,2048]{1,0:T(8,128)(2,1)} %reshape.230) | copy-start | bytes 1572868
  218.1 11.6 %copy-start.34 = (f32[128]{0:T(128)}, f32[128]{0:T(128)S(1)}, u32[]{:S(2)}) copy-start(f32[128]{0:T(128)S(1)} %get-tuple-element.94) | copy-start | bytes 1540
  234.2 3.9 %copy-start.33 = (f32[128]{0:T(128)S(1)}, f32[128]{0:T(128)}, u32[]{:S(2)}) copy-start(f32[128]{0:T(128)} %copy-done.32) | copy-start | bytes 1540
  234.2 3.9 %copy-start.35 = (f32[128]{0:T(128)S(1)}, f32[128]{0:T(128)}, u32[]{:S(2)}) copy-start(f32[128]{0:T(128)} %copy-done.34) | copy-start | bytes 1540
  255.6 15.7 %collective-permute-start.4 = (bf16[1,16,4,256]{3,2,1,0:T(4,128)(2,1)S(1)}, bf16[1,16,4,256]{3,2,1,0:T(4,128)(2,1)S(1)}, u32[]{:S(2)}, u32[]{:S(2)}) collective-permute-start(bf16[1,16,4,256]{3,2,1,0:T(4,128)(2,1)S(1)} %slice.178), channel_id=1, source_target_pairs={{0,4},{4,8},{8,12},{1,5},{5,9},{9,13},{2,6},{6,10},{10,14},{3,7},{... | collective-permute-start | bytes 98312 | tf_op jit(solution)/shard_map/ppermute | solution.py:18
  258.4 7.1 %copy-start.14 = (f32[16,16,4,256]{3,2,1,0:T(4,128)S(1)}, f32[16,16,4,256]{3,2,1,0:T(4,128)}, u32[]{:S(2)}) copy-start(f32[16,16,4,256]{3,2,1,0:T(4,128)} %reshape.259) | copy-start | bytes 3145732
  258.4 8.3 %copy-start.2 = (f32[8,8,2,2,2,2,256]{6,5,4,3,2,1,0:T(2,128)S(1)}, f32[8,8,2,2,2,2,256]{6,5,4,3,2,1,0:T(2,128)}, u32[]{:S(2)}) copy-start(f32[8,8,2,2,2,2,256]{6,5,4,3,2,1,0:T(2,128)} %reshape.262) | copy-start | bytes 3145732
  258.4 12.8 %collective-permute-start.5 = (bf16[1,16,4,256]{3,2,1,0:T(4,128)(2,1)S(1)}, bf16[1,16,4,256]{3,2,1,0:T(4,128)(2,1)S(1)}, u32[]{:S(2)}, u32[]{:S(2)}) collective-permute-start(bf16[1,16,4,256]{3,2,1,0:T(4,128)(2,1)S(1)} %slice.180), channel_id=1, source_target_pairs={{4,0},{8,4},{12,8},{5,1},{9,5},{13,9},{6,2},{10,6},{14,10},{7,3},{... | collective-permute-start | bytes 98312 | tf_op jit(solution)/shard_map/ppermute | solution.py:21
  272.5 7.7 %collective-permute-start.6 = (bf16[18,1,4,256]{3,1,0,2:T(2,128)(2,1)S(1)}, bf16[18,1,4,256]{3,1,0,2:T(2,128)(2,1)S(1)}, u32[]{:S(2)}, u32[]{:S(2)}) collective-permute-start(bf16[18,1,4,256]{3,1,0,2:T(2,128)(2,1)S(1)} %get-tuple-element.70), channel_id=1, source_target_pairs={{1,0},{2,1},{3,2},{5,4},{6,5},{7,6},{9,8},{10,9},{11,10},{13,12},{... | collective-permute-start | bytes 110600 | tf_op jit(solution)/shard_map/ppermute | solution.py:21
  273.8 7.2 %collective-permute-start.7 = (bf16[18,1,4,256]{3,1,0,2:T(2,128)(2,1)S(1)}, bf16[18,1,4,256]{3,1,0,2:T(2,128)(2,1)S(1)}, u32[]{:S(2)}, u32[]{:S(2)}) collective-permute-start(bf16[18,1,4,256]{3,1,0,2:T(2,128)(2,1)S(1)} %get-tuple-element.69), channel_id=1, source_target_pairs={{0,1},{1,2},{2,3},{4,5},{5,6},{6,7},{8,9},{9,10},{10,11},{12,13},{... | collective-permute-start | bytes 110600 | tf_op jit(solution)/shard_map/ppermute | solution.py:18
  293.4 4.0 %copy-start.24 = (bf16[2304,256]{1,0:T(8,128)(2,1)S(1)}, bf16[2304,256]{1,0:T(8,128)(2,1)}, u32[]{:S(2)}) copy-start(bf16[2304,256]{1,0:T(8,128)(2,1)} %convolution_convert_fusion.1) | copy-start | bytes 3538948
  299.5 52.8 %all-to-all-start.1 = ((bf16[16,432,256]{2,1,0:T(8,128)(2,1)}), bf16[16,432,256]{2,1,0:T(8,128)(2,1)}, u32[]{:S(2)}, u32[]{:S(2)}) async-start(bf16[16,432,256]{2,1,0:T(8,128)(2,1)} %bitcast.160), calls=%async_computation.1 | async-start | bytes 7077888 | tf_op jit(solution)/shard_map/all_to_all | solution.py:241
  318.4 7.8 %copy-start.22 = (bf16[16,16,4,256]{3,1,0,2:T(8,128)(2,1)S(1)}, bf16[16,16,4,256]{3,1,0,2:T(8,128)(2,1)}, u32[]{:S(2)}) copy-start(bf16[16,16,4,256]{3,1,0,2:T(8,128)(2,1)} %get-tuple-element.58) | copy-start | bytes 1572868
  318.4 8.7 %copy-start.16 = (bf16[16,16,4,256]{3,1,0,2:T(8,128)(2,1)S(1)}, bf16[16,16,4,256]{3,1,0,2:T(8,128)(2,1)}, u32[]{:S(2)}) copy-start(bf16[16,16,4,256]{3,1,0,2:T(8,128)(2,1)} %get-tuple-element.78) | copy-start | bytes 1572868
  (19 other events, 36.5 us)
Sparse Core Ops, SparseCore 0:
  62.8 55.5 all-gather.1
  234.4 72.7 reduce-scatter.4

commit v8 on v7

--- a/solution.py
+++ b/solution.py
@@ -120,7 +120,7 @@
     d_probs = jnp.einsum("ihe,jhe->hij", d_att_h, values_h, preferred_element_type=jnp.float32)
     d_probs = d_probs.astype(jnp.bfloat16).astype(jnp.float32)
     row_delta = jnp.sum(attn_probs * d_probs, axis=-1)
-    d_scores = attn_probs * (d_probs - row_delta[:, :, None])
+    d_scores = (attn_probs * (d_probs - row_delta[:, :, None])).astype(jnp.bfloat16)
     d_queries = (
         jnp.einsum(
             "hij,jhe->ihe", d_scores, keys_h, preferred_element_type=jnp.float32

time: 376 us -> 377 us (level)
  matrix products: 65.5 us -> 60 us
    unnamed x111 -> x109, local copies, waits for them, and re-layouts: 37.9 us -> 38.6 us
  transfers between devices with their start and end apart: 12 -> 12, of which waited for: 5 -> 5; matrix products, arithmetic and copies ran while one was open for 43% -> 42% of each run, Pallas kernels for 0% -> 0%
where the time goes in v8:
time: 377 us; the launch traced here: 370 us
  local copies, waits for them, and re-layouts  151 us (40%)
  waiting for transfers between devices  74.4 us (20%)
  matrix products  60 us (16%)
  other arithmetic  35.7 us (9%)
  starting transfers between devices  32.8 us (9%)
  between operations  15.3 us (4%)
    all_gather x1, waiting for transfers between devices, local(): lax.all_gather(qkv_rows[:, model_width:], ('gx', 'gy'), axis=0, tiled=True)  47.9 us
    unnamed x109, local copies, waits for them, and re-layouts  38.6 us
    reshape x9, local copies, waits for them, and re-layouts, plane_columns(): padded[start_x:start_x + extent_x, start_y:start_y + extent_y]  17.8 us
    convert_element_type x6, local copies, waits for them, and re-layouts, local(): d_act_grid = from_tokens(d_activation, extent_x, extent_y, extent_z).resh...  16.5 us
    ppermute x4, starting transfers between devices, padded_2(): lax.ppermute(lax.slice_in_dim(block, block.shape[dim] - width, None, axis...  14.9 us
    all_to_all x1, waiting for transfers between devices, local(): conv_rows = lax.all_to_all(conv_part, ('gx', 'gy'), 0, 0, tiled=True)  14.1 us
    dot_general x3, matrix products, local(): jnp.einsum('vr,vc->rc', columns, shifted.reshape(voxels, channels), prefe...  12.9 us
    concatenate x5, other arithmetic, padded_2(): block = jnp.concatenate([low, block, high], axis=dim)  11.7 us
  transfers between devices with their start and end apart: 12, of which 5 were waited for; matrix products, arithmetic and copies ran while one was open for 42% of the time, Pallas kernels for 0%

profile of v8, /device:TPU:1, one launch (start us, length us, event | category | flops | bytes accessed | tf_op | source)
XLA Modules:
  0.0 369.5 jit_solution(2719286676606922143)
XLA Ops:
  8.2 4.7 %collective-permute-start = (bf16[1,16,4,256]{3,2,1,0:T(4,128)(2,1)S(1)}, bf16[1,16,4,256]{3,2,1,0:T(4,128)(2,1)S(1)}, u32[]{:S(2)}, u32[]{:S(2)}) collective-permute-start(bf16[1,16,4,256]{3,2,1,0:T(4,128)(2,1)S(1)} %get-tuple-element.86), channel_id=1, source_target_pairs={{0,4},{4,8},{8,12},{1,5},{5,9},{9,13},{2,6},{6,10},{10,14},{3,7},{... | collective-permute-start | bytes 98312 | tf_op jit(solution)/shard_map/ppermute | solution.py:18
  14.9 3.3 collective-permute-done.1
  21.1 3.1 collective-permute-start.2
  33.3 6.2 %copy.202 = bf16[768,2304]{1,0:T(8,128)(2,1)} copy(bf16[768,2304]{0,1:T(8,128)(2,1)} %bitcast.165) | data formatting | bytes 7077888 | tf_op jit(solution)/shard_map/dot_general | solution.py:74
  39.8 3.8 %pad_maximum_fusion.6 = (bf16[16,16,4,256]{3,2,1,0:T(4,128)(2,1)S(1)}, bf16[16,16,4,256]{3,2,1,0:T(4,128)(2,1)S(1)}, bf16[16,16,4,256]{3,2,1,0:T(4,128)(2,1)S(1)...) fusion(bf16[18,1,4,256]{3,2,1,0:T(4,128)(2,1)S(1)} %collective-, ...), kind=kLoop, calls=%fused_computation.66 | loop fusion | flops 1572864 | bytes 3809280 | tf_op jit(solution)/shard_map/concatenate | solution.py:22
  46.8 3.8 %fusion.7 = f32[256,4,3,256]{3,0,2,1:T(8,128)S(1)} fusion(bf16[3,256,2304,1]{2,1,0,3:T(8,128)(2,1)S(1)} %bitcast.175, bf16[256,4,2304]{2,0,1:T(8,128)(2,1)S(1)} %constant_dynamic-update-slice_fusion.3), kind=kOutput, calls=%fused_computation.10 | convolution fusion | flops 3623878656 | bytes 11403264 | tf_op jit(solution)/shard_map/dot_general | solution.py:74
  70.6 47.9 %all-gather.2.cloned.1.call-done = bf16[2048,1024]{1,0:T(8,128)(2,1)} async-done(((bf16[128,1024]{1,0:T(8,128)(2,1)}), bf16[2048,1024]{1,0:T(8,128)(2,1)}) %all-gather.2.cloned.1.call-update) | async-done | bytes 4194320 | tf_op jit(solution)/shard_map/all_gather | solution.py:95
  118.4 4.5 %fusion.39 = (bf16[2048,512]{1,0:T(8,128)(2,1)}, bf16[2048,512]{1,0:T(8,128)(2,1)}) fusion(bf16[2048,1024]{1,0:T(8,128)(2,1)} %all-gather.2.cloned.1.call-done), kind=kLoop, calls=%fused_computation.127 | loop fusion | bytes 8388608 | tf_op jit(solution)/shard_map/slice | solution.py:99
  122.9 4.0 %copy.208 = bf16[2048,512]{0,1:T(8,128)(2,1)} copy(bf16[2048,512]{1,0:T(8,128)(2,1)} %get-tuple-element.50) | data formatting | bytes 4194304 | tf_op jit(solution)/shard_map/slice | solution.py:98
  126.9 3.9 %copy.211 = bf16[2048,512]{0,1:T(8,128)(2,1)} copy(bf16[2048,512]{1,0:T(8,128)(2,1)} %get-tuple-element.49) | data formatting | bytes 4194304 | tf_op jit(solution)/shard_map/slice | solution.py:99
  130.8 3.2 fusion.4
  148.5 5.4 %all-to-all-start = ((bf16[16,128,1024]{1,2,0:T(8,128)(2,1)}), bf16[16,128,1024]{1,2,0:T(8,128)(2,1)}, u32[]{:S(2)}, u32[]{:S(2)}) async-start(bf16[16,128,1024]{1,2,0:T(8,128)(2,1)} %pad_maximum_fusion.1), calls=%async_computation | async-start | bytes 8388608 | tf_op jit(solution)/shard_map/all_to_all | solution.py:148
  187.5 5.2 %fusion.14 = bf16[8,64,128]{2,1,0:T(8,128)(2,1)S(1)} fusion(bf16[2048,8,64]{0,2,1:T(8,128)(2,1)S(1)} %bitcast.180, f32[8,128,2048]{2,1,0:T(8,128)} %copy-done.2, f32[8,128]{1,0:T(8,128)S(1)} %get-tuple-element.89), kind=kOutput, calls=%fused_computation.32 | convolution fusion | flops 274792448 | bytes 10620928 | tf_op jit(solution)/shard_map/hij,jhe->ihe/dot_general | solution.py:111
  195.9 5.0 %fusion.13 = bf16[8,64,128]{2,1,0:T(8,128)(2,1)} fusion(bf16[2048,8,64]{0,2,1:T(8,128)(2,1)} %bitcast.160, bf16[8,128,2048]{2,1,0:T(8,128)(2,1)} %copy-done.1), kind=kOutput, calls=%fused_computation.31 | convolution fusion | flops 268566528 | bytes 6422528 | tf_op jit(solution)/shard_map/hij,jhe->ihe/dot_general | solution.py:125
  200.9 8.3 %all-to-all-done = bf16[16,128,1024]{1,2,0:T(8,128)(2,1)} async-done(((bf16[16,128,1024]{1,2,0:T(8,128)(2,1)}), bf16[16,128,1024]{1,2,0:T(8,128)(2,1)}, u32[]{:S(2)}, u32[]{:S(2)}) %all-to-all-start) | async-done | bytes 4194336 | tf_op jit(solution)/shard_map/all_to_all | solution.py:148
  209.2 3.5 reduce.2
  221.4 4.5 %reshape.249 = bf16[16,512,128]{2,1,0:T(8,128)(2,1)} reshape(bf16[2048,512]{1,0:T(8,128)(2,1)} %convolution_convert_fusion.4) | data formatting | bytes 4194304 | tf_op jit(solution)/shard_map/reshape | solution.py:226
  225.9 4.3 %reshape.250 = bf16[16,384,128]{2,1,0:T(8,128)(2,1)} reshape(bf16[512,1536]{1,0:T(8,128)(2,1)} %convolution_convert_fusion.5) | data formatting | bytes 3145728 | tf_op jit(solution)/shard_map/reshape | solution.py:226
  231.1 3.7 pad_maximum_fusion
  241.5 3.1 reshape.262
  247.3 3.2 reshape.259
  261.1 5.0 %convolution_convert_fusion.1 = bf16[2304,256]{1,0:T(8,128)(2,1)} fusion(bf16[1024,2304]{1,0:T(8,128)(2,1)} %constant_dynamic-update-slice_fusion.21, bf16[1024,256]{1,0:T(8,128)(2,1)} %copy-done.29), kind=kOutput, calls=%fused_computation.16 | convolution fusion | flops 1208549376 | bytes 6422528 | tf_op jit(solution)/shard_map/vr,vc->rc/dot_general | solution.py:189
  274.4 4.2 %collective-permute-start.7 = (bf16[18,1,4,256]{3,1,0,2:T(2,128)(2,1)S(1)}, bf16[18,1,4,256]{3,1,0,2:T(2,128)(2,1)S(1)}, u32[]{:S(2)}, u32[]{:S(2)}) collective-permute-start(bf16[18,1,4,256]{3,1,0,2:T(2,128)(2,1)S(1)} %get-tuple-element.69), channel_id=1, source_target_pairs={{0,1},{1,2},{2,3},{4,5},{5,6},{6,7},{8,9},{9,10},{10,11},{12,13},{... | collective-permute-start | bytes 110600 | tf_op jit(solution)/shard_map/ppermute | solution.py:18
  290.1 4.0 %convolution_convert_fusion.2 = bf16[2304,256]{1,0:T(8,128)(2,1)S(1)} fusion(bf16[1024,2304]{1,0:T(8,128)(2,1)} %constant_dynamic-update-slice_fusion.21, bf16[1024,256]{1,0:T(8,128)(2,1)} %reshape.247), kind=kOutput, calls=%fused_computation.17 | convolution fusion | flops 1208549376 | bytes 6422528 | tf_op jit(solution)/shard_map/vr,vc->rc/dot_general | solution.py:189
  294.1 3.9 %convolution_convert_fusion = bf16[2304,256]{1,0:T(8,128)(2,1)S(1)} fusion(bf16[1024,2304]{1,0:T(8,128)(2,1)} %constant_dynamic-update-slice_fusion.21, bf16[1024,256]{1,0:T(8,128)(2,1)S(1)} %reshape.248), kind=kOutput, calls=%fused_computation.15 | convolution fusion | flops 1208549376 | bytes 6422528 | tf_op jit(solution)/shard_map/vr,vc->rc/dot_general | solution.py:189
  300.0 5.8 %all-to-all-start.1 = ((bf16[16,432,256]{2,1,0:T(8,128)(2,1)}), bf16[16,432,256]{2,1,0:T(8,128)(2,1)}, u32[]{:S(2)}, u32[]{:S(2)}) async-start(bf16[16,432,256]{2,1,0:T(8,128)(2,1)} %bitcast.164), calls=%async_computation.1 | async-start | bytes 7077888 | tf_op jit(solution)/shard_map/all_to_all | solution.py:241
  305.9 8.0 %copy.223 = bf16[9,3,256,256]{2,1,3,0:T(4,128)(2,1)} copy(bf16[9,3,256,256]{3,2,1,0:T(8,128)(2,1)} %bitcast.167) | data formatting | bytes 7077888 | tf_op jit(solution)/shard_map/reshape | solution.py:69
  313.9 5.1 %copy.246 = bf16[288,8,3,256]{3,1,2,0:T(8,128)(2,1)} copy(bf16[288,8,3,256]{3,2,1,0:T(4,128)(2,1)} %bitcast.162) | data formatting | bytes 7077888
  319.0 5.9 %copy.224 = bf16[768,2304]{1,0:T(8,128)(2,1)} copy(bf16[768,2304]{0,1:T(8,128)(2,1)} %bitcast.166) | data formatting | bytes 7077888 | tf_op jit(solution)/shard_map/dot_general | solution.py:206
  330.5 6.8 %fusion.5 = f32[256,4,3,256]{3,0,2,1:T(8,128)S(1)} fusion(bf16[3,256,2304,1]{2,1,0,3:T(8,128)(2,1)} %bitcast.176, bf16[256,4,2304]{2,0,1:T(8,128)(2,1)} %constant_dynamic-update-slice_fusion.12), kind=kOutput, calls=%fused_computation.8 | convolution fusion | flops 3623878656 | bytes 11403264 | tf_op jit(solution)/shard_map/dot_general | solution.py:206
  338.9 14.1 %all-to-all-done.1 = bf16[16,432,256]{2,1,0:T(8,128)(2,1)} async-done(((bf16[16,432,256]{2,1,0:T(8,128)(2,1)}), bf16[16,432,256]{2,1,0:T(8,128)(2,1)}, u32[]{:S(2)}, u32[]{:S(2)}) %all-to-all-start.1) | async-done | bytes 3538976 | tf_op jit(solution)/shard_map/all_to_all | solution.py:241
  353.0 3.3 reduce_sum.91
  (219 shorter events, 153.3 us)
Async XLA Ops:
  7.2 50.4 %copy-start = (bf16[2048,512]{1,0:T(8,128)(2,1)S(1)}, bf16[2048,512]{1,0:T(8,128)(2,1)}, u32[]{:S(2)}) copy-start(bf16[2048,512]{1,0:T(8,128)(2,1)} %param.9) | copy-start | bytes 6291460
  7.2 111.2 %all-gather.2.cloned.1.call-start = ((), (), s32[]{:S(2)}) async-start(), calls=%async_computation.3 | async-start | bytes 4456448 | tf_op jit(solution)/shard_map/all_gather | solution.py:95
  7.2 20.2 %copy-start.3 = (bf16[6912,256]{1,0:T(8,128)(2,1)S(1)}, bf16[6912,256]{1,0:T(8,128)(2,1)}, u32[]{:S(2)}) copy-start(bf16[6912,256]{1,0:T(8,128)(2,1)} %param.8) | copy-start | bytes 10616836
  8.2 6.7 %collective-permute-start = (bf16[1,16,4,256]{3,2,1,0:T(4,128)(2,1)S(1)}, bf16[1,16,4,256]{3,2,1,0:T(4,128)(2,1)S(1)}, u32[]{:S(2)}, u32[]{:S(2)}) collective-permute-start(bf16[1,16,4,256]{3,2,1,0:T(4,128)(2,1)S(1)} %get-tuple-element.86), channel_id=1, source_target_pairs={{0,4},{4,8},{8,12},{1,5},{5,9},{9,13},{2,6},{6,10},{10,14},{3,7},{... | collective-permute-start | bytes 98312 | tf_op jit(solution)/shard_map/ppermute | solution.py:18
  12.9 5.2 %collective-permute-start.1 = (bf16[1,16,4,256]{3,2,1,0:T(4,128)(2,1)S(1)}, bf16[1,16,4,256]{3,2,1,0:T(4,128)(2,1)S(1)}, u32[]{:S(2)}, u32[]{:S(2)}) collective-permute-start(bf16[1,16,4,256]{3,2,1,0:T(4,128)(2,1)S(1)} %get-tuple-element.85), channel_id=1, source_target_pairs={{4,0},{8,4},{12,8},{5,1},{9,5},{13,9},{6,2},{10,6},{14,10},{7,3},{... | collective-permute-start | bytes 98312 | tf_op jit(solution)/shard_map/ppermute | solution.py:21
  21.0 18.5 %copy-start.7 = (bf16[16,16,4,256]{3,2,1,0:T(4,128)(2,1)}, bf16[16,16,4,256]{3,2,1,0:T(4,128)(2,1)S(1)}, u32[]{:S(2)}) copy-start(bf16[16,16,4,256]{3,2,1,0:T(4,128)(2,1)S(1)} %get-tuple-element.84) | copy-start | bytes 1572868
  21.1 18.6 %copy-start.6 = (bf16[16,16,4,256]{3,2,1,0:T(4,128)(2,1)}, bf16[16,16,4,256]{3,2,1,0:T(4,128)(2,1)S(1)}, u32[]{:S(2)}) copy-start(bf16[16,16,4,256]{3,2,1,0:T(4,128)(2,1)S(1)} %get-tuple-element.82) | copy-start | bytes 1572868
  21.1 6.4 %copy-start.28 = (bf16[18,16,4,256]{3,2,1,0:T(4,128)(2,1)}, bf16[18,16,4,256]{3,2,1,0:T(4,128)(2,1)S(1)}, u32[]{:S(2)}) copy-start(bf16[18,16,4,256]{3,2,1,0:T(4,128)(2,1)S(1)} %constant_dynamic-update-slice_fusion) | copy-start | bytes 1769476
  21.1 18.6 %collective-permute-start.2 = (bf16[18,1,4,256]{3,2,1,0:T(4,128)(2,1)S(1)}, bf16[18,1,4,256]{3,2,1,0:T(4,128)(2,1)S(1)}, u32[]{:S(2)}, u32[]{:S(2)}) collective-permute-start(bf16[18,1,4,256]{3,2,1,0:T(4,128)(2,1)S(1)} %get-tuple-element.75), channel_id=1, source_target_pairs={{0,1},{1,2},{2,3},{4,5},{5,6},{6,7},{8,9},{9,10},{10,11},{12,13},{... | collective-permute-start | bytes 110600 | tf_op jit(solution)/shard_map/ppermute | solution.py:18
  24.3 15.5 %collective-permute-start.3 = (bf16[18,1,4,256]{3,2,1,0:T(4,128)(2,1)S(1)}, bf16[18,1,4,256]{3,2,1,0:T(4,128)(2,1)S(1)}, u32[]{:S(2)}, u32[]{:S(2)}) collective-permute-start(bf16[18,1,4,256]{3,2,1,0:T(4,128)(2,1)S(1)} %get-tuple-element.74), channel_id=1, source_target_pairs={{1,0},{2,1},{3,2},{5,4},{6,5},{7,6},{9,8},{10,9},{11,10},{13,12},{... | collective-permute-start | bytes 110600 | tf_op jit(solution)/shard_map/ppermute | solution.py:21
  51.0 8.4 %copy-start.32 = (f32[512]{0:T(512)S(1)}, f32[512]{0:T(512)}, u32[]{:S(2)}) copy-start(f32[512]{0:T(512)} %param.10) | copy-start | bytes 6148
  59.3 159.3 %copy-start.33 = (f32[128]{0:T(128)}, f32[128]{0:T(128)S(1)}, u32[]{:S(2)}) copy-start(f32[128]{0:T(128)S(1)} %add_rsqrt_fusion) | copy-start | bytes 1540
  134.1 6.1 %copy-start.2 = (f32[8,128,2048]{2,1,0:T(8,128)}, f32[8,128,2048]{2,1,0:T(8,128)S(1)}, u32[]{:S(2)}) copy-start(f32[8,128,2048]{2,1,0:T(8,128)S(1)} %get-tuple-element.90) | copy-start | bytes 25165828
  148.5 60.7 %all-to-all-start = ((bf16[16,128,1024]{1,2,0:T(8,128)(2,1)}), bf16[16,128,1024]{1,2,0:T(8,128)(2,1)}, u32[]{:S(2)}, u32[]{:S(2)}) async-start(bf16[16,128,1024]{1,2,0:T(8,128)(2,1)} %pad_maximum_fusion.1), calls=%async_computation | async-start | bytes 8388608 | tf_op jit(solution)/shard_map/all_to_all | solution.py:148
  154.0 202.3 %reduce-scatter.5.cloned.1.call-start = ((), (), s32[]{:S(2)}) async-start(), calls=%async_computation.4 | async-start | bytes 4491264
  176.0 9.8 %copy-start.22 = (bf16[1024,256]{1,0:T(8,128)(2,1)S(1)}, bf16[1024,256]{1,0:T(8,128)(2,1)}, u32[]{:S(2)}) copy-start(bf16[1024,256]{1,0:T(8,128)(2,1)} %reshape.243) | copy-start | bytes 1572868
  176.0 10.7 %copy-start.21 = (bf16[1024,256]{1,0:T(8,128)(2,1)S(1)}, bf16[1024,256]{1,0:T(8,128)(2,1)}, u32[]{:S(2)}) copy-start(bf16[1024,256]{1,0:T(8,128)(2,1)} %reshape.244) | copy-start | bytes 1572868
  176.0 11.6 %copy-start.19 = (bf16[2048,512]{0,1:T(8,128)(2,1)S(1)}, bf16[2048,512]{0,1:T(8,128)(2,1)}, u32[]{:S(2)}) copy-start(bf16[2048,512]{0,1:T(8,128)(2,1)} %copy.211) | copy-start | bytes 6291460
  212.8 6.4 %copy-start.5 = (bf16[128,2048]{1,0:T(8,128)(2,1)S(1)}, bf16[128,2048]{1,0:T(8,128)(2,1)}, u32[]{:S(2)}) copy-start(bf16[128,2048]{1,0:T(8,128)(2,1)} %reshape.230) | copy-start | bytes 1572868
  218.7 11.5 %copy-start.35 = (f32[128]{0:T(128)}, f32[128]{0:T(128)S(1)}, u32[]{:S(2)}) copy-start(f32[128]{0:T(128)S(1)} %get-tuple-element.94) | copy-start | bytes 1540
  234.8 3.9 %copy-start.34 = (f32[128]{0:T(128)S(1)}, f32[128]{0:T(128)}, u32[]{:S(2)}) copy-start(f32[128]{0:T(128)} %copy-done.33) | copy-start | bytes 1540
  234.8 3.9 %copy-start.36 = (f32[128]{0:T(128)S(1)}, f32[128]{0:T(128)}, u32[]{:S(2)}) copy-start(f32[128]{0:T(128)} %copy-done.35) | copy-start | bytes 1540
  256.2 15.7 %collective-permute-start.4 = (bf16[1,16,4,256]{3,2,1,0:T(4,128)(2,1)S(1)}, bf16[1,16,4,256]{3,2,1,0:T(4,128)(2,1)S(1)}, u32[]{:S(2)}, u32[]{:S(2)}) collective-permute-start(bf16[1,16,4,256]{3,2,1,0:T(4,128)(2,1)S(1)} %slice.178), channel_id=1, source_target_pairs={{0,4},{4,8},{8,12},{1,5},{5,9},{9,13},{2,6},{6,10},{10,14},{3,7},{... | collective-permute-start | bytes 98312 | tf_op jit(solution)/shard_map/ppermute | solution.py:18
  259.0 7.1 %copy-start.15 = (f32[16,16,4,256]{3,2,1,0:T(4,128)S(1)}, f32[16,16,4,256]{3,2,1,0:T(4,128)}, u32[]{:S(2)}) copy-start(f32[16,16,4,256]{3,2,1,0:T(4,128)} %reshape.259) | copy-start | bytes 3145732
  259.0 8.3 %copy-start.4 = (f32[8,8,2,2,2,2,256]{6,5,4,3,2,1,0:T(2,128)S(1)}, f32[8,8,2,2,2,2,256]{6,5,4,3,2,1,0:T(2,128)}, u32[]{:S(2)}) copy-start(f32[8,8,2,2,2,2,256]{6,5,4,3,2,1,0:T(2,128)} %reshape.262) | copy-start | bytes 3145732
  259.0 12.8 %collective-permute-start.5 = (bf16[1,16,4,256]{3,2,1,0:T(4,128)(2,1)S(1)}, bf16[1,16,4,256]{3,2,1,0:T(4,128)(2,1)S(1)}, u32[]{:S(2)}, u32[]{:S(2)}) collective-permute-start(bf16[1,16,4,256]{3,2,1,0:T(4,128)(2,1)S(1)} %slice.180), channel_id=1, source_target_pairs={{4,0},{8,4},{12,8},{5,1},{9,5},{13,9},{6,2},{10,6},{14,10},{7,3},{... | collective-permute-start | bytes 98312 | tf_op jit(solution)/shard_map/ppermute | solution.py:21
  273.1 7.7 %collective-permute-start.6 = (bf16[18,1,4,256]{3,1,0,2:T(2,128)(2,1)S(1)}, bf16[18,1,4,256]{3,1,0,2:T(2,128)(2,1)S(1)}, u32[]{:S(2)}, u32[]{:S(2)}) collective-permute-start(bf16[18,1,4,256]{3,1,0,2:T(2,128)(2,1)S(1)} %get-tuple-element.70), channel_id=1, source_target_pairs={{1,0},{2,1},{3,2},{5,4},{6,5},{7,6},{9,8},{10,9},{11,10},{13,12},{... | collective-permute-start | bytes 110600 | tf_op jit(solution)/shard_map/ppermute | solution.py:21
  274.4 7.2 %collective-permute-start.7 = (bf16[18,1,4,256]{3,1,0,2:T(2,128)(2,1)S(1)}, bf16[18,1,4,256]{3,1,0,2:T(2,128)(2,1)S(1)}, u32[]{:S(2)}, u32[]{:S(2)}) collective-permute-start(bf16[18,1,4,256]{3,1,0,2:T(2,128)(2,1)S(1)} %get-tuple-element.69), channel_id=1, source_target_pairs={{0,1},{1,2},{2,3},{4,5},{5,6},{6,7},{8,9},{9,10},{10,11},{12,13},{... | collective-permute-start | bytes 110600 | tf_op jit(solution)/shard_map/ppermute | solution.py:18
  294.1 3.9 %copy-start.26 = (bf16[2304,256]{1,0:T(8,128)(2,1)S(1)}, bf16[2304,256]{1,0:T(8,128)(2,1)}, u32[]{:S(2)}) copy-start(bf16[2304,256]{1,0:T(8,128)(2,1)} %convolution_convert_fusion.1) | copy-start | bytes 3538948
  300.0 52.9 %all-to-all-start.1 = ((bf16[16,432,256]{2,1,0:T(8,128)(2,1)}), bf16[16,432,256]{2,1,0:T(8,128)(2,1)}, u32[]{:S(2)}, u32[]{:S(2)}) async-start(bf16[16,432,256]{2,1,0:T(8,128)(2,1)} %bitcast.164), calls=%async_computation.1 | async-start | bytes 7077888 | tf_op jit(solution)/shard_map/all_to_all | solution.py:241
  319.0 7.8 %copy-start.23 = (bf16[16,16,4,256]{3,1,0,2:T(8,128)(2,1)S(1)}, bf16[16,16,4,256]{3,1,0,2:T(8,128)(2,1)}, u32[]{:S(2)}) copy-start(bf16[16,16,4,256]{3,1,0,2:T(8,128)(2,1)} %get-tuple-element.58) | copy-start | bytes 1572868
  319.0 8.7 %copy-start.17 = (bf16[16,16,4,256]{3,1,0,2:T(8,128)(2,1)S(1)}, bf16[16,16,4,256]{3,1,0,2:T(8,128)(2,1)}, u32[]{:S(2)}) copy-start(bf16[16,16,4,256]{3,1,0,2:T(8,128)(2,1)} %get-tuple-element.78) | copy-start | bytes 1572868
  (18 other events, 31.7 us)
Sparse Core Ops, SparseCore 0:
  62.8 55.5 all-gather.1
  234.9 73.0 reduce-scatter.4

commit v9 on v7

--- a/solution.py
+++ b/solution.py
@@ -106,7 +106,7 @@
     )
     exp_scores = jnp.exp(scores)
     totals = jnp.sum(exp_scores, axis=-1)
-    attn_probs = exp_scores / totals[:, :, None]
+    attn_probs = exp_scores * (1.0 / totals)[:, :, None]
     probs_b = attn_probs.astype(jnp.bfloat16)
     attended = jnp.einsum("hij,jhe->ihe", probs_b, values_h, preferred_element_type=jnp.float32)
     attended = attended.reshape(tok_count, model_width).astype(jnp.bfloat16)

time: 376 us -> 382 us (1.016)
  matrix products: 65.5 us -> 71.9 us
    unnamed x111 -> x117, local copies, waits for them, and re-layouts: 37.9 us -> 37.9 us
where the time goes in v9:
time: 382 us; the launch traced here: 374 us
  local copies, waits for them, and re-layouts  150 us (39%)
  matrix products  71.9 us (19%)
  waiting for transfers between devices  71.3 us (19%)
  other arithmetic  33.3 us (9%)
  starting transfers between devices  32.5 us (9%)
  between operations  15.3 us (4%)
    all_gather x1, waiting for transfers between devices, local(): lax.all_gather(qkv_rows[:, model_width:], ('gx', 'gy'), axis=0, tiled=True)  47.9 us
    unnamed x117, local copies, waits for them, and re-layouts  37.9 us
    reshape x9, local copies, waits for them, and re-layouts, plane_columns(): padded[start_x:start_x + extent_x, start_y:start_y + extent_y]  17.7 us
    convert_element_type x6, local copies, waits for them, and re-layouts, local(): d_act_grid = from_tokens(d_activation, extent_x, extent_y, extent_z).resh...  16.5 us
    ppermute x4, starting transfers between devices, padded_2(): lax.ppermute(lax.slice_in_dim(block, block.shape[dim] - width, None, axis...  14.9 us
    all_to_all x1, waiting for transfers between devices, local(): conv_rows = lax.all_to_all(conv_part, ('gx', 'gy'), 0, 0, tiled=True)  14 us
    dot_general x3, matrix products, local(): jnp.einsum('vr,vc->rc', columns, shifted.reshape(voxels, channels), prefe...  12.9 us
    concatenate x5, other arithmetic, padded_2(): block = jnp.concatenate([low, block, high], axis=dim)  11.5 us
  transfers between devices with their start and end apart: 12, of which 5 were waited for; matrix products, arithmetic and copies ran while one was open for 43% of the time, Pallas kernels for 0%

profile of v9, /device:TPU:1, one launch (start us, length us, event | category | flops | bytes accessed | tf_op | source)
XLA Modules:
  0.0 374.3 jit_solution(5919224389130900838)
XLA Ops:
  8.2 4.7 %collective-permute-start = (bf16[1,16,4,256]{3,2,1,0:T(4,128)(2,1)S(1)}, bf16[1,16,4,256]{3,2,1,0:T(4,128)(2,1)S(1)}, u32[]{:S(2)}, u32[]{:S(2)}) collective-permute-start(bf16[1,16,4,256]{3,2,1,0:T(4,128)(2,1)S(1)} %get-tuple-element.86), channel_id=1, source_target_pairs={{0,4},{4,8},{8,12},{1,5},{5,9},{9,13},{2,6},{6,10},{10,14},{3,7},{... | collective-permute-start | bytes 98312 | tf_op jit(solution)/shard_map/ppermute | solution.py:18
  14.9 3.3 collective-permute-done.1
  21.1 3.1 collective-permute-start.2
  33.3 6.2 %copy.202 = bf16[768,2304]{1,0:T(8,128)(2,1)} copy(bf16[768,2304]{0,1:T(8,128)(2,1)} %bitcast.163) | data formatting | bytes 7077888 | tf_op jit(solution)/shard_map/dot_general | solution.py:74
  39.8 3.6 pad_maximum_fusion.6
  46.7 3.8 %fusion.7 = f32[256,4,3,256]{3,0,2,1:T(8,128)S(1)} fusion(bf16[3,256,2304,1]{2,1,0,3:T(8,128)(2,1)S(1)} %bitcast.176, bf16[256,4,2304]{2,0,1:T(8,128)(2,1)S(1)} %constant_dynamic-update-slice_fusion.3), kind=kOutput, calls=%fused_computation.10 | convolution fusion | flops 3623878656 | bytes 11403264 | tf_op jit(solution)/shard_map/dot_general | solution.py:74
  70.4 47.9 %all-gather.2.cloned.1.call-done = bf16[2048,1024]{1,0:T(8,128)(2,1)} async-done(((bf16[128,1024]{1,0:T(8,128)(2,1)}), bf16[2048,1024]{1,0:T(8,128)(2,1)}) %all-gather.2.cloned.1.call-update) | async-done | bytes 4194320 | tf_op jit(solution)/shard_map/all_gather | solution.py:95
  118.3 4.5 %fusion.48 = (bf16[2048,512]{1,0:T(8,128)(2,1)}, bf16[2048,512]{1,0:T(8,128)(2,1)}) fusion(bf16[2048,1024]{1,0:T(8,128)(2,1)} %all-gather.2.cloned.1.call-done), kind=kLoop, calls=%fused_computation.131 | loop fusion | bytes 8388608 | tf_op jit(solution)/shard_map/slice | solution.py:99
  122.8 3.9 %copy.208 = bf16[2048,512]{0,1:T(8,128)(2,1)} copy(bf16[2048,512]{1,0:T(8,128)(2,1)} %get-tuple-element.50) | data formatting | bytes 4194304 | tf_op jit(solution)/shard_map/slice | solution.py:98
  126.8 6.4 %fusion.3 = (f32[8,128]{1,0:T(8,128)S(1)}, f32[8,128,2048]{2,1,0:T(8,128)}) fusion(bf16[128,8,64]{0,2,1:T(8,128)(2,1)} %bitcast.198, bf16[2048,8,64]{0,2,1:T(8,128)(2,1)} %bitcast.170), kind=kOutput, calls=%fused_computation.6 | convolution fusion | flops 272628736 | bytes 10620928 | tf_op jit(solution)/shard_map/ihe,jhe->hij/dot_general | solution.py:104
  133.2 3.9 %copy.211 = bf16[2048,512]{0,1:T(8,128)(2,1)} copy(bf16[2048,512]{1,0:T(8,128)(2,1)} %get-tuple-element.49) | data formatting | bytes 4194304 | tf_op jit(solution)/shard_map/slice | solution.py:99
  137.1 5.4 %convolution_convert_fusion.6 = bf16[8,64,2048]{2,1,0:T(8,128)(2,1)S(1)} fusion(bf16[128,8,64]{0,2,1:T(8,128)(2,1)} %bitcast.196, f32[8,128,2048]{2,1,0:T(8,128)} %get-tuple-element.90, f32[8,128]{1,0:T(8,128)S(1)} %broadcast_divide_fusion), kind=kOutput, calls=%fused_computation.24 | convolution fusion | flops 275775488 | bytes 10620928 | tf_op jit(solution)/shard_map/hij,ihe->jhe/dot_general | solution.py:139
  154.1 5.4 %all-to-all-start = ((bf16[16,128,1024]{1,2,0:T(8,128)(2,1)}), bf16[16,128,1024]{1,2,0:T(8,128)(2,1)}, u32[]{:S(2)}, u32[]{:S(2)}) async-start(bf16[16,128,1024]{1,2,0:T(8,128)(2,1)} %pad_maximum_fusion.1), calls=%async_computation | async-start | bytes 8388608 | tf_op jit(solution)/shard_map/all_to_all | solution.py:148
  193.1 5.1 %convolution_convert_fusion.10 = bf16[8,64,128]{2,1,0:T(8,128)(2,1)S(1)} fusion(bf16[2048,8,64]{0,2,1:T(8,128)(2,1)S(1)} %bitcast.158, f32[8,128,2048]{2,1,0:T(8,128)} %get-tuple-element.90, f32[8,128]{1,0:T(8,128)S(1)} %broadcast_divide_fusion), kind=kOutput, calls=%fused_computation.30 | convolution fusion | flops 274792448 | bytes 10620928 | tf_op jit(solution)/shard_map/hij,jhe->ihe/dot_general | solution.py:111
  201.5 8.2 %fusion.19 = bf16[8,64,128]{2,1,0:T(8,128)(2,1)} fusion(bf16[2048,8,64]{0,2,1:T(8,128)(2,1)} %bitcast.171, bf16[8,128,2048]{2,1,0:T(8,128)(2,1)} %copy-done.4, f32[8,128,2048]{2,1,0:T(8,128)} %get-tuple-element.90, f32[8,128]{1,0:T(8,128)S(1)} %get-tuple-element.91, f32[8,128]{1,0:T(8,128)S(1)} %broadcast_divide_fusion), kind=kOutput, calls=%fused_computation.32 | convolution fusion | flops 279052288 | bytes 14819328 | tf_op jit(solution)/shard_map/hij,jhe->ihe/dot_general | solution.py:125
  209.7 5.1 %all-to-all-done = bf16[16,128,1024]{1,2,0:T(8,128)(2,1)} async-done(((bf16[16,128,1024]{1,2,0:T(8,128)(2,1)}), bf16[16,128,1024]{1,2,0:T(8,128)(2,1)}, u32[]{:S(2)}, u32[]{:S(2)}) %all-to-all-start) | async-done | bytes 4194336 | tf_op jit(solution)/shard_map/all_to_all | solution.py:148
  214.8 3.5 reduce.2
  227.0 4.5 %reshape.251 = bf16[16,512,128]{2,1,0:T(8,128)(2,1)} reshape(bf16[2048,512]{1,0:T(8,128)(2,1)} %convolution_convert_fusion.4) | data formatting | bytes 4194304 | tf_op jit(solution)/shard_map/reshape | solution.py:226
  231.5 4.3 %reshape.252 = bf16[16,384,128]{2,1,0:T(8,128)(2,1)} reshape(bf16[512,1536]{1,0:T(8,128)(2,1)} %convolution_convert_fusion.5) | data formatting | bytes 3145728 | tf_op jit(solution)/shard_map/reshape | solution.py:226
  236.0 3.7 pad_maximum_fusion
  252.1 3.2 reshape.261
  265.9 5.0 %convolution_convert_fusion.1 = bf16[2304,256]{1,0:T(8,128)(2,1)} fusion(bf16[1024,2304]{1,0:T(8,128)(2,1)} %constant_dynamic-update-slice_fusion.21, bf16[1024,256]{1,0:T(8,128)(2,1)} %copy-done.30), kind=kOutput, calls=%fused_computation.16 | convolution fusion | flops 1208549376 | bytes 6422528 | tf_op jit(solution)/shard_map/vr,vc->rc/dot_general | solution.py:189
  279.2 4.2 %collective-permute-start.7 = (bf16[18,1,4,256]{3,1,0,2:T(2,128)(2,1)S(1)}, bf16[18,1,4,256]{3,1,0,2:T(2,128)(2,1)S(1)}, u32[]{:S(2)}, u32[]{:S(2)}) collective-permute-start(bf16[18,1,4,256]{3,1,0,2:T(2,128)(2,1)S(1)} %get-tuple-element.69), channel_id=1, source_target_pairs={{0,1},{1,2},{2,3},{4,5},{5,6},{6,7},{8,9},{9,10},{10,11},{12,13},{... | collective-permute-start | bytes 110600 | tf_op jit(solution)/shard_map/ppermute | solution.py:18
  295.1 4.0 %convolution_convert_fusion.2 = bf16[2304,256]{1,0:T(8,128)(2,1)S(1)} fusion(bf16[1024,2304]{1,0:T(8,128)(2,1)} %constant_dynamic-update-slice_fusion.21, bf16[1024,256]{1,0:T(8,128)(2,1)} %reshape.249), kind=kOutput, calls=%fused_computation.17 | convolution fusion | flops 1208549376 | bytes 6422528 | tf_op jit(solution)/shard_map/vr,vc->rc/dot_general | solution.py:189
  299.1 3.9 %convolution_convert_fusion = bf16[2304,256]{1,0:T(8,128)(2,1)S(1)} fusion(bf16[1024,2304]{1,0:T(8,128)(2,1)} %constant_dynamic-update-slice_fusion.21, bf16[1024,256]{1,0:T(8,128)(2,1)S(1)} %reshape.250), kind=kOutput, calls=%fused_computation.15 | convolution fusion | flops 1208549376 | bytes 6422528 | tf_op jit(solution)/shard_map/vr,vc->rc/dot_general | solution.py:189
  305.1 5.6 %all-to-all-start.1 = ((bf16[16,432,256]{2,1,0:T(8,128)(2,1)}), bf16[16,432,256]{2,1,0:T(8,128)(2,1)}, u32[]{:S(2)}, u32[]{:S(2)}) async-start(bf16[16,432,256]{2,1,0:T(8,128)(2,1)} %bitcast.162), calls=%async_computation.1 | async-start | bytes 7077888 | tf_op jit(solution)/shard_map/all_to_all | solution.py:241
  310.7 8.0 %copy.223 = bf16[9,3,256,256]{2,1,3,0:T(4,128)(2,1)} copy(bf16[9,3,256,256]{3,2,1,0:T(8,128)(2,1)} %bitcast.165) | data formatting | bytes 7077888 | tf_op jit(solution)/shard_map/reshape | solution.py:69
  318.7 5.2 %copy.246 = bf16[288,8,3,256]{3,1,2,0:T(8,128)(2,1)} copy(bf16[288,8,3,256]{3,2,1,0:T(4,128)(2,1)} %bitcast.160) | data formatting | bytes 7077888
  323.8 5.9 %copy.224 = bf16[768,2304]{1,0:T(8,128)(2,1)} copy(bf16[768,2304]{0,1:T(8,128)(2,1)} %bitcast.164) | data formatting | bytes 7077888 | tf_op jit(solution)/shard_map/dot_general | solution.py:206
  335.4 6.8 %fusion.5 = f32[256,4,3,256]{3,0,2,1:T(8,128)S(1)} fusion(bf16[3,256,2304,1]{2,1,0,3:T(8,128)(2,1)} %bitcast.177, bf16[256,4,2304]{2,0,1:T(8,128)(2,1)} %constant_dynamic-update-slice_fusion.12), kind=kOutput, calls=%fused_computation.8 | convolution fusion | flops 3623878656 | bytes 11403264 | tf_op jit(solution)/shard_map/dot_general | solution.py:206
  343.7 14.0 %all-to-all-done.1 = bf16[16,432,256]{2,1,0:T(8,128)(2,1)} async-done(((bf16[16,432,256]{2,1,0:T(8,128)(2,1)}), bf16[16,432,256]{2,1,0:T(8,128)(2,1)}, u32[]{:S(2)}, u32[]{:S(2)}) %all-to-all-start.1) | async-done | bytes 3538976 | tf_op jit(solution)/shard_map/all_to_all | solution.py:241
  357.7 3.3 reduce_sum.91
  (227 shorter events, 153.1 us)
Async XLA Ops:
  7.2 50.2 %copy-start = (bf16[2048,512]{1,0:T(8,128)(2,1)S(1)}, bf16[2048,512]{1,0:T(8,128)(2,1)}, u32[]{:S(2)}) copy-start(bf16[2048,512]{1,0:T(8,128)(2,1)} %param.9) | copy-start | bytes 6291460
  7.2 111.1 %all-gather.2.cloned.1.call-start = ((), (), s32[]{:S(2)}) async-start(), calls=%async_computation.3 | async-start | bytes 4456448 | tf_op jit(solution)/shard_map/all_gather | solution.py:95
  7.2 20.2 %copy-start.5 = (bf16[6912,256]{1,0:T(8,128)(2,1)S(1)}, bf16[6912,256]{1,0:T(8,128)(2,1)}, u32[]{:S(2)}) copy-start(bf16[6912,256]{1,0:T(8,128)(2,1)} %param.8) | copy-start | bytes 10616836
  8.2 6.7 %collective-permute-start = (bf16[1,16,4,256]{3,2,1,0:T(4,128)(2,1)S(1)}, bf16[1,16,4,256]{3,2,1,0:T(4,128)(2,1)S(1)}, u32[]{:S(2)}, u32[]{:S(2)}) collective-permute-start(bf16[1,16,4,256]{3,2,1,0:T(4,128)(2,1)S(1)} %get-tuple-element.86), channel_id=1, source_target_pairs={{0,4},{4,8},{8,12},{1,5},{5,9},{9,13},{2,6},{6,10},{10,14},{3,7},{... | collective-permute-start | bytes 98312 | tf_op jit(solution)/shard_map/ppermute | solution.py:18
  12.9 5.2 %collective-permute-start.1 = (bf16[1,16,4,256]{3,2,1,0:T(4,128)(2,1)S(1)}, bf16[1,16,4,256]{3,2,1,0:T(4,128)(2,1)S(1)}, u32[]{:S(2)}, u32[]{:S(2)}) collective-permute-start(bf16[1,16,4,256]{3,2,1,0:T(4,128)(2,1)S(1)} %get-tuple-element.85), channel_id=1, source_target_pairs={{4,0},{8,4},{12,8},{5,1},{9,5},{13,9},{6,2},{10,6},{14,10},{7,3},{... | collective-permute-start | bytes 98312 | tf_op jit(solution)/shard_map/ppermute | solution.py:21
  21.0 18.5 %copy-start.9 = (bf16[16,16,4,256]{3,2,1,0:T(4,128)(2,1)}, bf16[16,16,4,256]{3,2,1,0:T(4,128)(2,1)S(1)}, u32[]{:S(2)}) copy-start(bf16[16,16,4,256]{3,2,1,0:T(4,128)(2,1)S(1)} %get-tuple-element.84) | copy-start | bytes 1572868
  21.1 18.6 %copy-start.8 = (bf16[16,16,4,256]{3,2,1,0:T(4,128)(2,1)}, bf16[16,16,4,256]{3,2,1,0:T(4,128)(2,1)S(1)}, u32[]{:S(2)}) copy-start(bf16[16,16,4,256]{3,2,1,0:T(4,128)(2,1)S(1)} %get-tuple-element.82) | copy-start | bytes 1572868
  21.1 18.6 %collective-permute-start.2 = (bf16[18,1,4,256]{3,2,1,0:T(4,128)(2,1)S(1)}, bf16[18,1,4,256]{3,2,1,0:T(4,128)(2,1)S(1)}, u32[]{:S(2)}, u32[]{:S(2)}) collective-permute-start(bf16[18,1,4,256]{3,2,1,0:T(4,128)(2,1)S(1)} %get-tuple-element.75), channel_id=1, source_target_pairs={{0,1},{1,2},{2,3},{4,5},{5,6},{6,7},{8,9},{9,10},{10,11},{12,13},{... | collective-permute-start | bytes 110600 | tf_op jit(solution)/shard_map/ppermute | solution.py:18
  24.3 15.5 %collective-permute-start.3 = (bf16[18,1,4,256]{3,2,1,0:T(4,128)(2,1)S(1)}, bf16[18,1,4,256]{3,2,1,0:T(4,128)(2,1)S(1)}, u32[]{:S(2)}, u32[]{:S(2)}) collective-permute-start(bf16[18,1,4,256]{3,2,1,0:T(4,128)(2,1)S(1)} %get-tuple-element.74), channel_id=1, source_target_pairs={{1,0},{2,1},{3,2},{5,4},{6,5},{7,6},{9,8},{10,9},{11,10},{13,12},{... | collective-permute-start | bytes 110600 | tf_op jit(solution)/shard_map/ppermute | solution.py:21
  50.8 8.3 %copy-start.32 = (f32[512]{0:T(512)S(1)}, f32[512]{0:T(512)}, u32[]{:S(2)}) copy-start(f32[512]{0:T(512)} %param.10) | copy-start | bytes 6148
  59.0 165.3 %copy-start.33 = (f32[128]{0:T(128)}, f32[128]{0:T(128)S(1)}, u32[]{:S(2)}) copy-start(f32[128]{0:T(128)S(1)} %broadcast_multiply_fusion.2) | copy-start | bytes 1540
  59.2 63.6 %copy-start.35 = (f32[128]{0:T(128)}, f32[128]{0:T(128)S(1)}, u32[]{:S(2)}) copy-start(f32[128]{0:T(128)S(1)} %add_rsqrt_fusion) | copy-start | bytes 1540
  137.1 6.4 %copy-start.2 = (bf16[2048,512]{0,1:T(8,128)(2,1)S(1)}, bf16[2048,512]{0,1:T(8,128)(2,1)}, u32[]{:S(2)}) copy-start(bf16[2048,512]{0,1:T(8,128)(2,1)} %copy.211) | copy-start | bytes 6291460
  137.1 6.4 %copy-start.25 = (bf16[128,512]{0,1:T(8,128)(2,1)S(1)}, bf16[128,512]{0,1:T(8,128)(2,1)}, u32[]{:S(2)}) copy-start(bf16[128,512]{0,1:T(8,128)(2,1)} %copy.210) | copy-start | bytes 393220
  154.1 60.7 %all-to-all-start = ((bf16[16,128,1024]{1,2,0:T(8,128)(2,1)}), bf16[16,128,1024]{1,2,0:T(8,128)(2,1)}, u32[]{:S(2)}, u32[]{:S(2)}) async-start(bf16[16,128,1024]{1,2,0:T(8,128)(2,1)} %pad_maximum_fusion.1), calls=%async_computation | async-start | bytes 8388608 | tf_op jit(solution)/shard_map/all_to_all | solution.py:148
  159.5 201.5 %reduce-scatter.5.cloned.1.call-start = ((), (), s32[]{:S(2)}) async-start(), calls=%async_computation.4 | async-start | bytes 4491264
  181.5 9.8 %copy-start.22 = (bf16[1024,256]{1,0:T(8,128)(2,1)S(1)}, bf16[1024,256]{1,0:T(8,128)(2,1)}, u32[]{:S(2)}) copy-start(bf16[1024,256]{1,0:T(8,128)(2,1)} %reshape.245) | copy-start | bytes 1572868
  181.5 10.7 %copy-start.21 = (bf16[1024,256]{1,0:T(8,128)(2,1)S(1)}, bf16[1024,256]{1,0:T(8,128)(2,1)}, u32[]{:S(2)}) copy-start(bf16[1024,256]{1,0:T(8,128)(2,1)} %reshape.246) | copy-start | bytes 1572868
  181.5 11.6 %copy-start.3 = (bf16[2048,512]{0,1:T(8,128)(2,1)S(1)}, bf16[2048,512]{0,1:T(8,128)(2,1)}, u32[]{:S(2)}) copy-start(bf16[2048,512]{0,1:T(8,128)(2,1)} %copy.211) | copy-start | bytes 6291460
  209.7 11.6 %copy-start.36 = (f32[128]{0:T(128)S(1)}, f32[128]{0:T(128)}, u32[]{:S(2)}) copy-start(f32[128]{0:T(128)} %copy-done.35) | copy-start | bytes 1540
  218.4 6.4 %copy-start.7 = (bf16[128,2048]{1,0:T(8,128)(2,1)S(1)}, bf16[128,2048]{1,0:T(8,128)(2,1)}, u32[]{:S(2)}) copy-start(bf16[128,2048]{1,0:T(8,128)(2,1)} %reshape.232) | copy-start | bytes 1572868
  224.3 11.5 %copy-start.38 = (f32[128]{0:T(128)}, f32[128]{0:T(128)S(1)}, u32[]{:S(2)}) copy-start(f32[128]{0:T(128)S(1)} %get-tuple-element.94) | copy-start | bytes 1540
  227.0 8.8 %copy-start.41 = (f32[512]{0:T(512)S(1)}, f32[512]{0:T(512)}, u32[]{:S(2)}) copy-start(f32[512]{0:T(512)} %get-tuple-element.42) | copy-start | bytes 6148
  261.0 15.7 %collective-permute-start.4 = (bf16[1,16,4,256]{3,2,1,0:T(4,128)(2,1)S(1)}, bf16[1,16,4,256]{3,2,1,0:T(4,128)(2,1)S(1)}, u32[]{:S(2)}, u32[]{:S(2)}) collective-permute-start(bf16[1,16,4,256]{3,2,1,0:T(4,128)(2,1)S(1)} %slice.178), channel_id=1, source_target_pairs={{0,4},{4,8},{8,12},{1,5},{5,9},{9,13},{2,6},{6,10},{10,14},{3,7},{... | collective-permute-start | bytes 98312 | tf_op jit(solution)/shard_map/ppermute | solution.py:18
  263.8 7.1 %copy-start.17 = (f32[16,16,4,256]{3,2,1,0:T(4,128)S(1)}, f32[16,16,4,256]{3,2,1,0:T(4,128)}, u32[]{:S(2)}) copy-start(f32[16,16,4,256]{3,2,1,0:T(4,128)} %reshape.261) | copy-start | bytes 3145732
  263.9 8.3 %copy-start.6 = (f32[8,8,2,2,2,2,256]{6,5,4,3,2,1,0:T(2,128)S(1)}, f32[8,8,2,2,2,2,256]{6,5,4,3,2,1,0:T(2,128)}, u32[]{:S(2)}) copy-start(f32[8,8,2,2,2,2,256]{6,5,4,3,2,1,0:T(2,128)} %reshape.264) | copy-start | bytes 3145732
  263.9 12.8 %collective-permute-start.5 = (bf16[1,16,4,256]{3,2,1,0:T(4,128)(2,1)S(1)}, bf16[1,16,4,256]{3,2,1,0:T(4,128)(2,1)S(1)}, u32[]{:S(2)}, u32[]{:S(2)}) collective-permute-start(bf16[1,16,4,256]{3,2,1,0:T(4,128)(2,1)S(1)} %slice.180), channel_id=1, source_target_pairs={{4,0},{8,4},{12,8},{5,1},{9,5},{13,9},{6,2},{10,6},{14,10},{7,3},{... | collective-permute-start | bytes 98312 | tf_op jit(solution)/shard_map/ppermute | solution.py:21
  277.9 7.7 %collective-permute-start.6 = (bf16[18,1,4,256]{3,1,0,2:T(2,128)(2,1)S(1)}, bf16[18,1,4,256]{3,1,0,2:T(2,128)(2,1)S(1)}, u32[]{:S(2)}, u32[]{:S(2)}) collective-permute-start(bf16[18,1,4,256]{3,1,0,2:T(2,128)(2,1)S(1)} %get-tuple-element.70), channel_id=1, source_target_pairs={{1,0},{2,1},{3,2},{5,4},{6,5},{7,6},{9,8},{10,9},{11,10},{13,12},{... | collective-permute-start | bytes 110600 | tf_op jit(solution)/shard_map/ppermute | solution.py:21
  279.2 7.4 %collective-permute-start.7 = (bf16[18,1,4,256]{3,1,0,2:T(2,128)(2,1)S(1)}, bf16[18,1,4,256]{3,1,0,2:T(2,128)(2,1)S(1)}, u32[]{:S(2)}, u32[]{:S(2)}) collective-permute-start(bf16[18,1,4,256]{3,1,0,2:T(2,128)(2,1)S(1)} %get-tuple-element.69), channel_id=1, source_target_pairs={{0,1},{1,2},{2,3},{4,5},{5,6},{6,7},{8,9},{9,10},{10,11},{12,13},{... | collective-permute-start | bytes 110600 | tf_op jit(solution)/shard_map/ppermute | solution.py:18
  305.1 52.7 %all-to-all-start.1 = ((bf16[16,432,256]{2,1,0:T(8,128)(2,1)}), bf16[16,432,256]{2,1,0:T(8,128)(2,1)}, u32[]{:S(2)}, u32[]{:S(2)}) async-start(bf16[16,432,256]{2,1,0:T(8,128)(2,1)} %bitcast.162), calls=%async_computation.1 | async-start | bytes 7077888 | tf_op jit(solution)/shard_map/all_to_all | solution.py:241
  323.8 7.8 %copy-start.23 = (bf16[16,16,4,256]{3,1,0,2:T(8,128)(2,1)S(1)}, bf16[16,16,4,256]{3,1,0,2:T(8,128)(2,1)}, u32[]{:S(2)}) copy-start(bf16[16,16,4,256]{3,1,0,2:T(8,128)(2,1)} %get-tuple-element.58) | copy-start | bytes 1572868
  323.8 8.7 %copy-start.19 = (bf16[16,16,4,256]{3,1,0,2:T(8,128)(2,1)S(1)}, bf16[16,16,4,256]{3,1,0,2:T(8,128)(2,1)}, u32[]{:S(2)}) copy-start(bf16[16,16,4,256]{3,1,0,2:T(8,128)(2,1)} %get-tuple-element.78) | copy-start | bytes 1572868
  (22 other events, 54.7 us)
Sparse Core Ops, SparseCore 0:
  62.7 55.5 all-gather.1
  239.8 74.2 reduce-scatter.4
